TPU v7x, 512 devices: a whole 4x4x16 slice. The times are simulated.
512 devices in a mesh: ctx: 32 (over z_hi, y, x), exp: 16 (over z_lo, core).
Axes of the slice: x: 4, y: 4, z: 16 (z_hi: 2, z_lo: 8; z = z_hi * 8 + z_lo), core: 2. Of those that a mesh axis runs over, the one named last changes fastest.
Arguments:
- hidden_in: bfloat16 [4096, 2880], P('ctx'), may hold values from -6 to 6
- query_input: bfloat16 [4096, 2048], P('ctx', 'exp'), may hold values from -16 to 16
- key_heads_input: bfloat16 [4096, 256], P('ctx'), may hold values from -16 to 16
- value_heads_input: bfloat16 [4096, 256], P('ctx'), may hold values from -6 to 6
- sink_logits: float32 [32], P('exp'), may hold values from 0 to 4
- out_proj: bfloat16 [2048, 2880], P('exp'), may hold values from -0.125 to 0.125
- norm_gain: float32 [2880], replicated, may hold values from 0.5 to 1.5
- expert_ids: int32 [4096, 4], P('ctx'), may hold values from 0 to 31, all different within a row; in each aligned block of 128 rows (0 to 127, 128 to 255, ...) at most 20 rows name the same one
- expert_gates: float32 [4096, 4], P('ctx'), may hold values from 0.1 to 1
- gate_up: bfloat16 [32, 2880, 2, 2880], P('ctx', None, None, 'exp'), may hold values from -0.109375 to 0.109375
- down_proj: bfloat16 [32, 2880, 2880], P('ctx', 'exp'), may hold values from -0.109375 to 0.109375
Outputs:
- layer_out: bfloat16 [4096, 2880], P('ctx', 'exp')
Inputs may be any that keep to these rules, and one draw needn't show every extreme that they name: `expert_ids`: each token names 4 different experts; within the 128 tokens of one device no expert is named by more than 20 tokens.
All inputs are finite; a program needn't handle non-finite values.
Results may differ from a plain program's by a relative error of at most 0.02.
Values may be sent and summed in bfloat16 or wider, within the bound.
No kernel may reach another device: no remote copies, remote signals or barrier semaphores. Data moves between devices by JAX's collectives and lax.ppermute only.
A program may use at most 64 MiB of HBM per device.

v0:
```python
import math

import jax
import jax.numpy as jnp
import numpy as np
from jax import lax
from jax.sharding import PartitionSpec as P

D = 2880
QUERY_HEADS = 32
KEY_VALUE_HEADS = 4
HEAD_SIZE = 64


yarn_base = 150000.0
yarn_factor = 32.0
yarn_initial = 4096.0
beta_fast = 32.0
beta_slow = 1.0
neg_large = -1e30


def yarn_frequencies(head_dim):
    half_dim = head_dim // 2

    def correction(rotations):
        return (
            head_dim
            * math.log(yarn_initial / (rotations * 2.0 * math.pi))
            / (2.0 * math.log(yarn_base))
        )

    lower_dim = max(math.floor(correction(beta_fast)), 0)
    upper_dim = min(math.ceil(correction(beta_slow)), head_dim - 1)
    extrap_freq = 1.0 / yarn_base ** (np.arange(0, head_dim, 2) / head_dim)
    interp_freq = extrap_freq / yarn_factor
    ramp_part = np.clip((np.arange(half_dim) - lower_dim) / (upper_dim - lower_dim), 0.0, 1.0)
    extrap_share = 1.0 - ramp_part
    return (interp_freq * (1.0 - extrap_share) + extrap_freq * extrap_share).astype(np.float32)


def rotate_with_yarn(heads_in, token_positions):
    head_dim = heads_in.shape[-1]
    freqs = jnp.asarray(yarn_frequencies(head_dim))
    angles = token_positions.astype(jnp.float32)[:, None] * freqs[None, :]
    factor = 0.1 * math.log(yarn_factor) + 1.0
    cosine = (jnp.cos(angles) * factor)[:, None, :]
    sine = (jnp.sin(angles) * factor)[:, None, :]
    first_half = heads_in[..., : head_dim // 2]
    second_half = heads_in[..., head_dim // 2 :]
    return jnp.concatenate(
        [first_half * cosine - second_half * sine, second_half * cosine + first_half * sine],
        axis=-1,
    )


def route_slots(ids_block, n_experts):
    flat_ids = ids_block.reshape(-1)
    onehot = (flat_ids[:, None] == jnp.arange(n_experts, dtype=jnp.int32)[None, :]).astype(
        jnp.int32
    )
    ranks = jnp.cumsum(onehot, axis=0) - onehot
    return jnp.sum(ranks * onehot, axis=1).reshape(ids_block.shape)


def per_device(
    hidden_in,
    query_input,
    key_heads_input,
    value_heads_input,
    sink_logits,
    out_proj,
    norm_gain,
    expert_ids,
    expert_gates,
    gate_up,
    down_proj,
):
    tok_rows = hidden_in.shape[0]
    ctx_count = lax.axis_size("ctx")
    exp_count = lax.axis_size("exp")
    local_heads = query_input.shape[1] // HEAD_SIZE
    token_positions = lax.axis_index("ctx") * tok_rows + jnp.arange(tok_rows, dtype=jnp.int32)
    q_rot = rotate_with_yarn(
        query_input.astype(jnp.float32).reshape(tok_rows, local_heads, HEAD_SIZE), token_positions
    ).astype(jnp.bfloat16)
    shared_key_head = lax.axis_index("exp") * local_heads // (QUERY_HEADS // KEY_VALUE_HEADS)
    key_block = lax.dynamic_slice_in_dim(key_heads_input, shared_key_head * HEAD_SIZE, HEAD_SIZE, 1)
    value_block = lax.dynamic_slice_in_dim(
        value_heads_input, shared_key_head * HEAD_SIZE, HEAD_SIZE, 1
    )
    key_rot = (
        rotate_with_yarn(
            key_block.astype(jnp.float32).reshape(tok_rows, 1, HEAD_SIZE), token_positions
        )
        .reshape(tok_rows, HEAD_SIZE)
        .astype(jnp.bfloat16)
    )
    key_value = jnp.concatenate([key_rot, value_block], axis=1)
    score_scale = 1.0 / math.sqrt(HEAD_SIZE)
    block_part = lax.all_gather(key_value, "ctx", axis=0, tiled=True)
    run_max = jnp.broadcast_to(sink_logits[:, None], (local_heads, tok_rows))
    run_total = jnp.ones((local_heads, tok_rows), jnp.float32)
    run_sum = jnp.zeros((local_heads, tok_rows, HEAD_SIZE), jnp.float32)
    key_count = block_part.shape[0]
    key_part = block_part[:, :HEAD_SIZE]
    value_part = block_part[:, HEAD_SIZE:].astype(jnp.float32)
    scores = (
        jnp.einsum("rhd,kd->hrk", q_rot, key_part, preferred_element_type=jnp.float32) * score_scale
    )
    key_pos = jnp.arange(key_count, dtype=jnp.int32)
    visible = token_positions[:, None] >= key_pos[None, :]
    scores = jnp.where(visible[None, :, :], scores, neg_large)
    new_max = jnp.maximum(run_max, jnp.max(scores, axis=2))
    weights = jnp.exp(scores - new_max[:, :, None])
    factor = jnp.exp(run_max - new_max)
    run_total = run_total * factor + jnp.sum(weights, axis=2)
    run_sum = run_sum * factor[:, :, None] + jnp.einsum(
        "hrk,kd->hrd", weights, value_part, precision=lax.Precision.HIGHEST
    )
    run_max, run_total, run_sum = (new_max, run_total, run_sum)
    attended = (
        (run_sum / run_total[:, :, None])
        .transpose(1, 0, 2)
        .reshape(tok_rows, local_heads * HEAD_SIZE)
        .astype(jnp.bfloat16)
    )
    head_part = jnp.dot(attended, out_proj, preferred_element_type=jnp.float32)
    residual = hidden_in.astype(jnp.float32) + lax.psum(
        head_part.astype(jnp.bfloat16), "exp"
    ).astype(jnp.float32)
    mean_square = jnp.mean(residual * residual, axis=1, keepdims=True)
    normed = (residual * lax.rsqrt(mean_square + 1e-05) * norm_gain[None, :]).astype(jnp.bfloat16)
    exp_local = gate_up.shape[0]
    n_experts = exp_local * ctx_count
    top_count = expert_ids.shape[1]
    capacity = max(2, tok_rows * top_count * 5 // (4 * n_experts))
    slot_index = route_slots(expert_ids, n_experts)
    dest_row = expert_ids * capacity + slot_index
    spread_rows = jnp.broadcast_to(normed[:, None, :], (tok_rows, top_count, D)).reshape(
        tok_rows * top_count, D
    )
    send_rows = (
        jnp.zeros((n_experts * capacity, D), jnp.bfloat16).at[dest_row.reshape(-1)].set(spread_rows)
    )
    bucket_rows = ctx_count * capacity
    unit_count = gate_up.shape[-1]
    col_width = D // exp_count
    weights_flat = gate_up.reshape(exp_local, D, 2 * unit_count)
    received = lax.all_to_all(
        send_rows.reshape(ctx_count, exp_local * capacity, D),
        "ctx",
        split_axis=0,
        concat_axis=0,
        tiled=True,
    )
    expert_rows = (
        received.reshape(ctx_count, exp_local, capacity, D)
        .transpose(1, 0, 2, 3)
        .reshape(exp_local, bucket_rows, D)
    )
    gate_up_out = jnp.einsum(
        "erd,edf->erf", expert_rows, weights_flat, preferred_element_type=jnp.float32
    )
    gate_up_out = gate_up_out.reshape(exp_local, bucket_rows, 2, unit_count)
    gate_value = gate_up_out[:, :, 0]
    up_value = gate_up_out[:, :, 1]
    activated = ((up_value + 1.0) * gate_value * jax.nn.sigmoid(1.702 * gate_value)).astype(
        jnp.bfloat16
    )
    partial_value = jnp.einsum(
        "erf,efd->erd", activated, down_proj, preferred_element_type=jnp.float32
    )
    partial_rounded = partial_value.astype(jnp.bfloat16)
    outgoing = partial_rounded.reshape(exp_local, ctx_count, capacity, D).transpose(1, 0, 2, 3)
    returned = lax.all_to_all(
        outgoing.reshape(ctx_count, exp_local * capacity, D),
        "ctx",
        split_axis=0,
        concat_axis=0,
        tiled=True,
    )
    picked_rows = returned.reshape(n_experts * capacity, D)[dest_row]
    gated = jnp.sum(expert_gates[:, :, None] * picked_rows.astype(jnp.float32), axis=1)
    moe_cols = lax.psum_scatter(
        gated.astype(jnp.bfloat16), "exp", scatter_dimension=1, tiled=True
    ).astype(jnp.float32)
    residual_cols = lax.dynamic_slice_in_dim(
        residual, lax.axis_index("exp") * col_width, col_width, 1
    )
    return (residual_cols + moe_cols).astype(jnp.bfloat16)


def solution(mesh):
    placed = (
        P("ctx", None),
        P("ctx", "exp"),
        P("ctx", None),
        P("ctx", None),
        P("exp"),
        P("exp", None),
        P(),
        P("ctx", None),
        P("ctx", None),
        P("ctx", None, None, "exp"),
        P("ctx", "exp", None),
    )
    return jax.shard_map(
        per_device, mesh=mesh, in_specs=placed, out_specs=P("ctx", "exp"), check_vma=False
    )
```

profile of v0, /device:TPU:8, one launch (start us, length us, event | category | flops | bytes accessed | tf_op | source)
XLA Modules:
  0.0 880.9 jit_solution(616412392526156827)
XLA Ops:
  12.2 119.5 %all-gather.2.cloned.1.call-done = bf16[4096,128]{0,1:T(8,128)(2,1)} async-done(((bf16[128,128]{0,1:T(8,128)(2,1)}), bf16[4096,128]{0,1:T(8,128)(2,1)}) %all-gather.2.cloned.1.call-update) | async-done | bytes 1048592 | tf_op jit(solution)/shard_map/all_gather | solution.py:101
  134.4 2.1 fusion.16
  140.0 186.8 %all-reduce.4.cloned.1.call-done = bf16[128,2880]{0,1:T(8,128)(2,1)} async-done(((bf16[128,2880]{0,1:T(8,128)(2,1)}), bf16[128,2880]{0,1:T(8,128)(2,1)}) %all-reduce.4.cloned.1.call-update) | async-done | bytes 737296 | tf_op jit(solution)/shard_map/psum | solution.py:129
  328.3 2.7 multiply_convert_fusion
  331.4 2.4 broadcast_in_dim.27
  333.8 5.6 reshape.397
  339.4 8.4 scatter_custom_fusion
  347.7 6.4 reshape.376
  354.1 17.0 %all-to-all-start = ((bf16[32,20,2880]{2,1,0:T(8,128)(2,1)}), bf16[32,20,2880]{2,1,0:T(8,128)(2,1)}, u32[]{:S(2)}, u32[]{:S(2)}) async-start(bf16[32,20,2880]{2,1,0:T(8,128)(2,1)} %reshape.376), calls=%async_computation | async-start | bytes 9043968 | tf_op jit(solution)/shard_map/all_to_all | solution.py:150
  372.9 2.3 reshape.378
  375.1 2.1 dot_general.28
  377.2 174.9 %all-to-all-done = bf16[32,20,2880]{2,1,0:T(8,128)(2,1)} async-done(((bf16[32,20,2880]{2,1,0:T(8,128)(2,1)}), bf16[32,20,2880]{2,1,0:T(8,128)(2,1)}, u32[]{:S(2)}, u32[]{:S(2)}) %all-to-all-start) | async-done | bytes 3686432 | tf_op jit(solution)/shard_map/all_to_all | solution.py:150
  552.2 6.6 reshape.377
  558.7 4.0 fusion.10
  562.8 3.3 convolution_convert_fusion
  566.1 6.2 copy.62
  572.3 6.4 reshape_transpose_reshape.4
  578.6 122.0 %all-to-all-start.1 = ((bf16[32,20,2880]{2,1,0:T(8,128)(2,1)}), bf16[32,20,2880]{2,1,0:T(8,128)(2,1)}, u32[]{:S(2)}, u32[]{:S(2)}) async-start(bf16[32,20,2880]{2,1,0:T(8,128)(2,1)} %reshape_transpose_reshape.4), calls=%async_computation.1 | async-start | bytes 9043968 | tf_op jit(solution)/shard_map/all_to_all | solution.py:176
  701.0 80.2 %all-to-all-done.1 = bf16[32,20,2880]{2,1,0:T(8,128)(2,1)} async-done(((bf16[32,20,2880]{2,1,0:T(8,128)(2,1)}), bf16[32,20,2880]{2,1,0:T(8,128)(2,1)}, u32[]{:S(2)}, u32[]{:S(2)}) %all-to-all-start.1) | async-done | bytes 3686432 | tf_op jit(solution)/shard_map/all_to_all | solution.py:176
  781.2 6.6 reshape.380
  787.8 9.3 %gather_fusion = bf16[512,2880]{1,0:T(8,128)(2,1)} fusion(bf16[640,2880]{1,0:T(8,128)(2,1)} %reshape.380, s32[1024]{0:T(1024)S(1)} %pad_clamp_fusion), kind=kCustom, calls=%fused_computation | custom fusion | bytes 5900288 | tf_op jit(solution)/shard_map/gather | solution.py:183
  797.1 6.6 reshape.403
  803.7 7.1 multiply_reduce_fusion
  811.2 57.7 %fusion = bf16[128,192]{0,1:T(8,128)(2,1)S(1)} fusion(bf16[128,2880]{0,1:T(8,128)(2,1)S(1)} %copy.64), kind=kCustom, calls=%all-reduce-scatter | all-reduce-scatter fusion | flops 393217 | bytes 788480
  (70 shorter events, 20.7 us)
Async XLA Ops:
  6.5 556.2 %copy-start = (bf16[1,180,2880]{2,1,0:T(8,128)(2,1)S(1)}, bf16[1,180,2880]{2,1,0:T(8,128)(2,1)}, u32[]{:S(2)}) copy-start(bf16[1,180,2880]{2,1,0:T(8,128)(2,1)} %param.23) | copy-start | bytes 3110404
  6.5 125.1 %all-gather.2.cloned.1.call-start = ((), (), s32[]{:S(2)}) async-start(), calls=%async_computation.2 | async-start | bytes 1081344 | tf_op jit(solution)/shard_map/all_gather | solution.py:101
  7.6 126.1 %copy-start.8 = (f32[2]{0:T(128)S(1)}, f32[2]{0:T(128)}, u32[]{:S(2)}) copy-start(f32[2]{0:T(128)} %param.17) | copy-start | bytes 28
  9.2 317.6 %all-reduce.4.cloned.1.call-start = ((), (), s32[]{:S(2)}) async-start(), calls=%async_computation.3 | async-start | bytes 1474560 | tf_op jit(solution)/shard_map/psum | solution.py:129
  131.7 2.7 copy-start.4
  133.8 2.7 copy-start.3
  134.4 5.4 copy-start.6
  134.4 192.4 %copy-start.2 = (bf16[128,2880]{0,1:T(8,128)(2,1)S(1)}, bf16[128,2880]{0,1:T(8,128)(2,1)}, u32[]{:S(2)}) copy-start(bf16[128,2880]{0,1:T(8,128)(2,1)} %param.13) | copy-start | bytes 2211844
  134.4 193.9 %copy-start.5 = (f32[2880]{0:T(1024)S(1)}, f32[2880]{0:T(1024)}, u32[]{:S(2)}) copy-start(f32[2880]{0:T(1024)} %param.19) | copy-start | bytes 34564
  354.1 198.1 %all-to-all-start = ((bf16[32,20,2880]{2,1,0:T(8,128)(2,1)}), bf16[32,20,2880]{2,1,0:T(8,128)(2,1)}, u32[]{:S(2)}, u32[]{:S(2)}) async-start(bf16[32,20,2880]{2,1,0:T(8,128)(2,1)} %reshape.376), calls=%async_computation | async-start | bytes 9043968 | tf_op jit(solution)/shard_map/all_to_all | solution.py:150
  578.6 122.2 %copy-start.7 = (f32[128,4]{0,1:T(4,128)S(1)}, f32[128,4]{0,1:T(4,128)}, u32[]{:S(2)}) copy-start(f32[128,4]{0,1:T(4,128)} %param.21) | copy-start | bytes 6148
  578.6 202.6 %all-to-all-start.1 = ((bf16[32,20,2880]{2,1,0:T(8,128)(2,1)}), bf16[32,20,2880]{2,1,0:T(8,128)(2,1)}, u32[]{:S(2)}, u32[]{:S(2)}) async-start(bf16[32,20,2880]{2,1,0:T(8,128)(2,1)} %reshape_transpose_reshape.4), calls=%async_computation.1 | async-start | bytes 9043968 | tf_op jit(solution)/shard_map/all_to_all | solution.py:176
  797.1 77.0 %copy-start.1 = (bf16[1,180,2880]{2,1,0:T(8,128)(2,1)S(1)}, bf16[1,180,2880]{2,1,0:T(8,128)(2,1)}, u32[]{:S(2)}) copy-start(bf16[1,180,2880]{2,1,0:T(8,128)(2,1)} %param.23) | copy-start | bytes 3110404
  868.9 3.2 collective-permute-start
Sparse Core Ops, SparseCore 0:
  11.4 120.1 all-gather.1
  137.8 188.8 all-reduce.3
where the time goes:
time: 883 us; the launch traced here: 881 us
  waiting for transfers between devices  561 us (64%)
  starting transfers between devices  140 us (16%)
  local copies, waits for them, and re-layouts  76.8 us (9%)
  blocking collectives  57.7 us (7%)
  other arithmetic  17.7 us (2%)
  between operations  14.3 us (2%)
  matrix products  12.6 us (1%)
    psum x1, waiting for transfers between devices, per_device(): lax.psum(head_part.astype(jnp.bfloat16), 'exp').astype(jnp.float32)  187 us
    all_to_all x1, waiting for transfers between devices, per_device(): lax.all_to_all(send_rows.reshape(ctx_count, exp_local * capacity, D), 'ct...  175 us
    all_to_all x1, starting transfers between devices, per_device(): lax.all_to_all(outgoing.reshape(ctx_count, exp_local * capacity, D), 'ctx...  122 us
    all_gather x1, waiting for transfers between devices, per_device(): block_part = lax.all_gather(key_value, 'ctx', axis=0, tiled=True)  119 us
    all_to_all x1, waiting for transfers between devices, per_device(): lax.all_to_all(outgoing.reshape(ctx_count, exp_local * capacity, D), 'ctx...  80.2 us
    unnamed x1, blocking collectives  57.7 us
  transfers between devices with their start and end apart: 5, of which 4 were waited for; matrix products, arithmetic and copies ran while one was open for 1% of the time, Pallas kernels for 0%

commit v1 on v0

v1 whole, which is shorter than its diff:
```python
import functools
import math

import jax
import jax.numpy as jnp
import numpy as np
from jax import lax
from jax.sharding import Mesh, PartitionSpec as P

D = 2880
QUERY_HEADS = 32
KEY_VALUE_HEADS = 4
HEAD_SIZE = 64


yarn_base = 150000.0
yarn_factor = 32.0
yarn_initial = 4096.0
beta_fast = 32.0
beta_slow = 1.0
neg_large = -1e30


def yarn_frequencies(head_dim):
    half_dim = head_dim // 2

    def correction(rotations):
        return (
            head_dim
            * math.log(yarn_initial / (rotations * 2.0 * math.pi))
            / (2.0 * math.log(yarn_base))
        )

    lower_dim = max(math.floor(correction(beta_fast)), 0)
    upper_dim = min(math.ceil(correction(beta_slow)), head_dim - 1)
    extrap_freq = 1.0 / yarn_base ** (np.arange(0, head_dim, 2) / head_dim)
    interp_freq = extrap_freq / yarn_factor
    ramp_part = np.clip((np.arange(half_dim) - lower_dim) / (upper_dim - lower_dim), 0.0, 1.0)
    extrap_share = 1.0 - ramp_part
    return (interp_freq * (1.0 - extrap_share) + extrap_freq * extrap_share).astype(np.float32)


def rotate_with_yarn(heads_in, token_positions):
    head_dim = heads_in.shape[-1]
    freqs = jnp.asarray(yarn_frequencies(head_dim))
    angles = token_positions.astype(jnp.float32)[:, None] * freqs[None, :]
    factor = 0.1 * math.log(yarn_factor) + 1.0
    cosine = (jnp.cos(angles) * factor)[:, None, :]
    sine = (jnp.sin(angles) * factor)[:, None, :]
    first_half = heads_in[..., : head_dim // 2]
    second_half = heads_in[..., head_dim // 2 :]
    return jnp.concatenate(
        [first_half * cosine - second_half * sine, second_half * cosine + first_half * sine],
        axis=-1,
    )


def route_slots(ids_block, n_experts):
    flat_ids = ids_block.reshape(-1)
    onehot = (flat_ids[:, None] == jnp.arange(n_experts, dtype=jnp.int32)[None, :]).astype(
        jnp.int32
    )
    ranks = jnp.cumsum(onehot, axis=0) - onehot
    return jnp.sum(ranks * onehot, axis=1).reshape(ids_block.shape)


CTX = ("zh", "y", "x")
EXP = ("zl", "c")


def per_device(
    hidden_in,
    query_input,
    key_heads_input,
    value_heads_input,
    sink_logits,
    out_proj,
    norm_gain,
    expert_ids,
    expert_gates,
    gate_up,
    down_proj,
    *,
    ctx_count,
    zl_count,
    c_count,
):
    tok_rows = hidden_in.shape[0]
    exp_count = zl_count * c_count
    local_heads = query_input.shape[1] // HEAD_SIZE
    ctx_index = lax.axis_index(CTX)
    exp_index = lax.axis_index(EXP)
    token_positions = ctx_index * tok_rows + jnp.arange(tok_rows, dtype=jnp.int32)
    q_rot = rotate_with_yarn(
        query_input.astype(jnp.float32).reshape(tok_rows, local_heads, HEAD_SIZE), token_positions
    ).astype(jnp.bfloat16)
    shared_key_head = exp_index * local_heads // (QUERY_HEADS // KEY_VALUE_HEADS)
    key_block = lax.dynamic_slice_in_dim(key_heads_input, shared_key_head * HEAD_SIZE, HEAD_SIZE, 1)
    value_block = lax.dynamic_slice_in_dim(
        value_heads_input, shared_key_head * HEAD_SIZE, HEAD_SIZE, 1
    )
    key_rot = (
        rotate_with_yarn(
            key_block.astype(jnp.float32).reshape(tok_rows, 1, HEAD_SIZE), token_positions
        )
        .reshape(tok_rows, HEAD_SIZE)
        .astype(jnp.bfloat16)
    )
    key_value = jnp.concatenate([key_rot, value_block], axis=1)
    score_scale = 1.0 / math.sqrt(HEAD_SIZE)
    block_part = lax.all_gather(key_value, CTX, axis=0, tiled=True)
    run_max = jnp.broadcast_to(sink_logits[:, None], (local_heads, tok_rows))
    run_total = jnp.ones((local_heads, tok_rows), jnp.float32)
    key_count = block_part.shape[0]
    key_part = block_part[:, :HEAD_SIZE]
    value_part = block_part[:, HEAD_SIZE:].astype(jnp.float32)
    scores = (
        jnp.einsum("rhd,kd->hrk", q_rot, key_part, preferred_element_type=jnp.float32) * score_scale
    )
    key_pos = jnp.arange(key_count, dtype=jnp.int32)
    visible = token_positions[:, None] >= key_pos[None, :]
    scores = jnp.where(visible[None, :, :], scores, neg_large)
    new_max = jnp.maximum(run_max, jnp.max(scores, axis=2))
    weights = jnp.exp(scores - new_max[:, :, None])
    factor = jnp.exp(run_max - new_max)
    run_total = run_total * factor + jnp.sum(weights, axis=2)
    run_sum = jnp.einsum("hrk,kd->hrd", weights, value_part, precision=lax.Precision.HIGHEST)
    attended = (
        (run_sum / run_total[:, :, None])
        .transpose(1, 0, 2)
        .reshape(tok_rows, local_heads * HEAD_SIZE)
        .astype(jnp.bfloat16)
    )
    col_width = D // exp_count
    head_part = jnp.dot(attended, out_proj, preferred_element_type=jnp.float32).astype(jnp.bfloat16)
    head_part = head_part.reshape(tok_rows, zl_count, c_count, col_width).transpose(2, 1, 0, 3)
    head_part = lax.psum_scatter(head_part, "c", scatter_dimension=0, tiled=True)[0]
    head_cols = lax.psum_scatter(head_part, "zl", scatter_dimension=0, tiled=True)[0]
    residual_cols = lax.dynamic_slice_in_dim(
        hidden_in, exp_index * col_width, col_width, 1
    ).astype(jnp.float32) + head_cols.astype(jnp.float32)
    square_sum = lax.psum(jnp.sum(residual_cols * residual_cols, axis=1), EXP)
    gain_cols = lax.dynamic_slice_in_dim(norm_gain, exp_index * col_width, col_width, 0)
    normed_cols = (
        residual_cols * lax.rsqrt(square_sum / D + 1e-05)[:, None] * gain_cols[None, :]
    ).astype(jnp.bfloat16)
    exp_local = gate_up.shape[0]
    n_experts = exp_local * ctx_count
    top_count = expert_ids.shape[1]
    capacity = max(2, tok_rows * top_count * 5 // (4 * n_experts))
    slot_index = route_slots(expert_ids, n_experts)
    dest_row = expert_ids * capacity + slot_index
    spread_rows = jnp.broadcast_to(
        normed_cols[:, None, :], (tok_rows, top_count, col_width)
    ).reshape(tok_rows * top_count, col_width)
    send_rows = (
        jnp.zeros((n_experts * capacity, col_width), jnp.bfloat16)
        .at[dest_row.reshape(-1)]
        .set(spread_rows)
    )
    bucket_rows = ctx_count * capacity
    unit_count = gate_up.shape[-1]
    received = lax.all_to_all(
        send_rows.reshape(ctx_count, exp_local * capacity, col_width),
        CTX,
        split_axis=0,
        concat_axis=0,
        tiled=True,
    ).reshape(bucket_rows, col_width)
    gathered = lax.all_gather(received, "zl", axis=0, tiled=False)
    gathered = lax.all_gather(gathered, "c", axis=0, tiled=False)
    weights_flat = gate_up.reshape(zl_count, c_count, col_width, 2 * unit_count)
    gate_up_out = jnp.einsum(
        "czrk,zckf->rf", gathered, weights_flat, preferred_element_type=jnp.float32
    )
    gate_up_out = gate_up_out.reshape(bucket_rows, 2, unit_count)
    gate_value = gate_up_out[:, 0]
    up_value = gate_up_out[:, 1]
    activated = ((up_value + 1.0) * gate_value * jax.nn.sigmoid(1.702 * gate_value)).astype(
        jnp.bfloat16
    )
    down_local = down_proj.reshape(unit_count, zl_count, c_count, col_width)
    partial_value = jnp.einsum(
        "rf,fzcd->czrd", activated, down_local, preferred_element_type=jnp.float32
    ).astype(jnp.bfloat16)
    partial_value = lax.psum_scatter(partial_value, "c", scatter_dimension=0, tiled=True)[0]
    expert_cols = lax.psum_scatter(partial_value, "zl", scatter_dimension=0, tiled=True)[0]
    returned = lax.all_to_all(
        expert_cols.reshape(ctx_count, capacity, col_width),
        CTX,
        split_axis=0,
        concat_axis=0,
        tiled=True,
    )
    picked_rows = returned.reshape(n_experts * capacity, col_width)[dest_row]
    moe_cols = jnp.sum(expert_gates[:, :, None] * picked_rows.astype(jnp.float32), axis=1)
    return (residual_cols + moe_cols).astype(jnp.bfloat16)


def solution(mesh):
    ctx_count, exp_count = mesh.devices.shape
    zh, y, x = (mesh.devices.shape[0] // 16, 4, 4)
    c_count = 2
    zl_count = exp_count // c_count
    fine = Mesh(mesh.devices.reshape(zh, y, x, zl_count, c_count), ("zh", "y", "x", "zl", "c"))
    placed = (
        P(CTX, None),
        P(CTX, EXP),
        P(CTX, None),
        P(CTX, None),
        P(EXP),
        P(EXP, None),
        P(),
        P(CTX, None),
        P(CTX, None),
        P(CTX, None, None, EXP),
        P(CTX, EXP, None),
    )
    return jax.shard_map(
        functools.partial(per_device, ctx_count=ctx_count, zl_count=zl_count, c_count=c_count),
        mesh=fine,
        in_specs=placed,
        out_specs=P(CTX, EXP),
        check_vma=False,
    )
```

time: 883 us -> 535 us (0.61)
  the two profiles are of different devices: /device:TPU:8 before, /device:TPU:32 now
where the time goes in v1:
time: 535 us
  waiting for transfers between devices  367 us (69%)
  blocking collectives  74.4 us (14%)
  local copies, waits for them, and re-layouts  46.9 us (9%)
  starting transfers between devices  17.6 us (3%)
  between operations  13.8 us (3%)
  matrix products  9.28 us (2%)
    unnamed x9, waiting for transfers between devices  125 us
    all_gather x1, waiting for transfers between devices, per_device(): block_part = lax.all_gather(key_value, CTX, axis=0, tiled=True)  113 us
    all_gather x1, waiting for transfers between devices, per_device(): gathered = lax.all_gather(received, 'zl', axis=0, tiled=False)  62 us
    psum x1, blocking collectives, per_device(): square_sum = lax.psum(jnp.sum(residual_cols * residual_cols, axis=1), EXP)  44.4 us
    all_to_all x1, blocking collectives, per_device(): lax.all_to_all(send_rows.reshape(ctx_count, exp_local * capacity, col_wid...  30 us
    reduce_scatter x1, waiting for transfers between devices, per_device(): lax.psum_scatter(partial_value, 'c', scatter_dimension=0, tiled=True)[0]  23.2 us
    all_to_all x1, waiting for transfers between devices, per_device(): lax.all_to_all(expert_cols.reshape(ctx_count, capacity, col_width), CTX,...  22.2 us
    all_to_all x1, starting transfers between devices, per_device(): lax.all_to_all(expert_cols.reshape(ctx_count, capacity, col_width), CTX,...  17 us
  transfers between devices with their start and end apart: 8, of which 8 were waited for; matrix products, arithmetic and copies ran while one was open for 5% of the time, Pallas kernels for 0%

profile of v1, /device:TPU:32, one launch (start us, length us, event | category | flops | bytes accessed | tf_op | source)
XLA Modules:
  0.0 534.8 jit_solution(13582523231836904942)
XLA Ops:
  11.3 113.0 %all-gather.5.cloned.1.call-done = bf16[4096,128]{0,1:T(8,128)(2,1)} async-done(((bf16[128,128]{0,1:T(8,128)(2,1)}), bf16[4096,128]{0,1:T(8,128)(2,1)}) %all-gather.5.cloned.1.call-update) | async-done | bytes 1048592 | tf_op jit(solution)/shard_map/all_gather | solution.py:111
  124.3 2.0 fusion.45
  127.0 2.1 fusion.13
  131.1 16.4 %reduce-scatter.11.cloned.1.call-done = bf16[1,8,128,180]{2,1,3,0:T(8,128)(2,1)} async-done(((bf16[2,8,128,180]{2,1,3,0:T(8,128)(2,1)}), bf16[1,8,128,180]{2,1,3,0:T(8,128)(2,1)}) %reduce-scatter.11.cloned.1.call-update) | async-done | bytes 368656 | tf_op jit(solution)/shard_map/reduce_scatter | solution.py:137
  153.0 55.7 %reduce-scatter.15.cloned.1.call-done = bf16[1,128,180]{1,2,0:T(8,128)(2,1)} async-done(((bf16[8,128,180]{1,2,0:T(8,128)(2,1)}), bf16[1,128,180]{1,2,0:T(8,128)(2,1)}) %reduce-scatter.15.cloned.1.call-update) | async-done | bytes 46096
  209.7 44.4 %psum.7 = f32[128]{0:T(128)S(1)} all-reduce(f32[128]{0:T(128)S(1)} %multiply_reduce_fusion.1), channel_id=1, replica_groups=mesh['zh'=2,'y'=4,'x'=4,'zl'=8,'c'=2] {'zl','c'}, use_global_device_ids=true, to_apply=%region_8.9 | all-reduce | flops 128 | bytes 1024 | tf_op jit(solution)/shard_map/psum | solution.py:142
  254.4 2.4 scatter_custom_fusion
  256.9 30.0 %all_to_all.10 = bf16[32,20,180]{2,1,0:T(8,128)(2,1)S(1)} all-to-all(bf16[32,20,180]{2,1,0:T(8,128)(2,1)S(1)} %reshape.312), channel_id=1, replica_groups=mesh['zh'=2,'y'=4,'x'=4,'zl'=8,'c'=2] {'zh','y','x'}, dimensions={0} | all-to-all | bytes 460800 | tf_op jit(solution)/shard_map/all_to_all | solution.py:163
  288.0 62.0 %all-gather.7.cloned.1.call-done = bf16[8,640,180]{1,2,0:T(8,128)(2,1)} async-done(((bf16[1,640,180]{1,2,0:T(8,128)(2,1)}), bf16[8,640,180]{1,2,0:T(8,128)(2,1)}) %all-gather.7.cloned.1.call-update) | async-done | bytes 1843216 | tf_op jit(solution)/shard_map/all_gather | solution.py:170
  349.9 3.0 copy.79
  353.2 1.8 copy.81
  355.0 9.8 %reshape.313 = bf16[8,2,180,360]{2,1,0,3:T(2,128)(2,1)} reshape(bf16[1,2880,2,180]{1,3,2,0:T(8,128)(2,1)S(1)} %copy.81) | data formatting | bytes 4147200 | tf_op jit(solution)/shard_map/reshape | solution.py:172
  364.8 6.4 %reshape.314 = bf16[180,8,2,180]{3,2,1,0:T(2,128)(2,1)S(1)} reshape(bf16[1,180,2880]{2,1,0:T(8,128)(2,1)} %param.23) | data formatting | bytes 2073600 | tf_op jit(solution)/shard_map/reshape | solution.py:182
  371.2 5.6 %all-gather.9.cloned.1.call-done = bf16[16,640,180]{1,0,2:T(8,128)(2,1)} async-done(((bf16[8,640,180]{1,0,2:T(8,128)(2,1)}), bf16[16,640,180]{1,0,2:T(8,128)(2,1)}) %all-gather.9.cloned.1.call-update) | async-done | bytes 3686416 | tf_op jit(solution)/shard_map/all_gather | solution.py:171
  376.8 3.0 copy.80
  379.8 3.0 fusion.8
  382.9 1.8 convert_bitcast_fusion
  384.7 2.6 copy.85
  387.5 23.2 %reduce-scatter.13.cloned.1.call-done = bf16[1,8,640,180]{2,1,3,0:T(8,128)(2,1)} async-done(((bf16[2,8,640,180]{2,1,3,0:T(8,128)(2,1)}), bf16[1,8,640,180]{2,1,3,0:T(8,128)(2,1)}) %reduce-scatter.13.cloned.1.call-update) | async-done | bytes 1843216 | tf_op jit(solution)/shard_map/reduce_scatter | solution.py:186
  410.8 3.0 copy.86
  413.8 69.3 %reduce-scatter.17.cloned.1.call-done = bf16[1,640,180]{1,2,0:T(8,128)(2,1)} async-done(((bf16[8,640,180]{1,2,0:T(8,128)(2,1)}), bf16[1,640,180]{1,2,0:T(8,128)(2,1)}) %reduce-scatter.17.cloned.1.call-update) | async-done | bytes 230416
  485.0 17.0 %all-to-all-start.1 = ((bf16[32,20,180]{2,1,0:T(8,128)(2,1)}), bf16[32,20,180]{2,1,0:T(8,128)(2,1)S(1)}, u32[]{:S(2)}, u32[]{:S(2)}) async-start(bf16[32,20,180]{2,1,0:T(8,128)(2,1)} %reshape_squeeze.3), calls=%async_computation.3 | async-start | bytes 786432 | tf_op jit(solution)/shard_map/all_to_all | solution.py:188
  502.3 22.2 %all-to-all-done.1 = bf16[32,20,180]{2,1,0:T(8,128)(2,1)S(1)} async-done(((bf16[32,20,180]{2,1,0:T(8,128)(2,1)}), bf16[32,20,180]{2,1,0:T(8,128)(2,1)S(1)}, u32[]{:S(2)}, u32[]{:S(2)}) %all-to-all-start.1) | async-done | bytes 230432 | tf_op jit(solution)/shard_map/all_to_all | solution.py:188
  524.6 2.0 gather_fusion
  (84 shorter events, 19.4 us)
Async XLA Ops:
  6.5 122.5 %copy-start = (bf16[128,2880]{0,1:T(8,128)(2,1)S(1)}, bf16[128,2880]{0,1:T(8,128)(2,1)}, u32[]{:S(2)}) copy-start(bf16[128,2880]{0,1:T(8,128)(2,1)} %param.18) | copy-start | bytes 2211844
  6.5 119.7 %copy-start.5 = (f32[2]{0:T(128)S(1)}, f32[2]{0:T(128)}, u32[]{:S(2)}) copy-start(f32[2]{0:T(128)} %param.17) | copy-start | bytes 28
  6.5 117.7 %all-gather.5.cloned.1.call-start = ((), (), s32[]{:S(2)}) async-start(), calls=%async_computation.6 | async-start | bytes 1081344 | tf_op jit(solution)/shard_map/all_gather | solution.py:111
  9.2 138.3 %reduce-scatter.11.cloned.1.call-start = ((), (), s32[]{:S(2)}) async-start(), calls=%async_computation.7 | async-start | bytes 1105920 | tf_op jit(solution)/shard_map/reduce_scatter | solution.py:137
  124.3 2.7 copy-start.2
  129.1 1.6 copy-start.3
  130.7 78.0 %reduce-scatter.15.cloned.1.call-start = ((), (), s32[]{:S(2)}) async-start(), calls=%async_computation.11 | async-start | bytes 423936
  149.3 200.7 %all-gather.7.cloned.1.call-start = ((), (), s32[]{:S(2)}) async-start(), calls=%async_computation.8 | async-start | bytes 2119680 | tf_op jit(solution)/shard_map/all_gather | solution.py:170
  287.9 88.9 %all-gather.9.cloned.1.call-start = ((), (), s32[]{:S(2)}) async-start(), calls=%async_computation.10 | async-start | bytes 5529600 | tf_op jit(solution)/shard_map/all_gather | solution.py:171
  353.0 57.8 %reduce-scatter.13.cloned.1.call-start = ((), (), s32[]{:S(2)}) async-start(), calls=%async_computation.9 | async-start | bytes 5529600 | tf_op jit(solution)/shard_map/reduce_scatter | solution.py:186
  376.8 3.0 copy-start.1
  387.3 95.8 %reduce-scatter.17.cloned.1.call-start = ((), (), s32[]{:S(2)}) async-start(), calls=%async_computation.12 | async-start | bytes 2119680
  410.8 91.4 %copy-start.4 = (f32[128,4]{0,1:T(4,128)S(1)}, f32[128,4]{0,1:T(4,128)}, u32[]{:S(2)}) copy-start(f32[128,4]{0,1:T(4,128)} %param.21) | copy-start | bytes 6148
  485.0 39.5 %all-to-all-start.1 = ((bf16[32,20,180]{2,1,0:T(8,128)(2,1)}), bf16[32,20,180]{2,1,0:T(8,128)(2,1)S(1)}, u32[]{:S(2)}, u32[]{:S(2)}) async-start(bf16[32,20,180]{2,1,0:T(8,128)(2,1)} %reshape_squeeze.3), calls=%async_computation.3 | async-start | bytes 786432 | tf_op jit(solution)/shard_map/all_to_all | solution.py:188
Sparse Core Ops, SparseCore 0:
  11.4 112.7 all-gather.4
  130.8 16.6 reduce-scatter.10
  150.3 58.3 reduce-scatter.14
  288.1 61.8 all-gather.6
  353.1 23.7 all-gather.8
  387.4 23.3 reduce-scatter.12
  413.9 69.0 reduce-scatter.16

commit v2 on v1

--- a/solution.py
+++ b/solution.py
@@ -108,7 +108,21 @@
     )
     key_value = jnp.concatenate([key_rot, value_block], axis=1)
     score_scale = 1.0 / math.sqrt(HEAD_SIZE)
-    block_part = lax.all_gather(key_value, CTX, axis=0, tiled=True)
+    block_part = lax.all_gather(key_value, "zh", axis=0, tiled=False)
+    block_part = lax.all_gather(block_part, "y", axis=0, tiled=False)
+    block_part = lax.all_gather(block_part, "x", axis=0, tiled=False)
+    zh_count = block_part.shape[2]
+    y_count = block_part.shape[1]
+    x_count = block_part.shape[0]
+    block_of_key = (
+        lax.broadcasted_iota(jnp.int32, (x_count, y_count, zh_count), 2) * (y_count * x_count)
+        + lax.broadcasted_iota(jnp.int32, (x_count, y_count, zh_count), 1) * x_count
+        + lax.broadcasted_iota(jnp.int32, (x_count, y_count, zh_count), 0)
+    )
+    key_pos = (
+        block_of_key[:, :, :, None] * tok_rows + jnp.arange(tok_rows, dtype=jnp.int32)
+    ).reshape(-1)
+    block_part = block_part.reshape(-1, 2 * HEAD_SIZE)
     run_max = jnp.broadcast_to(sink_logits[:, None], (local_heads, tok_rows))
     run_total = jnp.ones((local_heads, tok_rows), jnp.float32)
     key_count = block_part.shape[0]
@@ -117,7 +131,6 @@
     scores = (
         jnp.einsum("rhd,kd->hrk", q_rot, key_part, preferred_element_type=jnp.float32) * score_scale
     )
-    key_pos = jnp.arange(key_count, dtype=jnp.int32)
     visible = token_positions[:, None] >= key_pos[None, :]
     scores = jnp.where(visible[None, :, :], scores, neg_large)
     new_max = jnp.maximum(run_max, jnp.max(scores, axis=2))
@@ -139,11 +152,19 @@
     residual_cols = lax.dynamic_slice_in_dim(
         hidden_in, exp_index * col_width, col_width, 1
     ).astype(jnp.float32) + head_cols.astype(jnp.float32)
-    square_sum = lax.psum(jnp.sum(residual_cols * residual_cols, axis=1), EXP)
+    square_part = jnp.sum(residual_cols * residual_cols, axis=1)
+    square_high = square_part.astype(jnp.bfloat16)
+    square_low = (square_part - square_high.astype(jnp.float32)).astype(jnp.bfloat16)
     gain_cols = lax.dynamic_slice_in_dim(norm_gain, exp_index * col_width, col_width, 0)
-    normed_cols = (
-        residual_cols * lax.rsqrt(square_sum / D + 1e-05)[:, None] * gain_cols[None, :]
-    ).astype(jnp.bfloat16)
+    normed_cols = jnp.concatenate(
+        [
+            (residual_cols * gain_cols[None, :]).astype(jnp.bfloat16),
+            square_high[:, None],
+            square_low[:, None],
+        ],
+        axis=1,
+    )
+    send_width = col_width + 2
     exp_local = gate_up.shape[0]
     n_experts = exp_local * ctx_count
     top_count = expert_ids.shape[1]
@@ -151,28 +172,37 @@
     slot_index = route_slots(expert_ids, n_experts)
     dest_row = expert_ids * capacity + slot_index
     spread_rows = jnp.broadcast_to(
-        normed_cols[:, None, :], (tok_rows, top_count, col_width)
-    ).reshape(tok_rows * top_count, col_width)
+        normed_cols[:, None, :], (tok_rows, top_count, send_width)
+    ).reshape(tok_rows * top_count, send_width)
     send_rows = (
-        jnp.zeros((n_experts * capacity, col_width), jnp.bfloat16)
+        jnp.zeros((n_experts * capacity, send_width), jnp.bfloat16)
         .at[dest_row.reshape(-1)]
         .set(spread_rows)
     )
     bucket_rows = ctx_count * capacity
     unit_count = gate_up.shape[-1]
     received = lax.all_to_all(
-        send_rows.reshape(ctx_count, exp_local * capacity, col_width),
+        send_rows.reshape(ctx_count, exp_local * capacity, send_width),
         CTX,
         split_axis=0,
         concat_axis=0,
         tiled=True,
-    ).reshape(bucket_rows, col_width)
+    ).reshape(bucket_rows, send_width)
     gathered = lax.all_gather(received, "zl", axis=0, tiled=False)
     gathered = lax.all_gather(gathered, "c", axis=0, tiled=False)
+    row_squares = jnp.sum(
+        gathered[:, :, :, col_width].astype(jnp.float32)
+        + gathered[:, :, :, col_width + 1].astype(jnp.float32),
+        axis=(0, 1),
+    )
+    row_scale = lax.rsqrt(row_squares / D + 1e-05)
     weights_flat = gate_up.reshape(zl_count, c_count, col_width, 2 * unit_count)
     gate_up_out = jnp.einsum(
-        "czrk,zckf->rf", gathered, weights_flat, preferred_element_type=jnp.float32
-    )
+        "czrk,zckf->rf",
+        gathered[:, :, :, :col_width],
+        weights_flat,
+        preferred_element_type=jnp.float32,
+    ) * row_scale[:, None]
     gate_up_out = gate_up_out.reshape(bucket_rows, 2, unit_count)
     gate_value = gate_up_out[:, 0]
     up_value = gate_up_out[:, 1]

time: 535 us -> 451 us (0.84)
  waiting for transfers between devices: 367 us -> 284 us
  blocking collectives: 74.4 us -> 67.5 us
    all_gather x1, waiting for transfers between devices: 113 us -> 30.5 us  [per_device(): block_part = lax.all_gather(block_part, 'x', axis=0, tiled=False)]
    psum x1 -> x0, blocking collectives: 44.4 us -> none  [per_device(): square_sum = lax.psum(jnp.sum(residual_cols * residual_cols, axis=1), EXP)]
    all_gather x0 -> x2, blocking collectives: none -> 29 us  [the longest x1 15.9 us: per_device(): block_part = lax.all_gather(key_value, 'zh', axis=0, tiled=False)]
    all_to_all x1, blocking collectives: 30 us -> 38.5 us  [per_device(): lax.all_to_all(send_rows.reshape(ctx_count, exp_local * capacity, send_wi...]
  transfers between devices with their start and end apart: 8 -> 8, of which waited for: 8 -> 8; matrix products, arithmetic and copies ran while one was open for 5% -> 6% of each run, Pallas kernels for 0% -> 0%
where the time goes in v2:
time: 451 us; the launch traced here: 450 us
  waiting for transfers between devices  284 us (63%)
  blocking collectives  67.5 us (15%)
  local copies, waits for them, and re-layouts  51.5 us (11%)
  starting transfers between devices  17.5 us (4%)
  between operations  13.9 us (3%)
  matrix products  9.23 us (2%)
  other arithmetic  6.46 us (1%)
    unnamed x9, waiting for transfers between devices  125 us
    all_gather x1, waiting for transfers between devices, per_device(): gathered = lax.all_gather(received, 'zl', axis=0, tiled=False)  57.9 us
    all_to_all x1, blocking collectives, per_device(): lax.all_to_all(send_rows.reshape(ctx_count, exp_local * capacity, send_wi...  38.5 us
    all_gather x1, waiting for transfers between devices, per_device(): block_part = lax.all_gather(block_part, 'x', axis=0, tiled=False)  30.5 us
    reduce_scatter x1, waiting for transfers between devices, per_device(): lax.psum_scatter(partial_value, 'c', scatter_dimension=0, tiled=True)[0]  23.2 us
    all_to_all x1, waiting for transfers between devices, per_device(): lax.all_to_all(expert_cols.reshape(ctx_count, capacity, col_width), CTX,...  22.2 us
    reduce_scatter x1, waiting for transfers between devices, per_device(): lax.psum_scatter(head_part, 'c', scatter_dimension=0, tiled=True)[0]  19.5 us
    all_to_all x1, starting transfers between devices, per_device(): lax.all_to_all(expert_cols.reshape(ctx_count, capacity, col_width), CTX,...  17 us
  transfers between devices with their start and end apart: 8, of which 8 were waited for; matrix products, arithmetic and copies ran while one was open for 6% of the time, Pallas kernels for 0%

profile of v2, /device:TPU:32, one launch (start us, length us, event | category | flops | bytes accessed | tf_op | source)
XLA Modules:
  0.0 450.2 jit_solution(14388736838774526752)
XLA Ops:
  8.5 15.9 %all-gather = bf16[256,128]{0,1:T(8,128)(2,1)S(1)} all-gather(bf16[128,128]{0,1:T(8,128)(2,1)S(1)} %pad_maximum_fusion.1), channel_id=2, replica_groups=mesh['zh'=2,'y'=4,'x'=4,'zl'=8,'c'=2] {'zh'}, dimensions={0}, use_global_device_ids=true | all-gather | bytes 98304 | tf_op jit(solution)/shard_map/all_gather | solution.py:111
  24.6 13.1 %all-gather.1 = bf16[8,128,128]{2,1,0:T(8,128)(2,1)S(1)} all-gather(bf16[2,128,128]{2,1,0:T(8,128)(2,1)S(1)} %bitcast.98), channel_id=3, replica_groups=mesh['zh'=2,'y'=4,'x'=4,'zl'=8,'c'=2] {'y'}, dimensions={0}, use_global_device_ids=true | all-gather | bytes 327680 | tf_op jit(solution)/shard_map/all_gather | solution.py:112
  40.5 1.9 broadcast_compare_fusion
  42.4 30.5 %all-gather.10.cloned.1.call-done = bf16[16,2,128,128]{2,1,0,3:T(2,128)(2,1)} async-done(((bf16[4,2,128,128]{2,1,0,3:T(2,128)(2,1)}), bf16[16,2,128,128]{2,1,0,3:T(2,128)(2,1)}) %all-gather.10.cloned.1.call-update) | async-done | bytes 1048592 | tf_op jit(solution)/shard_map/all_gather | solution.py:113
  76.4 2.1 fusion.21
  80.4 19.5 %reduce-scatter.11.cloned.1.call-done = bf16[1,8,128,180]{2,1,3,0:T(8,128)(2,1)} async-done(((bf16[2,8,128,180]{2,1,3,0:T(8,128)(2,1)}), bf16[1,8,128,180]{2,1,3,0:T(8,128)(2,1)}) %reduce-scatter.11.cloned.1.call-update) | async-done | bytes 368656 | tf_op jit(solution)/shard_map/reduce_scatter | solution.py:150
  105.4 55.7 %reduce-scatter.15.cloned.1.call-done = bf16[1,128,180]{1,2,0:T(8,128)(2,1)} async-done(((bf16[8,128,180]{1,2,0:T(8,128)(2,1)}), bf16[1,128,180]{1,2,0:T(8,128)(2,1)}) %reduce-scatter.15.cloned.1.call-update) | async-done | bytes 46096
  162.8 2.4 scatter_custom_fusion
  165.3 38.5 %all_to_all.10 = bf16[32,20,182]{2,1,0:T(8,128)(2,1)S(1)} all-to-all(bf16[32,20,182]{2,1,0:T(8,128)(2,1)S(1)} %reshape.373), channel_id=1, replica_groups=mesh['zh'=2,'y'=4,'x'=4,'zl'=8,'c'=2] {'zh','y','x'}, dimensions={0} | all-to-all | bytes 465920 | tf_op jit(solution)/shard_map/all_to_all | solution.py:184
  204.8 57.9 %all-gather.8.cloned.1.call-done = bf16[8,640,182]{1,2,0:T(8,128)(2,1)} async-done(((bf16[1,640,182]{1,2,0:T(8,128)(2,1)}), bf16[8,640,182]{1,2,0:T(8,128)(2,1)}) %all-gather.8.cloned.1.call-update) | async-done | bytes 1863696 | tf_op jit(solution)/shard_map/all_gather | solution.py:191
  262.7 3.0 copy.80
  267.6 9.9 %reshape.374 = bf16[8,2,180,360]{2,1,0,3:T(2,128)(2,1)} reshape(bf16[1,2880,2,180]{1,3,2,0:T(8,128)(2,1)S(1)} %copy.82) | data formatting | bytes 4147200 | tf_op jit(solution)/shard_map/reshape | solution.py:199
  277.5 6.4 %reshape.376 = bf16[180,8,2,180]{3,2,1,0:T(2,128)(2,1)S(1)} reshape(bf16[1,180,2880]{2,1,0:T(8,128)(2,1)} %param.23) | data formatting | bytes 2073600 | tf_op jit(solution)/shard_map/reshape | solution.py:212
  283.9 5.7 %all-gather.12.cloned.1.call-done = bf16[16,640,182]{1,0,2:T(8,128)(2,1)} async-done(((bf16[8,640,182]{1,0,2:T(8,128)(2,1)}), bf16[16,640,182]{1,0,2:T(8,128)(2,1)}) %all-gather.12.cloned.1.call-update) | async-done | bytes 3727376 | tf_op jit(solution)/shard_map/all_gather | solution.py:192
  289.7 3.0 copy.81
  292.8 4.1 fusion.14
  298.2 1.8 convert_bitcast_fusion
  300.0 2.6 copy.85
  302.9 23.2 %reduce-scatter.13.cloned.1.call-done = bf16[1,8,640,180]{2,1,3,0:T(8,128)(2,1)} async-done(((bf16[2,8,640,180]{2,1,3,0:T(8,128)(2,1)}), bf16[1,8,640,180]{2,1,3,0:T(8,128)(2,1)}) %reduce-scatter.13.cloned.1.call-update) | async-done | bytes 1843216 | tf_op jit(solution)/shard_map/reduce_scatter | solution.py:216
  326.1 3.0 copy.86
  329.1 69.3 %reduce-scatter.17.cloned.1.call-done = bf16[1,640,180]{1,2,0:T(8,128)(2,1)} async-done(((bf16[8,640,180]{1,2,0:T(8,128)(2,1)}), bf16[1,640,180]{1,2,0:T(8,128)(2,1)}) %reduce-scatter.17.cloned.1.call-update) | async-done | bytes 230416
  400.4 17.0 %all-to-all-start.1 = ((bf16[32,20,180]{2,1,0:T(8,128)(2,1)}), bf16[32,20,180]{2,1,0:T(8,128)(2,1)S(1)}, u32[]{:S(2)}, u32[]{:S(2)}) async-start(bf16[32,20,180]{2,1,0:T(8,128)(2,1)} %reshape_squeeze.3), calls=%async_computation.3 | async-start | bytes 786432 | tf_op jit(solution)/shard_map/all_to_all | solution.py:218
  417.7 22.2 %all-to-all-done.1 = bf16[32,20,180]{2,1,0:T(8,128)(2,1)S(1)} async-done(((bf16[32,20,180]{2,1,0:T(8,128)(2,1)}), bf16[32,20,180]{2,1,0:T(8,128)(2,1)S(1)}, u32[]{:S(2)}, u32[]{:S(2)}) %all-to-all-start.1) | async-done | bytes 230432 | tf_op jit(solution)/shard_map/all_to_all | solution.py:218
  440.0 2.0 gather_fusion
  (96 shorter events, 25.6 us)
Async XLA Ops:
  6.5 71.9 %copy-start = (bf16[128,2880]{0,1:T(8,128)(2,1)S(1)}, bf16[128,2880]{0,1:T(8,128)(2,1)}, u32[]{:S(2)}) copy-start(bf16[128,2880]{0,1:T(8,128)(2,1)} %param.18) | copy-start | bytes 2211844
  6.5 66.4 %all-gather.10.cloned.1.call-start = ((), (), s32[]{:S(2)}) async-start(), calls=%async_computation.9 | async-start | bytes 1310720 | tf_op jit(solution)/shard_map/all_gather | solution.py:113
  38.6 61.3 %reduce-scatter.11.cloned.1.call-start = ((), (), s32[]{:S(2)}) async-start(), calls=%async_computation.6 | async-start | bytes 1105920 | tf_op jit(solution)/shard_map/reduce_scatter | solution.py:150
  42.4 33.3 %copy-start.4 = (f32[2]{0:T(128)S(1)}, f32[2]{0:T(128)}, u32[]{:S(2)}) copy-start(f32[2]{0:T(128)} %param.17) | copy-start | bytes 28
  78.4 1.6 copy-start.2
  80.0 81.1 %reduce-scatter.15.cloned.1.call-start = ((), (), s32[]{:S(2)}) async-start(), calls=%async_computation.11 | async-start | bytes 423936
  101.7 161.0 %all-gather.8.cloned.1.call-start = ((), (), s32[]{:S(2)}) async-start(), calls=%async_computation.7 | async-start | bytes 2119680 | tf_op jit(solution)/shard_map/all_gather | solution.py:191
  204.8 84.9 %all-gather.12.cloned.1.call-start = ((), (), s32[]{:S(2)}) async-start(), calls=%async_computation.10 | async-start | bytes 5591040 | tf_op jit(solution)/shard_map/all_gather | solution.py:192
  265.7 60.4 %reduce-scatter.13.cloned.1.call-start = ((), (), s32[]{:S(2)}) async-start(), calls=%async_computation.8 | async-start | bytes 5529600 | tf_op jit(solution)/shard_map/reduce_scatter | solution.py:216
  289.7 3.1 copy-start.1
  302.6 95.8 %reduce-scatter.17.cloned.1.call-start = ((), (), s32[]{:S(2)}) async-start(), calls=%async_computation.12 | async-start | bytes 2119680
  326.1 91.5 %copy-start.3 = (f32[128,4]{0,1:T(4,128)S(1)}, f32[128,4]{0,1:T(4,128)}, u32[]{:S(2)}) copy-start(f32[128,4]{0,1:T(4,128)} %param.21) | copy-start | bytes 6148
  400.4 39.5 %all-to-all-start.1 = ((bf16[32,20,180]{2,1,0:T(8,128)(2,1)}), bf16[32,20,180]{2,1,0:T(8,128)(2,1)S(1)}, u32[]{:S(2)}, u32[]{:S(2)}) async-start(bf16[32,20,180]{2,1,0:T(8,128)(2,1)} %reshape_squeeze.3), calls=%async_computation.3 | async-start | bytes 786432 | tf_op jit(solution)/shard_map/all_to_all | solution.py:218
Sparse Core Ops, SparseCore 0:
  38.7 34.1 all-gather.9
  80.1 19.6 reduce-scatter.10
  102.7 58.3 reduce-scatter.14
  204.9 57.7 all-gather.7
  265.9 23.7 all-gather.11
  302.7 23.3 reduce-scatter.12
  329.3 69.1 reduce-scatter.16

commit v3 on v2

--- a/solution.py
+++ b/solution.py
@@ -90,6 +90,7 @@
     local_heads = query_input.shape[1] // HEAD_SIZE
     ctx_index = lax.axis_index(CTX)
     exp_index = lax.axis_index(EXP)
+    col_width = D // exp_count
     token_positions = ctx_index * tok_rows + jnp.arange(tok_rows, dtype=jnp.int32)
     q_rot = rotate_with_yarn(
         query_input.astype(jnp.float32).reshape(tok_rows, local_heads, HEAD_SIZE), token_positions
@@ -144,14 +145,13 @@
         .reshape(tok_rows, local_heads * HEAD_SIZE)
         .astype(jnp.bfloat16)
     )
-    col_width = D // exp_count
     head_part = jnp.dot(attended, out_proj, preferred_element_type=jnp.float32).astype(jnp.bfloat16)
-    head_part = head_part.reshape(tok_rows, zl_count, c_count, col_width).transpose(2, 1, 0, 3)
-    head_part = lax.psum_scatter(head_part, "c", scatter_dimension=0, tiled=True)[0]
-    head_cols = lax.psum_scatter(head_part, "zl", scatter_dimension=0, tiled=True)[0]
+    head_part = head_part.reshape(tok_rows, exp_count, col_width).transpose(1, 0, 2)
+    head_part = lax.all_to_all(head_part, EXP, split_axis=0, concat_axis=0, tiled=True)
+    head_cols = jnp.sum(head_part.astype(jnp.float32), axis=0)
     residual_cols = lax.dynamic_slice_in_dim(
         hidden_in, exp_index * col_width, col_width, 1
-    ).astype(jnp.float32) + head_cols.astype(jnp.float32)
+    ).astype(jnp.float32) + head_cols
     square_part = jnp.sum(residual_cols * residual_cols, axis=1)
     square_high = square_part.astype(jnp.bfloat16)
     square_low = (square_part - square_high.astype(jnp.float32)).astype(jnp.bfloat16)

time: 451 us -> 417 us (0.925)
  waiting for transfers between devices: 284 us -> 240 us
  starting transfers between devices: 17.5 us -> 27.7 us
  local copies, waits for them, and re-layouts: 51.5 us -> 46.9 us
    unnamed x9 -> x6, waiting for transfers between devices: 125 us -> 69.4 us
    all_to_all x0 -> x1, waiting for transfers between devices: none -> 30.3 us  [per_device(): lax.all_to_all(head_part, EXP, split_axis=0, concat_axis=0, tiled=True)]
    reduce_scatter x1 -> x0, waiting for transfers between devices: 19.5 us -> none  [per_device(): lax.psum_scatter(head_part, 'c', scatter_dimension=0, tiled=True)[0]]
    all_to_all x0 -> x1, starting transfers between devices: none -> 10.5 us  [per_device(): lax.all_to_all(head_part, EXP, split_axis=0, concat_axis=0, tiled=True)]
  transfers between devices with their start and end apart: 8 -> 7, of which waited for: 8 -> 7; matrix products, arithmetic and copies ran while one was open for 6% -> 6% of each run, Pallas kernels for 0% -> 0%
where the time goes in v3:
time: 417 us; the launch traced here: 416 us
  waiting for transfers between devices  240 us (58%)
  blocking collectives  70.1 us (17%)
  local copies, waits for them, and re-layouts  46.9 us (11%)
  starting transfers between devices  27.7 us (7%)
  between operations  13.5 us (3%)
  matrix products  9.23 us (2%)
  other arithmetic  8.73 us (2%)
    unnamed x6, waiting for transfers between devices  69.4 us
    all_gather x1, waiting for transfers between devices, per_device(): gathered = lax.all_gather(received, 'zl', axis=0, tiled=False)  58.2 us
    all_to_all x1, blocking collectives, per_device(): lax.all_to_all(send_rows.reshape(ctx_count, exp_local * capacity, send_wi...  41.1 us
    all_gather x1, waiting for transfers between devices, per_device(): block_part = lax.all_gather(block_part, 'x', axis=0, tiled=False)  30.6 us
    all_to_all x1, waiting for transfers between devices, per_device(): lax.all_to_all(head_part, EXP, split_axis=0, concat_axis=0, tiled=True)  30.3 us
    reduce_scatter x1, waiting for transfers between devices, per_device(): lax.psum_scatter(partial_value, 'c', scatter_dimension=0, tiled=True)[0]  23.2 us
    all_to_all x1, waiting for transfers between devices, per_device(): lax.all_to_all(expert_cols.reshape(ctx_count, capacity, col_width), CTX,...  22.2 us
    all_to_all x1, starting transfers between devices, per_device(): lax.all_to_all(expert_cols.reshape(ctx_count, capacity, col_width), CTX,...  16.9 us
  transfers between devices with their start and end apart: 7, of which 7 were waited for; matrix products, arithmetic and copies ran while one was open for 6% of the time, Pallas kernels for 0%

profile of v3, /device:TPU:32, one launch (start us, length us, event | category | flops | bytes accessed | tf_op | source)
XLA Modules:
  0.0 415.8 jit_solution(14578538444073572695)
XLA Ops:
  8.5 15.9 %all-gather = bf16[256,128]{0,1:T(8,128)(2,1)S(1)} all-gather(bf16[128,128]{0,1:T(8,128)(2,1)S(1)} %pad_maximum_fusion.1), channel_id=2, replica_groups=mesh['zh'=2,'y'=4,'x'=4,'zl'=8,'c'=2] {'zh'}, dimensions={0}, use_global_device_ids=true | all-gather | bytes 98304 | tf_op jit(solution)/shard_map/all_gather | solution.py:112
  24.6 13.1 %all-gather.1 = bf16[8,128,128]{2,1,0:T(8,128)(2,1)S(1)} all-gather(bf16[2,128,128]{2,1,0:T(8,128)(2,1)S(1)} %bitcast.90), channel_id=3, replica_groups=mesh['zh'=2,'y'=4,'x'=4,'zl'=8,'c'=2] {'y'}, dimensions={0}, use_global_device_ids=true | all-gather | bytes 327680 | tf_op jit(solution)/shard_map/all_gather | solution.py:113
  40.5 1.9 broadcast_compare_fusion
  42.3 30.6 %all-gather.10.cloned.1.call-done = bf16[16,2,128,128]{2,1,0,3:T(2,128)(2,1)} async-done(((bf16[4,2,128,128]{2,1,0,3:T(2,128)(2,1)}), bf16[16,2,128,128]{2,1,0,3:T(2,128)(2,1)}) %all-gather.10.cloned.1.call-update) | async-done | bytes 1048592 | tf_op jit(solution)/shard_map/all_gather | solution.py:114
  76.4 2.1 fusion.21
  79.8 10.5 %all-to-all-start = ((bf16[16,128,180]{1,2,0:T(8,128)(2,1)}), bf16[16,128,180]{1,2,0:T(8,128)(2,1)S(1)}, u32[]{:S(2)}, u32[]{:S(2)}) async-start(bf16[16,128,180]{1,2,0:T(8,128)(2,1)} %bitcast.13), calls=%async_computation | async-start | bytes 1507328 | tf_op jit(solution)/shard_map/all_to_all | solution.py:150
  93.4 30.3 %all-to-all-done = bf16[16,128,180]{1,2,0:T(8,128)(2,1)S(1)} async-done(((bf16[16,128,180]{1,2,0:T(8,128)(2,1)}), bf16[16,128,180]{1,2,0:T(8,128)(2,1)S(1)}, u32[]{:S(2)}, u32[]{:S(2)}) %all-to-all-start) | async-done | bytes 737312 | tf_op jit(solution)/shard_map/all_to_all | solution.py:150
  125.1 2.4 scatter_custom_fusion
  127.6 41.1 %all_to_all.15 = bf16[32,20,182]{2,1,0:T(8,128)(2,1)S(1)} all-to-all(bf16[32,20,182]{2,1,0:T(8,128)(2,1)S(1)} %reshape.371), channel_id=1, replica_groups=mesh['zh'=2,'y'=4,'x'=4,'zl'=8,'c'=2] {'zh','y','x'}, dimensions={0} | all-to-all | bytes 465920 | tf_op jit(solution)/shard_map/all_to_all | solution.py:184
  169.7 58.2 %all-gather.8.cloned.1.call-done = bf16[8,640,182]{1,2,0:T(8,128)(2,1)} async-done(((bf16[1,640,182]{1,2,0:T(8,128)(2,1)}), bf16[8,640,182]{1,2,0:T(8,128)(2,1)}) %all-gather.8.cloned.1.call-update) | async-done | bytes 1863696 | tf_op jit(solution)/shard_map/all_gather | solution.py:191
  228.0 3.0 copy.91
  232.9 9.9 %reshape.372 = bf16[8,2,180,360]{2,1,0,3:T(2,128)(2,1)} reshape(bf16[1,2880,2,180]{1,3,2,0:T(8,128)(2,1)S(1)} %copy.93) | data formatting | bytes 4147200 | tf_op jit(solution)/shard_map/reshape | solution.py:199
  242.8 6.4 %reshape.374 = bf16[180,8,2,180]{3,2,1,0:T(2,128)(2,1)S(1)} reshape(bf16[1,180,2880]{2,1,0:T(8,128)(2,1)} %param.23) | data formatting | bytes 2073600 | tf_op jit(solution)/shard_map/reshape | solution.py:212
  249.2 5.7 %all-gather.12.cloned.1.call-done = bf16[16,640,182]{1,0,2:T(8,128)(2,1)} async-done(((bf16[8,640,182]{1,0,2:T(8,128)(2,1)}), bf16[16,640,182]{1,0,2:T(8,128)(2,1)}) %all-gather.12.cloned.1.call-update) | async-done | bytes 3727376 | tf_op jit(solution)/shard_map/all_gather | solution.py:192
  254.9 3.0 copy.92
  258.0 4.1 fusion.14
  263.4 1.8 convert_bitcast_fusion
  265.3 2.6 copy.96
  268.1 23.2 %reduce-scatter.6.cloned.1.call-done = bf16[1,8,640,180]{2,1,3,0:T(8,128)(2,1)} async-done(((bf16[2,8,640,180]{2,1,3,0:T(8,128)(2,1)}), bf16[1,8,640,180]{2,1,3,0:T(8,128)(2,1)}) %reduce-scatter.6.cloned.1.call-update) | async-done | bytes 1843216 | tf_op jit(solution)/shard_map/reduce_scatter | solution.py:216
  291.4 3.0 copy.97
  294.4 69.3 %reduce-scatter.8.cloned.1.call-done = bf16[1,640,180]{1,2,0:T(8,128)(2,1)} async-done(((bf16[8,640,180]{1,2,0:T(8,128)(2,1)}), bf16[1,640,180]{1,2,0:T(8,128)(2,1)}) %reduce-scatter.8.cloned.1.call-update) | async-done | bytes 230416
  365.7 16.9 %all-to-all-start.2 = ((bf16[32,20,180]{2,1,0:T(8,128)(2,1)}), bf16[32,20,180]{2,1,0:T(8,128)(2,1)S(1)}, u32[]{:S(2)}, u32[]{:S(2)}) async-start(bf16[32,20,180]{2,1,0:T(8,128)(2,1)} %reshape_squeeze.3), calls=%async_computation.3 | async-start | bytes 786432 | tf_op jit(solution)/shard_map/all_to_all | solution.py:218
  382.9 22.2 %all-to-all-done.2 = bf16[32,20,180]{2,1,0:T(8,128)(2,1)S(1)} async-done(((bf16[32,20,180]{2,1,0:T(8,128)(2,1)}), bf16[32,20,180]{2,1,0:T(8,128)(2,1)S(1)}, u32[]{:S(2)}, u32[]{:S(2)}) %all-to-all-start.2) | async-done | bytes 230432 | tf_op jit(solution)/shard_map/all_to_all | solution.py:218
  405.2 2.0 gather_fusion
  (87 shorter events, 23.2 us)
Async XLA Ops:
  6.5 71.9 %copy-start = (bf16[128,2880]{0,1:T(8,128)(2,1)S(1)}, bf16[128,2880]{0,1:T(8,128)(2,1)}, u32[]{:S(2)}) copy-start(bf16[128,2880]{0,1:T(8,128)(2,1)} %param.18) | copy-start | bytes 2211844
  6.5 66.4 %all-gather.10.cloned.1.call-start = ((), (), s32[]{:S(2)}) async-start(), calls=%async_computation.7 | async-start | bytes 1310720 | tf_op jit(solution)/shard_map/all_gather | solution.py:114
  42.3 33.3 %copy-start.4 = (f32[2]{0:T(128)S(1)}, f32[2]{0:T(128)}, u32[]{:S(2)}) copy-start(f32[2]{0:T(128)} %param.17) | copy-start | bytes 28
  76.4 13.9 %copy-start.2 = (s32[128,4]{0,1:T(4,128)S(1)}, s32[128,4]{0,1:T(4,128)}, u32[]{:S(2)}) copy-start(s32[128,4]{0,1:T(4,128)} %param.20) | copy-start | bytes 6148
  79.8 43.9 %all-to-all-start = ((bf16[16,128,180]{1,2,0:T(8,128)(2,1)}), bf16[16,128,180]{1,2,0:T(8,128)(2,1)S(1)}, u32[]{:S(2)}, u32[]{:S(2)}) async-start(bf16[16,128,180]{1,2,0:T(8,128)(2,1)} %bitcast.13), calls=%async_computation | async-start | bytes 1507328 | tf_op jit(solution)/shard_map/all_to_all | solution.py:150
  90.3 137.7 %all-gather.8.cloned.1.call-start = ((), (), s32[]{:S(2)}) async-start(), calls=%async_computation.5 | async-start | bytes 2119680 | tf_op jit(solution)/shard_map/all_gather | solution.py:191
  169.7 85.2 %all-gather.12.cloned.1.call-start = ((), (), s32[]{:S(2)}) async-start(), calls=%async_computation.8 | async-start | bytes 5591040 | tf_op jit(solution)/shard_map/all_gather | solution.py:192
  231.0 60.4 %reduce-scatter.6.cloned.1.call-start = ((), (), s32[]{:S(2)}) async-start(), calls=%async_computation.6 | async-start | bytes 5529600 | tf_op jit(solution)/shard_map/reduce_scatter | solution.py:216
  254.9 3.1 copy-start.1
  267.8 95.9 %reduce-scatter.8.cloned.1.call-start = ((), (), s32[]{:S(2)}) async-start(), calls=%async_computation.9 | async-start | bytes 2119680
  291.4 91.4 %copy-start.3 = (f32[128,4]{0,1:T(4,128)S(1)}, f32[128,4]{0,1:T(4,128)}, u32[]{:S(2)}) copy-start(f32[128,4]{0,1:T(4,128)} %param.21) | copy-start | bytes 6148
  365.7 39.4 %all-to-all-start.2 = ((bf16[32,20,180]{2,1,0:T(8,128)(2,1)}), bf16[32,20,180]{2,1,0:T(8,128)(2,1)S(1)}, u32[]{:S(2)}, u32[]{:S(2)}) async-start(bf16[32,20,180]{2,1,0:T(8,128)(2,1)} %reshape_squeeze.3), calls=%async_computation.3 | async-start | bytes 786432 | tf_op jit(solution)/shard_map/all_to_all | solution.py:218
Sparse Core Ops, SparseCore 0:
  38.7 34.1 all-gather.9
  169.8 58.1 all-gather.7
  231.1 23.7 all-gather.11
  268.0 23.3 reduce-scatter.5
  294.5 69.1 reduce-scatter.7

commit v4 on v3

--- a/solution.py
+++ b/solution.py
@@ -65,7 +65,8 @@
 
 
 CTX = ("zh", "y", "x")
-EXP = ("zl", "c")
+ZL = ("zlh", "zll")
+EXP = ("zlh", "zll", "c")
 
 
 def per_device(
@@ -188,7 +189,7 @@
         concat_axis=0,
         tiled=True,
     ).reshape(bucket_rows, send_width)
-    gathered = lax.all_gather(received, "zl", axis=0, tiled=False)
+    gathered = lax.all_gather(received, ZL, axis=0, tiled=False)
     gathered = lax.all_gather(gathered, "c", axis=0, tiled=False)
     row_squares = jnp.sum(
         gathered[:, :, :, col_width].astype(jnp.float32)
@@ -209,12 +210,17 @@
     activated = ((up_value + 1.0) * gate_value * jax.nn.sigmoid(1.702 * gate_value)).astype(
         jnp.bfloat16
     )
-    down_local = down_proj.reshape(unit_count, zl_count, c_count, col_width)
+    zlh_count = zl_count // 2
+    down_local = down_proj.reshape(unit_count, zlh_count, 2, c_count, col_width)
     partial_value = jnp.einsum(
-        "rf,fzcd->czrd", activated, down_local, preferred_element_type=jnp.float32
+        "rf,fhlcd->chlrd", activated, down_local, preferred_element_type=jnp.float32
     ).astype(jnp.bfloat16)
-    partial_value = lax.psum_scatter(partial_value, "c", scatter_dimension=0, tiled=True)[0]
-    expert_cols = lax.psum_scatter(partial_value, "zl", scatter_dimension=0, tiled=True)[0]
+    partial_value = lax.all_to_all(partial_value, "c", 0, 0, tiled=True)
+    partial_value = jnp.sum(partial_value.astype(jnp.float32), axis=0).astype(jnp.bfloat16)
+    partial_value = lax.all_to_all(partial_value.transpose(1, 0, 2, 3), "zll", 0, 0, tiled=True)
+    partial_value = jnp.sum(partial_value.astype(jnp.float32), axis=0).astype(jnp.bfloat16)
+    partial_value = lax.all_to_all(partial_value, "zlh", 0, 0, tiled=True)
+    expert_cols = jnp.sum(partial_value.astype(jnp.float32), axis=0).astype(jnp.bfloat16)
     returned = lax.all_to_all(
         expert_cols.reshape(ctx_count, capacity, col_width),
         CTX,
@@ -232,7 +238,9 @@
     zh, y, x = (mesh.devices.shape[0] // 16, 4, 4)
     c_count = 2
     zl_count = exp_count // c_count
-    fine = Mesh(mesh.devices.reshape(zh, y, x, zl_count, c_count), ("zh", "y", "x", "zl", "c"))
+    fine = Mesh(
+        mesh.devices.reshape(zh, y, x, zl_count // 2, 2, c_count), ("zh", "y", "x", "zlh", "zll", "c")
+    )
     placed = (
         P(CTX, None),
         P(CTX, EXP),

time: 417 us -> 409 us (0.981)
  the two profiles are of different devices: /device:TPU:32 before, /device:TPU:64 now
where the time goes in v4:
time: 409 us; the launch traced here: 408 us
  waiting for transfers between devices  156 us (38%)
  blocking collectives  147 us (36%)
  local copies, waits for them, and re-layouts  43.8 us (11%)
  starting transfers between devices  22.1 us (5%)
  other arithmetic  15.9 us (4%)
  between operations  13.6 us (3%)
  matrix products  9.23 us (2%)
    all_gather x1, waiting for transfers between devices, per_device(): gathered = lax.all_gather(received, ZL, axis=0, tiled=False)  61.6 us
    all_to_all x1, blocking collectives, per_device(): partial_value = lax.all_to_all(partial_value, 'zlh', 0, 0, tiled=True)  52.8 us
    all_to_all x1, blocking collectives, per_device(): lax.all_to_all(send_rows.reshape(ctx_count, exp_local * capacity, send_wi...  33.4 us
    all_to_all x1, waiting for transfers between devices, per_device(): lax.all_to_all(head_part, EXP, split_axis=0, concat_axis=0, tiled=True)  32.5 us
    all_gather x1, waiting for transfers between devices, per_device(): block_part = lax.all_gather(block_part, 'x', axis=0, tiled=False)  31.1 us
    all_to_all x1, blocking collectives, per_device(): lax.all_to_all(partial_value.transpose(1, 0, 2, 3), 'zll', 0, 0, tiled=True)  25.3 us
    all_to_all x1, waiting for transfers between devices, per_device(): lax.all_to_all(expert_cols.reshape(ctx_count, capacity, col_width), CTX,...  23.3 us
    all_gather x1, blocking collectives, per_device(): block_part = lax.all_gather(key_value, 'zh', axis=0, tiled=False)  15 us
  transfers between devices with their start and end apart: 5, of which 5 were waited for; matrix products, arithmetic and copies ran while one was open for 6% of the time, Pallas kernels for 0%

profile of v4, /device:TPU:64, one launch (start us, length us, event | category | flops | bytes accessed | tf_op | source)
XLA Modules:
  0.0 408.4 jit_solution(3406970214370340965)
XLA Ops:
  8.5 15.0 %all-gather = bf16[256,128]{0,1:T(8,128)(2,1)S(1)} all-gather(bf16[128,128]{0,1:T(8,128)(2,1)S(1)} %pad_maximum_fusion.1), channel_id=2, replica_groups=mesh['zh'=2,'y'=4,'x'=4,'zlh'=4,'zll'=2,'c'=2] {'zh'}, dimensions={0}, use_global_device_ids=true | all-gather | bytes 98304 | tf_op jit(solution)/shard_map/all_gather | solution.py:113
  23.7 13.1 %all-gather.1 = bf16[8,128,128]{2,1,0:T(8,128)(2,1)S(1)} all-gather(bf16[2,128,128]{2,1,0:T(8,128)(2,1)S(1)} %bitcast.91), channel_id=3, replica_groups=mesh['zh'=2,'y'=4,'x'=4,'zlh'=4,'zll'=2,'c'=2] {'y'}, dimensions={0}, use_global_device_ids=true | all-gather | bytes 327680 | tf_op jit(solution)/shard_map/all_gather | solution.py:114
  41.5 31.1 %all-gather.10.cloned.1.call-done = bf16[16,2,128,128]{2,1,0,3:T(2,128)(2,1)} async-done(((bf16[4,2,128,128]{2,1,0,3:T(2,128)(2,1)}), bf16[16,2,128,128]{2,1,0,3:T(2,128)(2,1)}) %all-gather.10.cloned.1.call-update) | async-done | bytes 1048592 | tf_op jit(solution)/shard_map/all_gather | solution.py:115
  76.0 2.1 fusion.21
  79.4 10.4 %all-to-all-start = ((bf16[16,128,180]{1,2,0:T(8,128)(2,1)}), bf16[16,128,180]{1,2,0:T(8,128)(2,1)S(1)}, u32[]{:S(2)}, u32[]{:S(2)}) async-start(bf16[16,128,180]{1,2,0:T(8,128)(2,1)} %bitcast.13), calls=%async_computation | async-start | bytes 1507328 | tf_op jit(solution)/shard_map/all_to_all | solution.py:151
  93.0 32.5 %all-to-all-done = bf16[16,128,180]{1,2,0:T(8,128)(2,1)S(1)} async-done(((bf16[16,128,180]{1,2,0:T(8,128)(2,1)}), bf16[16,128,180]{1,2,0:T(8,128)(2,1)S(1)}, u32[]{:S(2)}, u32[]{:S(2)}) %all-to-all-start) | async-done | bytes 737312 | tf_op jit(solution)/shard_map/all_to_all | solution.py:151
  127.5 2.4 scatter_custom_fusion
  130.0 33.4 %all_to_all.30 = bf16[32,20,182]{2,1,0:T(8,128)(2,1)S(1)} all-to-all(bf16[32,20,182]{2,1,0:T(8,128)(2,1)S(1)} %reshape.374), channel_id=1, replica_groups=mesh['zh'=2,'y'=4,'x'=4,'zlh'=4,'zll'=2,'c'=2] {'zh','y','x'}, dimensions={0} | all-to-all | bytes 465920 | tf_op jit(solution)/shard_map/all_to_all | solution.py:185
  164.6 61.6 %all-gather.8.cloned.1.call-done = bf16[8,640,182]{1,2,0:T(8,128)(2,1)} async-done(((bf16[1,640,182]{1,2,0:T(8,128)(2,1)}), bf16[8,640,182]{1,2,0:T(8,128)(2,1)}) %all-gather.8.cloned.1.call-update) | async-done | bytes 1863696 | tf_op jit(solution)/shard_map/all_gather | solution.py:192
  226.3 3.0 copy.91
  231.1 9.7 %reshape.375 = bf16[8,2,180,360]{2,1,0,3:T(2,128)(2,1)} reshape(bf16[1,2880,2,180]{1,3,2,0:T(8,128)(2,1)S(1)} %copy.93) | data formatting | bytes 4147200 | tf_op jit(solution)/shard_map/reshape | solution.py:200
  240.9 6.4 %reshape.377 = bf16[180,4,2,2,180]{4,3,2,1,0:T(2,128)(2,1)S(1)} reshape(bf16[1,180,2880]{2,1,0:T(8,128)(2,1)} %param.23) | data formatting | bytes 2073600 | tf_op jit(solution)/shard_map/reshape | solution.py:214
  247.3 7.9 %all-gather.12.cloned.1.call-done = bf16[16,640,182]{1,0,2:T(8,128)(2,1)} async-done(((bf16[8,640,182]{1,0,2:T(8,128)(2,1)}), bf16[16,640,182]{1,0,2:T(8,128)(2,1)}) %all-gather.12.cloned.1.call-update) | async-done | bytes 3727376 | tf_op jit(solution)/shard_map/all_gather | solution.py:193
  255.2 3.0 copy.92
  258.3 4.1 %fusion.14 = f32[640,360]{0,1:T(8,128)} fusion(bf16[8,2,180,360]{2,1,0,3:T(2,128)(2,1)S(1)} %copy-done.1, bf16[2,8,640,182]{2,3,1,0:T(8,128)(2,1)S(1)} %bitcast.89, f32[640]{0:T(1024)S(1)} %add_rsqrt_fusion), kind=kOutput, calls=%fused_computation.18 | convolution fusion | flops 1327334400 | bytes 6725120 | tf_op jit(solution)/shard_map/czrk,zckf->rf/dot_general | solution.py:201
  265.5 1.9 copy.96
  267.4 7.7 %all_to_all.31 = bf16[2,4,2,640,180]{3,1,4,2,0:T(4,128)(2,1)} all-to-all(bf16[2,4,2,640,180]{3,1,4,2,0:T(4,128)(2,1)S(1)} %copy.96), channel_id=1, replica_groups=mesh['zh'=2,'y'=4,'x'=4,'zlh'=4,'zll'=2,'c'=2] {'c'}, dimensions={0} | all-to-all | bytes 7372800 | tf_op jit(solution)/shard_map/all_to_all | solution.py:218
  275.2 5.0 %reduce_sum.98 = bf16[4,2,640,180]{2,0,3,1:T(4,128)(2,1)S(1)} reduce(bf16[2,4,2,640,180]{3,1,4,2,0:T(4,128)(2,1)} %all_to_all.31, bf16[]{:T(256)} %constant.89.clone.1), dimensions={0}, to_apply=%region_9.10 | reduce | flops 921600 | bytes 5529602 | tf_op jit(solution)/shard_map/reduce_sum | solution.py:219
  281.2 25.3 %all_to_all.32 = bf16[2,4,640,180]{2,1,3,0:T(4,128)(2,1)S(1)} all-to-all(bf16[2,4,640,180]{2,1,3,0:T(4,128)(2,1)S(1)} %copy.98), channel_id=1, replica_groups=mesh['zh'=2,'y'=4,'x'=4,'zlh'=4,'zll'=2,'c'=2] {'zll'}, dimensions={0} | all-to-all | bytes 3686400 | tf_op jit(solution)/shard_map/all_to_all | solution.py:220
  306.4 2.0 reduce_sum.99
  308.6 52.8 %all_to_all.33 = bf16[4,640,180]{1,2,0:T(8,128)(2,1)S(1)} all-to-all(bf16[4,640,180]{1,2,0:T(8,128)(2,1)S(1)} %copy.99), channel_id=1, replica_groups=mesh['zh'=2,'y'=4,'x'=4,'zlh'=4,'zll'=2,'c'=2] {'zlh'}, dimensions={0} | all-to-all | bytes 1843200 | tf_op jit(solution)/shard_map/all_to_all | solution.py:222
  362.6 11.5 %all-to-all-start.5 = ((bf16[32,20,180]{2,1,0:T(8,128)(2,1)}), bf16[32,20,180]{2,1,0:T(8,128)(2,1)S(1)}, u32[]{:S(2)}, u32[]{:S(2)}) async-start(bf16[32,20,180]{2,1,0:T(8,128)(2,1)} %reshape.378), calls=%async_computation.5 | async-start | bytes 786432 | tf_op jit(solution)/shard_map/all_to_all | solution.py:224
  374.4 23.3 %all-to-all-done.5 = bf16[32,20,180]{2,1,0:T(8,128)(2,1)S(1)} async-done(((bf16[32,20,180]{2,1,0:T(8,128)(2,1)}), bf16[32,20,180]{2,1,0:T(8,128)(2,1)S(1)}, u32[]{:S(2)}, u32[]{:S(2)}) %all-to-all-start.5) | async-done | bytes 230432 | tf_op jit(solution)/shard_map/all_to_all | solution.py:224
  397.8 2.0 gather_fusion
  (93 shorter events, 27.7 us)
Async XLA Ops:
  6.5 71.5 %copy-start = (bf16[128,2880]{0,1:T(8,128)(2,1)S(1)}, bf16[128,2880]{0,1:T(8,128)(2,1)}, u32[]{:S(2)}) copy-start(bf16[128,2880]{0,1:T(8,128)(2,1)} %param.18) | copy-start | bytes 2211844
  6.5 66.0 %all-gather.10.cloned.1.call-start = ((), (), s32[]{:S(2)}) async-start(), calls=%async_computation.7 | async-start | bytes 1310720 | tf_op jit(solution)/shard_map/all_gather | solution.py:115
  41.5 33.8 %copy-start.6 = (f32[2]{0:T(128)S(1)}, f32[2]{0:T(128)}, u32[]{:S(2)}) copy-start(f32[2]{0:T(128)} %param.17) | copy-start | bytes 28
  76.0 13.9 %copy-start.4 = (s32[128,4]{0,1:T(4,128)S(1)}, s32[128,4]{0,1:T(4,128)}, u32[]{:S(2)}) copy-start(s32[128,4]{0,1:T(4,128)} %param.20) | copy-start | bytes 6148
  79.4 46.0 %all-to-all-start = ((bf16[16,128,180]{1,2,0:T(8,128)(2,1)}), bf16[16,128,180]{1,2,0:T(8,128)(2,1)S(1)}, u32[]{:S(2)}, u32[]{:S(2)}) async-start(bf16[16,128,180]{1,2,0:T(8,128)(2,1)} %bitcast.13), calls=%async_computation | async-start | bytes 1507328 | tf_op jit(solution)/shard_map/all_to_all | solution.py:151
  89.8 136.5 %all-gather.8.cloned.1.call-start = ((), (), s32[]{:S(2)}) async-start(), calls=%async_computation.6 | async-start | bytes 2119680 | tf_op jit(solution)/shard_map/all_gather | solution.py:192
  125.5 0.6 copy-start.2
  164.4 90.8 %all-gather.12.cloned.1.call-start = ((), (), s32[]{:S(2)}) async-start(), calls=%async_computation.8 | async-start | bytes 5591040 | tf_op jit(solution)/shard_map/all_gather | solution.py:193
  255.2 3.1 copy-start.1
  308.4 65.9 %copy-start.5 = (f32[128,4]{0,1:T(4,128)S(1)}, f32[128,4]{0,1:T(4,128)}, u32[]{:S(2)}) copy-start(f32[128,4]{0,1:T(4,128)} %param.21) | copy-start | bytes 6148
  361.6 38.9 %copy-start.3 = (f32[128,180]{0,1:T(8,128)S(1)}, f32[128,180]{0,1:T(8,128)}, u32[]{:S(2)}) copy-start(f32[128,180]{0,1:T(8,128)} %copy-done.2) | copy-start | bytes 276484
  362.6 35.1 %all-to-all-start.5 = ((bf16[32,20,180]{2,1,0:T(8,128)(2,1)}), bf16[32,20,180]{2,1,0:T(8,128)(2,1)S(1)}, u32[]{:S(2)}, u32[]{:S(2)}) async-start(bf16[32,20,180]{2,1,0:T(8,128)(2,1)} %reshape.378), calls=%async_computation.5 | async-start | bytes 786432 | tf_op jit(solution)/shard_map/all_to_all | solution.py:224
Sparse Core Ops, SparseCore 0:
  37.8 34.6 all-gather.9
  164.5 61.6 all-gather.7
  229.4 25.7 all-gather.11

commit v5 on v4

--- a/solution.py
+++ b/solution.py
@@ -111,18 +111,15 @@
     key_value = jnp.concatenate([key_rot, value_block], axis=1)
     score_scale = 1.0 / math.sqrt(HEAD_SIZE)
     block_part = lax.all_gather(key_value, "zh", axis=0, tiled=False)
-    block_part = lax.all_gather(block_part, "y", axis=0, tiled=False)
-    block_part = lax.all_gather(block_part, "x", axis=0, tiled=False)
-    zh_count = block_part.shape[2]
-    y_count = block_part.shape[1]
-    x_count = block_part.shape[0]
+    block_part = lax.all_gather(block_part, ("y", "x"), axis=0, tiled=False)
+    zh_count = block_part.shape[1]
+    plane_count = block_part.shape[0]
     block_of_key = (
-        lax.broadcasted_iota(jnp.int32, (x_count, y_count, zh_count), 2) * (y_count * x_count)
-        + lax.broadcasted_iota(jnp.int32, (x_count, y_count, zh_count), 1) * x_count
-        + lax.broadcasted_iota(jnp.int32, (x_count, y_count, zh_count), 0)
+        lax.broadcasted_iota(jnp.int32, (plane_count, zh_count), 1) * plane_count
+        + lax.broadcasted_iota(jnp.int32, (plane_count, zh_count), 0)
     )
     key_pos = (
-        block_of_key[:, :, :, None] * tok_rows + jnp.arange(tok_rows, dtype=jnp.int32)
+        block_of_key[:, :, None] * tok_rows + jnp.arange(tok_rows, dtype=jnp.int32)
     ).reshape(-1)
     block_part = block_part.reshape(-1, 2 * HEAD_SIZE)
     run_max = jnp.broadcast_to(sink_logits[:, None], (local_heads, tok_rows))
@@ -147,8 +144,10 @@
         .astype(jnp.bfloat16)
     )
     head_part = jnp.dot(attended, out_proj, preferred_element_type=jnp.float32).astype(jnp.bfloat16)
-    head_part = head_part.reshape(tok_rows, exp_count, col_width).transpose(1, 0, 2)
-    head_part = lax.all_to_all(head_part, EXP, split_axis=0, concat_axis=0, tiled=True)
+    head_part = head_part.reshape(tok_rows, zl_count, c_count, col_width).transpose(2, 1, 0, 3)
+    head_part = lax.all_to_all(head_part, "c", split_axis=0, concat_axis=0, tiled=True)
+    head_part = jnp.sum(head_part.astype(jnp.float32), axis=0).astype(jnp.bfloat16)
+    head_part = lax.all_to_all(head_part, ZL, split_axis=0, concat_axis=0, tiled=True)
     head_cols = jnp.sum(head_part.astype(jnp.float32), axis=0)
     residual_cols = lax.dynamic_slice_in_dim(
         hidden_in, exp_index * col_width, col_width, 1

time: 409 us -> 410 us (level)
  waiting for transfers between devices: 156 us -> 171 us
  blocking collectives: 147 us -> 133 us
    all_gather x1, waiting for transfers between devices: 31.1 us -> 56.7 us  [per_device(): block_part = lax.all_gather(block_part, ('y', 'x'), axis=0, tiled=False)]
    all_to_all x1, waiting for transfers between devices: 32.5 us -> 16.6 us  [per_device(): lax.all_to_all(head_part, ZL, split_axis=0, concat_axis=0, tiled=True)]
    all_gather x1 -> x0, blocking collectives: 13.1 us -> none  [per_device(): block_part = lax.all_gather(block_part, 'y', axis=0, tiled=False)]
    all_to_all x1, blocking collectives: 33.4 us -> 27.5 us  [per_device(): lax.all_to_all(send_rows.reshape(ctx_count, exp_local * capacity, send_wi...]
    all_gather x1, waiting for transfers between devices: 61.6 us -> 66.5 us  [per_device(): gathered = lax.all_gather(received, ZL, axis=0, tiled=False)]
    all_to_all x0 -> x1, blocking collectives: none -> 4.3 us  [per_device(): lax.all_to_all(head_part, 'c', split_axis=0, concat_axis=0, tiled=True)]
where the time goes in v5:
time: 410 us; the launch traced here: 409 us
  waiting for transfers between devices  171 us (42%)
  blocking collectives  133 us (32%)
  local copies, waits for them, and re-layouts  42.3 us (10%)
  starting transfers between devices  22 us (5%)
  other arithmetic  16.1 us (4%)
  between operations  13.6 us (3%)
  matrix products  10.9 us (3%)
    all_gather x1, waiting for transfers between devices, per_device(): gathered = lax.all_gather(received, ZL, axis=0, tiled=False)  66.5 us
    all_gather x1, waiting for transfers between devices, per_device(): block_part = lax.all_gather(block_part, ('y', 'x'), axis=0, tiled=False)  56.7 us
    all_to_all x1, blocking collectives, per_device(): partial_value = lax.all_to_all(partial_value, 'zlh', 0, 0, tiled=True)  52.8 us
    all_to_all x1, blocking collectives, per_device(): lax.all_to_all(send_rows.reshape(ctx_count, exp_local * capacity, send_wi...  27.5 us
    all_to_all x1, blocking collectives, per_device(): lax.all_to_all(partial_value.transpose(1, 0, 2, 3), 'zll', 0, 0, tiled=True)  25.3 us
    all_to_all x1, waiting for transfers between devices, per_device(): lax.all_to_all(expert_cols.reshape(ctx_count, capacity, col_width), CTX,...  23.3 us
    all_to_all x1, waiting for transfers between devices, per_device(): lax.all_to_all(head_part, ZL, split_axis=0, concat_axis=0, tiled=True)  16.6 us
    all_gather x1, blocking collectives, per_device(): block_part = lax.all_gather(key_value, 'zh', axis=0, tiled=False)  15 us
  transfers between devices with their start and end apart: 5, of which 5 were waited for; matrix products, arithmetic and copies ran while one was open for 6% of the time, Pallas kernels for 0%

profile of v5, /device:TPU:64, one launch (start us, length us, event | category | flops | bytes accessed | tf_op | source)
XLA Modules:
  0.0 408.7 jit_solution(1020845502821032745)
XLA Ops:
  8.5 15.0 %all-gather = bf16[256,128]{0,1:T(8,128)(2,1)S(1)} all-gather(bf16[128,128]{0,1:T(8,128)(2,1)S(1)} %pad_maximum_fusion.1), channel_id=2, replica_groups=mesh['zh'=2,'y'=4,'x'=4,'zlh'=4,'zll'=2,'c'=2] {'zh'}, dimensions={0}, use_global_device_ids=true | all-gather | bytes 98304 | tf_op jit(solution)/shard_map/all_gather | solution.py:113
  28.0 56.7 %all-gather.9.cloned.1.call-done = bf16[32,128,128]{2,1,0:T(8,128)(2,1)} async-done(((bf16[2,128,128]{2,1,0:T(8,128)(2,1)}), bf16[32,128,128]{2,1,0:T(8,128)(2,1)}) %all-gather.9.cloned.1.call-update) | async-done | bytes 1048592 | tf_op jit(solution)/shard_map/all_gather | solution.py:114
  84.7 2.1 fusion.56
  88.0 2.5 fusion.21
  91.2 4.3 %all_to_all.35 = bf16[2,8,128,180]{2,1,3,0:T(8,128)(2,1)S(1)} all-to-all(bf16[2,8,128,180]{2,1,3,0:T(8,128)(2,1)S(1)} %copy.87), channel_id=1, replica_groups=mesh['zh'=2,'y'=4,'x'=4,'zlh'=4,'zll'=2,'c'=2] {'c'}, dimensions={0} | all-to-all | bytes 1474560 | tf_op jit(solution)/shard_map/all_to_all | solution.py:148
  96.6 10.4 %all-to-all-start.1 = ((bf16[8,128,180]{1,2,0:T(8,128)(2,1)}), bf16[8,128,180]{1,2,0:T(8,128)(2,1)S(1)}, u32[]{:S(2)}, u32[]{:S(2)}) async-start(bf16[8,128,180]{1,2,0:T(8,128)(2,1)} %copy.114), calls=%async_computation.1 | async-start | bytes 753664 | tf_op jit(solution)/shard_map/all_to_all | solution.py:150
  110.1 16.6 %all-to-all-done.1 = bf16[8,128,180]{1,2,0:T(8,128)(2,1)S(1)} async-done(((bf16[8,128,180]{1,2,0:T(8,128)(2,1)}), bf16[8,128,180]{1,2,0:T(8,128)(2,1)S(1)}, u32[]{:S(2)}, u32[]{:S(2)}) %all-to-all-start.1) | async-done | bytes 368672 | tf_op jit(solution)/shard_map/all_to_all | solution.py:150
  128.7 2.4 scatter_custom_fusion
  131.2 27.5 %all_to_all.36 = bf16[32,20,182]{2,1,0:T(8,128)(2,1)S(1)} all-to-all(bf16[32,20,182]{2,1,0:T(8,128)(2,1)S(1)} %reshape.382), channel_id=1, replica_groups=mesh['zh'=2,'y'=4,'x'=4,'zlh'=4,'zll'=2,'c'=2] {'zh','y','x'}, dimensions={0} | all-to-all | bytes 465920 | tf_op jit(solution)/shard_map/all_to_all | solution.py:184
  160.0 66.5 %all-gather.7.cloned.1.call-done = bf16[8,640,182]{1,2,0:T(8,128)(2,1)} async-done(((bf16[1,640,182]{1,2,0:T(8,128)(2,1)}), bf16[8,640,182]{1,2,0:T(8,128)(2,1)}) %all-gather.7.cloned.1.call-update) | async-done | bytes 1863696 | tf_op jit(solution)/shard_map/all_gather | solution.py:191
  226.5 3.0 copy.97
  231.3 9.7 %reshape.383 = bf16[8,2,180,360]{2,1,0,3:T(2,128)(2,1)} reshape(bf16[1,2880,2,180]{1,3,2,0:T(8,128)(2,1)S(1)} %copy.99) | data formatting | bytes 4147200 | tf_op jit(solution)/shard_map/reshape | solution.py:199
  241.1 6.4 %reshape.385 = bf16[180,4,2,2,180]{4,3,2,1,0:T(2,128)(2,1)S(1)} reshape(bf16[1,180,2880]{2,1,0:T(8,128)(2,1)} %param.23) | data formatting | bytes 2073600 | tf_op jit(solution)/shard_map/reshape | solution.py:213
  247.5 7.9 %all-gather.11.cloned.1.call-done = bf16[16,640,182]{1,0,2:T(8,128)(2,1)} async-done(((bf16[8,640,182]{1,0,2:T(8,128)(2,1)}), bf16[16,640,182]{1,0,2:T(8,128)(2,1)}) %all-gather.11.cloned.1.call-update) | async-done | bytes 3727376 | tf_op jit(solution)/shard_map/all_gather | solution.py:192
  255.4 3.0 copy.98
  258.5 4.1 %fusion.14 = f32[640,360]{0,1:T(8,128)} fusion(bf16[8,2,180,360]{2,1,0,3:T(2,128)(2,1)S(1)} %copy-done.1, bf16[2,8,640,182]{2,3,1,0:T(8,128)(2,1)S(1)} %bitcast.89, f32[640]{0:T(1024)S(1)} %add_rsqrt_fusion), kind=kOutput, calls=%fused_computation.17 | convolution fusion | flops 1327334400 | bytes 6725120 | tf_op jit(solution)/shard_map/czrk,zckf->rf/dot_general | solution.py:200
  267.7 7.7 %all_to_all.37 = bf16[2,4,2,640,180]{3,1,4,2,0:T(4,128)(2,1)} all-to-all(bf16[2,4,2,640,180]{3,1,4,2,0:T(4,128)(2,1)S(1)} %copy.102), channel_id=1, replica_groups=mesh['zh'=2,'y'=4,'x'=4,'zlh'=4,'zll'=2,'c'=2] {'c'}, dimensions={0} | all-to-all | bytes 7372800 | tf_op jit(solution)/shard_map/all_to_all | solution.py:217
  275.4 5.0 %reduce_sum.111 = bf16[4,2,640,180]{2,0,3,1:T(4,128)(2,1)S(1)} reduce(bf16[2,4,2,640,180]{3,1,4,2,0:T(4,128)(2,1)} %all_to_all.37, bf16[]{:T(256)} %constant.89.clone.1), dimensions={0}, to_apply=%region_10.11 | reduce | flops 921600 | bytes 5529602 | tf_op jit(solution)/shard_map/reduce_sum | solution.py:218
  281.4 25.3 %all_to_all.38 = bf16[2,4,640,180]{2,1,3,0:T(4,128)(2,1)S(1)} all-to-all(bf16[2,4,640,180]{2,1,3,0:T(4,128)(2,1)S(1)} %copy.104), channel_id=1, replica_groups=mesh['zh'=2,'y'=4,'x'=4,'zlh'=4,'zll'=2,'c'=2] {'zll'}, dimensions={0} | all-to-all | bytes 3686400 | tf_op jit(solution)/shard_map/all_to_all | solution.py:219
  306.7 2.0 reduce_sum.112
  308.8 52.8 %all_to_all.39 = bf16[4,640,180]{1,2,0:T(8,128)(2,1)S(1)} all-to-all(bf16[4,640,180]{1,2,0:T(8,128)(2,1)S(1)} %copy.105), channel_id=1, replica_groups=mesh['zh'=2,'y'=4,'x'=4,'zlh'=4,'zll'=2,'c'=2] {'zlh'}, dimensions={0} | all-to-all | bytes 1843200 | tf_op jit(solution)/shard_map/all_to_all | solution.py:221
  362.8 11.5 %all-to-all-start.6 = ((bf16[32,20,180]{2,1,0:T(8,128)(2,1)}), bf16[32,20,180]{2,1,0:T(8,128)(2,1)S(1)}, u32[]{:S(2)}, u32[]{:S(2)}) async-start(bf16[32,20,180]{2,1,0:T(8,128)(2,1)} %reshape.386), calls=%async_computation.6 | async-start | bytes 786432 | tf_op jit(solution)/shard_map/all_to_all | solution.py:223
  374.7 23.3 %all-to-all-done.6 = bf16[32,20,180]{2,1,0:T(8,128)(2,1)S(1)} async-done(((bf16[32,20,180]{2,1,0:T(8,128)(2,1)}), bf16[32,20,180]{2,1,0:T(8,128)(2,1)S(1)}, u32[]{:S(2)}, u32[]{:S(2)}) %all-to-all-start.6) | async-done | bytes 230432 | tf_op jit(solution)/shard_map/all_to_all | solution.py:223
  398.1 2.0 gather_fusion
  (95 shorter events, 27.4 us)
Async XLA Ops:
  6.5 84.0 %copy-start = (bf16[128,2880]{0,1:T(8,128)(2,1)S(1)}, bf16[128,2880]{0,1:T(8,128)(2,1)}, u32[]{:S(2)}) copy-start(bf16[128,2880]{0,1:T(8,128)(2,1)} %param.18) | copy-start | bytes 2211844
  6.5 78.1 %all-gather.9.cloned.1.call-start = ((), (), s32[]{:S(2)}) async-start(), calls=%async_computation.8 | async-start | bytes 1114112 | tf_op jit(solution)/shard_map/all_gather | solution.py:114
  28.0 58.7 %copy-start.7 = (f32[2]{0:T(128)S(1)}, f32[2]{0:T(128)}, u32[]{:S(2)}) copy-start(f32[2]{0:T(128)} %param.17) | copy-start | bytes 28
  86.7 1.2 copy-start.2
  90.9 16.1 %copy-start.5 = (s32[128,4]{0,1:T(4,128)S(1)}, s32[128,4]{0,1:T(4,128)}, u32[]{:S(2)}) copy-start(s32[128,4]{0,1:T(4,128)} %param.20) | copy-start | bytes 6148
  96.6 30.1 %all-to-all-start.1 = ((bf16[8,128,180]{1,2,0:T(8,128)(2,1)}), bf16[8,128,180]{1,2,0:T(8,128)(2,1)S(1)}, u32[]{:S(2)}, u32[]{:S(2)}) async-start(bf16[8,128,180]{1,2,0:T(8,128)(2,1)} %copy.114), calls=%async_computation.1 | async-start | bytes 753664 | tf_op jit(solution)/shard_map/all_to_all | solution.py:150
  107.0 119.5 %all-gather.7.cloned.1.call-start = ((), (), s32[]{:S(2)}) async-start(), calls=%async_computation.7 | async-start | bytes 2119680 | tf_op jit(solution)/shard_map/all_gather | solution.py:191
  126.8 0.6 copy-start.3
  159.7 95.7 %all-gather.11.cloned.1.call-start = ((), (), s32[]{:S(2)}) async-start(), calls=%async_computation.9 | async-start | bytes 5591040 | tf_op jit(solution)/shard_map/all_gather | solution.py:192
  255.4 3.1 copy-start.1
  308.7 65.9 %copy-start.6 = (f32[128,4]{0,1:T(4,128)S(1)}, f32[128,4]{0,1:T(4,128)}, u32[]{:S(2)}) copy-start(f32[128,4]{0,1:T(4,128)} %param.21) | copy-start | bytes 6148
  361.8 38.9 %copy-start.4 = (f32[128,180]{0,1:T(8,128)S(1)}, f32[128,180]{0,1:T(8,128)}, u32[]{:S(2)}) copy-start(f32[128,180]{0,1:T(8,128)} %copy-done.3) | copy-start | bytes 276484
  362.8 35.1 %all-to-all-start.6 = ((bf16[32,20,180]{2,1,0:T(8,128)(2,1)}), bf16[32,20,180]{2,1,0:T(8,128)(2,1)S(1)}, u32[]{:S(2)}, u32[]{:S(2)}) async-start(bf16[32,20,180]{2,1,0:T(8,128)(2,1)} %reshape.386), calls=%async_computation.6 | async-start | bytes 786432 | tf_op jit(solution)/shard_map/all_to_all | solution.py:223
Sparse Core Ops, SparseCore 0:
  24.4 60.1 all-gather.8
  159.9 66.5 all-gather.6
  229.6 25.7 all-gather.10

commit v6 on v4

--- a/solution.py
+++ b/solution.py
@@ -147,8 +147,10 @@
         .astype(jnp.bfloat16)
     )
     head_part = jnp.dot(attended, out_proj, preferred_element_type=jnp.float32).astype(jnp.bfloat16)
-    head_part = head_part.reshape(tok_rows, exp_count, col_width).transpose(1, 0, 2)
-    head_part = lax.all_to_all(head_part, EXP, split_axis=0, concat_axis=0, tiled=True)
+    head_part = head_part.reshape(tok_rows, zl_count, c_count, col_width).transpose(2, 1, 0, 3)
+    head_part = lax.all_to_all(head_part, "c", split_axis=0, concat_axis=0, tiled=True)
+    head_part = jnp.sum(head_part.astype(jnp.float32), axis=0).astype(jnp.bfloat16)
+    head_part = lax.all_to_all(head_part, ZL, split_axis=0, concat_axis=0, tiled=True)
     head_cols = jnp.sum(head_part.astype(jnp.float32), axis=0)
     residual_cols = lax.dynamic_slice_in_dim(
         hidden_in, exp_index * col_width, col_width, 1

time: 409 us -> 399 us (0.976)
  waiting for transfers between devices: 156 us -> 145 us
    all_to_all x1, waiting for transfers between devices: 32.5 us -> 16.6 us  [per_device(): lax.all_to_all(head_part, ZL, split_axis=0, concat_axis=0, tiled=True)]
    all_gather x1, waiting for transfers between devices: 61.6 us -> 66.5 us  [per_device(): gathered = lax.all_gather(received, ZL, axis=0, tiled=False)]
    all_to_all x0 -> x1, blocking collectives: none -> 4.3 us  [per_device(): lax.all_to_all(head_part, 'c', split_axis=0, concat_axis=0, tiled=True)]
    all_to_all x1, blocking collectives: 33.4 us -> 29.2 us  [per_device(): lax.all_to_all(send_rows.reshape(ctx_count, exp_local * capacity, send_wi...]
where the time goes in v6:
time: 399 us; the launch traced here: 398 us
  blocking collectives  148 us (37%)
  waiting for transfers between devices  145 us (36%)
  local copies, waits for them, and re-layouts  43.9 us (11%)
  starting transfers between devices  22 us (6%)
  other arithmetic  16.2 us (4%)
  between operations  13.6 us (3%)
  matrix products  9.24 us (2%)
    all_gather x1, waiting for transfers between devices, per_device(): gathered = lax.all_gather(received, ZL, axis=0, tiled=False)  66.5 us
    all_to_all x1, blocking collectives, per_device(): partial_value = lax.all_to_all(partial_value, 'zlh', 0, 0, tiled=True)  52.8 us
    all_gather x1, waiting for transfers between devices, per_device(): block_part = lax.all_gather(block_part, 'x', axis=0, tiled=False)  31.1 us
    all_to_all x1, blocking collectives, per_device(): lax.all_to_all(send_rows.reshape(ctx_count, exp_local * capacity, send_wi...  29.2 us
    all_to_all x1, blocking collectives, per_device(): lax.all_to_all(partial_value.transpose(1, 0, 2, 3), 'zll', 0, 0, tiled=True)  25.3 us
    all_to_all x1, waiting for transfers between devices, per_device(): lax.all_to_all(expert_cols.reshape(ctx_count, capacity, col_width), CTX,...  23.3 us
    all_to_all x1, waiting for transfers between devices, per_device(): lax.all_to_all(head_part, ZL, split_axis=0, concat_axis=0, tiled=True)  16.6 us
    all_gather x1, blocking collectives, per_device(): block_part = lax.all_gather(key_value, 'zh', axis=0, tiled=False)  15 us
  transfers between devices with their start and end apart: 5, of which 5 were waited for; matrix products, arithmetic and copies ran while one was open for 6% of the time, Pallas kernels for 0%

profile of v6, /device:TPU:64, one launch (start us, length us, event | category | flops | bytes accessed | tf_op | source)
XLA Modules:
  0.0 398.0 jit_solution(8022348854454238381)
XLA Ops:
  8.5 15.0 %all-gather = bf16[256,128]{0,1:T(8,128)(2,1)S(1)} all-gather(bf16[128,128]{0,1:T(8,128)(2,1)S(1)} %pad_maximum_fusion.1), channel_id=2, replica_groups=mesh['zh'=2,'y'=4,'x'=4,'zlh'=4,'zll'=2,'c'=2] {'zh'}, dimensions={0}, use_global_device_ids=true | all-gather | bytes 98304 | tf_op jit(solution)/shard_map/all_gather | solution.py:113
  23.7 13.1 %all-gather.1 = bf16[8,128,128]{2,1,0:T(8,128)(2,1)S(1)} all-gather(bf16[2,128,128]{2,1,0:T(8,128)(2,1)S(1)} %bitcast.92), channel_id=3, replica_groups=mesh['zh'=2,'y'=4,'x'=4,'zlh'=4,'zll'=2,'c'=2] {'y'}, dimensions={0}, use_global_device_ids=true | all-gather | bytes 327680 | tf_op jit(solution)/shard_map/all_gather | solution.py:114
  41.5 31.1 %all-gather.10.cloned.1.call-done = bf16[16,2,128,128]{2,1,0,3:T(2,128)(2,1)} async-done(((bf16[4,2,128,128]{2,1,0,3:T(2,128)(2,1)}), bf16[16,2,128,128]{2,1,0,3:T(2,128)(2,1)}) %all-gather.10.cloned.1.call-update) | async-done | bytes 1048592 | tf_op jit(solution)/shard_map/all_gather | solution.py:115
  76.0 2.1 fusion.21
  78.8 4.3 %all_to_all.35 = bf16[2,8,128,180]{2,1,3,0:T(8,128)(2,1)S(1)} all-to-all(bf16[2,8,128,180]{2,1,3,0:T(8,128)(2,1)S(1)} %copy.87), channel_id=1, replica_groups=mesh['zh'=2,'y'=4,'x'=4,'zlh'=4,'zll'=2,'c'=2] {'c'}, dimensions={0} | all-to-all | bytes 1474560 | tf_op jit(solution)/shard_map/all_to_all | solution.py:151
  84.2 10.4 %all-to-all-start.1 = ((bf16[8,128,180]{1,2,0:T(8,128)(2,1)}), bf16[8,128,180]{1,2,0:T(8,128)(2,1)S(1)}, u32[]{:S(2)}, u32[]{:S(2)}) async-start(bf16[8,128,180]{1,2,0:T(8,128)(2,1)} %copy.113), calls=%async_computation.1 | async-start | bytes 753664 | tf_op jit(solution)/shard_map/all_to_all | solution.py:153
  97.7 16.6 %all-to-all-done.1 = bf16[8,128,180]{1,2,0:T(8,128)(2,1)S(1)} async-done(((bf16[8,128,180]{1,2,0:T(8,128)(2,1)}), bf16[8,128,180]{1,2,0:T(8,128)(2,1)S(1)}, u32[]{:S(2)}, u32[]{:S(2)}) %all-to-all-start.1) | async-done | bytes 368672 | tf_op jit(solution)/shard_map/all_to_all | solution.py:153
  116.3 2.4 scatter_custom_fusion
  118.8 29.2 %all_to_all.36 = bf16[32,20,182]{2,1,0:T(8,128)(2,1)S(1)} all-to-all(bf16[32,20,182]{2,1,0:T(8,128)(2,1)S(1)} %reshape.374), channel_id=1, replica_groups=mesh['zh'=2,'y'=4,'x'=4,'zlh'=4,'zll'=2,'c'=2] {'zh','y','x'}, dimensions={0} | all-to-all | bytes 465920 | tf_op jit(solution)/shard_map/all_to_all | solution.py:187
  149.2 66.5 %all-gather.8.cloned.1.call-done = bf16[8,640,182]{1,2,0:T(8,128)(2,1)} async-done(((bf16[1,640,182]{1,2,0:T(8,128)(2,1)}), bf16[8,640,182]{1,2,0:T(8,128)(2,1)}) %all-gather.8.cloned.1.call-update) | async-done | bytes 1863696 | tf_op jit(solution)/shard_map/all_gather | solution.py:194
  215.8 3.0 copy.97
  220.6 9.7 %reshape.375 = bf16[8,2,180,360]{2,1,0,3:T(2,128)(2,1)} reshape(bf16[1,2880,2,180]{1,3,2,0:T(8,128)(2,1)S(1)} %copy.99) | data formatting | bytes 4147200 | tf_op jit(solution)/shard_map/reshape | solution.py:202
  230.4 6.4 %reshape.377 = bf16[180,4,2,2,180]{4,3,2,1,0:T(2,128)(2,1)S(1)} reshape(bf16[1,180,2880]{2,1,0:T(8,128)(2,1)} %param.23) | data formatting | bytes 2073600 | tf_op jit(solution)/shard_map/reshape | solution.py:216
  236.8 7.9 %all-gather.12.cloned.1.call-done = bf16[16,640,182]{1,0,2:T(8,128)(2,1)} async-done(((bf16[8,640,182]{1,0,2:T(8,128)(2,1)}), bf16[16,640,182]{1,0,2:T(8,128)(2,1)}) %all-gather.12.cloned.1.call-update) | async-done | bytes 3727376 | tf_op jit(solution)/shard_map/all_gather | solution.py:195
  244.7 3.0 copy.98
  247.8 4.1 %fusion.14 = f32[640,360]{0,1:T(8,128)} fusion(bf16[8,2,180,360]{2,1,0,3:T(2,128)(2,1)S(1)} %copy-done.1, bf16[2,8,640,182]{2,3,1,0:T(8,128)(2,1)S(1)} %bitcast.89, f32[640]{0:T(1024)S(1)} %add_rsqrt_fusion), kind=kOutput, calls=%fused_computation.17 | convolution fusion | flops 1327334400 | bytes 6725120 | tf_op jit(solution)/shard_map/czrk,zckf->rf/dot_general | solution.py:203
  256.9 7.7 %all_to_all.37 = bf16[2,4,2,640,180]{3,1,4,2,0:T(4,128)(2,1)} all-to-all(bf16[2,4,2,640,180]{3,1,4,2,0:T(4,128)(2,1)S(1)} %copy.102), channel_id=1, replica_groups=mesh['zh'=2,'y'=4,'x'=4,'zlh'=4,'zll'=2,'c'=2] {'c'}, dimensions={0} | all-to-all | bytes 7372800 | tf_op jit(solution)/shard_map/all_to_all | solution.py:220
  264.7 5.0 %reduce_sum.111 = bf16[4,2,640,180]{2,0,3,1:T(4,128)(2,1)S(1)} reduce(bf16[2,4,2,640,180]{3,1,4,2,0:T(4,128)(2,1)} %all_to_all.37, bf16[]{:T(256)} %constant.90.clone.1), dimensions={0}, to_apply=%region_10.11 | reduce | flops 921600 | bytes 5529602 | tf_op jit(solution)/shard_map/reduce_sum | solution.py:221
  270.7 25.3 %all_to_all.38 = bf16[2,4,640,180]{2,1,3,0:T(4,128)(2,1)S(1)} all-to-all(bf16[2,4,640,180]{2,1,3,0:T(4,128)(2,1)S(1)} %copy.104), channel_id=1, replica_groups=mesh['zh'=2,'y'=4,'x'=4,'zlh'=4,'zll'=2,'c'=2] {'zll'}, dimensions={0} | all-to-all | bytes 3686400 | tf_op jit(solution)/shard_map/all_to_all | solution.py:222
  296.0 2.0 reduce_sum.112
  298.1 52.8 %all_to_all.39 = bf16[4,640,180]{1,2,0:T(8,128)(2,1)S(1)} all-to-all(bf16[4,640,180]{1,2,0:T(8,128)(2,1)S(1)} %copy.105), channel_id=1, replica_groups=mesh['zh'=2,'y'=4,'x'=4,'zlh'=4,'zll'=2,'c'=2] {'zlh'}, dimensions={0} | all-to-all | bytes 1843200 | tf_op jit(solution)/shard_map/all_to_all | solution.py:224
  352.1 11.5 %all-to-all-start.6 = ((bf16[32,20,180]{2,1,0:T(8,128)(2,1)}), bf16[32,20,180]{2,1,0:T(8,128)(2,1)S(1)}, u32[]{:S(2)}, u32[]{:S(2)}) async-start(bf16[32,20,180]{2,1,0:T(8,128)(2,1)} %reshape.378), calls=%async_computation.6 | async-start | bytes 786432 | tf_op jit(solution)/shard_map/all_to_all | solution.py:226
  363.9 23.3 %all-to-all-done.6 = bf16[32,20,180]{2,1,0:T(8,128)(2,1)S(1)} async-done(((bf16[32,20,180]{2,1,0:T(8,128)(2,1)}), bf16[32,20,180]{2,1,0:T(8,128)(2,1)S(1)}, u32[]{:S(2)}, u32[]{:S(2)}) %all-to-all-start.6) | async-done | bytes 230432 | tf_op jit(solution)/shard_map/all_to_all | solution.py:226
  387.4 2.0 gather_fusion
  (97 shorter events, 29.9 us)
Async XLA Ops:
  6.5 71.5 %copy-start = (bf16[128,2880]{0,1:T(8,128)(2,1)S(1)}, bf16[128,2880]{0,1:T(8,128)(2,1)}, u32[]{:S(2)}) copy-start(bf16[128,2880]{0,1:T(8,128)(2,1)} %param.18) | copy-start | bytes 2211844
  6.5 66.0 %all-gather.10.cloned.1.call-start = ((), (), s32[]{:S(2)}) async-start(), calls=%async_computation.8 | async-start | bytes 1310720 | tf_op jit(solution)/shard_map/all_gather | solution.py:115
  41.5 33.8 %copy-start.6 = (f32[2]{0:T(128)S(1)}, f32[2]{0:T(128)}, u32[]{:S(2)}) copy-start(f32[2]{0:T(128)} %param.17) | copy-start | bytes 28
  78.4 16.1 %copy-start.4 = (s32[128,4]{0,1:T(4,128)S(1)}, s32[128,4]{0,1:T(4,128)}, u32[]{:S(2)}) copy-start(s32[128,4]{0,1:T(4,128)} %param.20) | copy-start | bytes 6148
  84.2 30.1 %all-to-all-start.1 = ((bf16[8,128,180]{1,2,0:T(8,128)(2,1)}), bf16[8,128,180]{1,2,0:T(8,128)(2,1)S(1)}, u32[]{:S(2)}, u32[]{:S(2)}) async-start(bf16[8,128,180]{1,2,0:T(8,128)(2,1)} %copy.113), calls=%async_computation.1 | async-start | bytes 753664 | tf_op jit(solution)/shard_map/all_to_all | solution.py:153
  94.6 121.2 %all-gather.8.cloned.1.call-start = ((), (), s32[]{:S(2)}) async-start(), calls=%async_computation.7 | async-start | bytes 2119680 | tf_op jit(solution)/shard_map/all_gather | solution.py:194
  114.3 0.6 copy-start.2
  149.0 95.7 %all-gather.12.cloned.1.call-start = ((), (), s32[]{:S(2)}) async-start(), calls=%async_computation.9 | async-start | bytes 5591040 | tf_op jit(solution)/shard_map/all_gather | solution.py:195
  244.7 3.1 copy-start.1
  298.0 65.9 %copy-start.5 = (f32[128,4]{0,1:T(4,128)S(1)}, f32[128,4]{0,1:T(4,128)}, u32[]{:S(2)}) copy-start(f32[128,4]{0,1:T(4,128)} %param.21) | copy-start | bytes 6148
  351.1 38.9 %copy-start.3 = (f32[128,180]{0,1:T(8,128)S(1)}, f32[128,180]{0,1:T(8,128)}, u32[]{:S(2)}) copy-start(f32[128,180]{0,1:T(8,128)} %copy-done.2) | copy-start | bytes 276484
  352.1 35.1 %all-to-all-start.6 = ((bf16[32,20,180]{2,1,0:T(8,128)(2,1)}), bf16[32,20,180]{2,1,0:T(8,128)(2,1)S(1)}, u32[]{:S(2)}, u32[]{:S(2)}) async-start(bf16[32,20,180]{2,1,0:T(8,128)(2,1)} %reshape.378), calls=%async_computation.6 | async-start | bytes 786432 | tf_op jit(solution)/shard_map/all_to_all | solution.py:226
Sparse Core Ops, SparseCore 0:
  37.8 34.6 all-gather.9
  149.1 66.5 all-gather.7
  218.9 25.7 all-gather.11

commit v7 on v6

--- a/solution.py
+++ b/solution.py
@@ -112,7 +112,13 @@
     score_scale = 1.0 / math.sqrt(HEAD_SIZE)
     block_part = lax.all_gather(key_value, "zh", axis=0, tiled=False)
     block_part = lax.all_gather(block_part, "y", axis=0, tiled=False)
-    block_part = lax.all_gather(block_part, "x", axis=0, tiled=False)
+    block_part = lax.all_to_all(
+        jnp.broadcast_to(block_part[None], (lax.axis_size("x"),) + block_part.shape),
+        "x",
+        0,
+        0,
+        tiled=True,
+    )
     zh_count = block_part.shape[2]
     y_count = block_part.shape[1]
     x_count = block_part.shape[0]

time: 399 us -> 380 us (0.952)
  waiting for transfers between devices: 145 us -> 123 us
  starting transfers between devices: 22 us -> 27.1 us
    all_gather x1 -> x0, waiting for transfers between devices: 31.1 us -> none  [per_device(): block_part = lax.all_gather(block_part, 'x', axis=0, tiled=False)]
    all_to_all x0 -> x1, waiting for transfers between devices: none -> 8.52 us  [per_device(): lax.all_to_all(jnp.broadcast_to(block_part[None], (lax.axis_size('x'),) +...]
    all_to_all x0 -> x1, starting transfers between devices: none -> 4.29 us  [per_device(): lax.all_to_all(jnp.broadcast_to(block_part[None], (lax.axis_size('x'),) +...]
where the time goes in v7:
time: 380 us; the launch traced here: 379 us
  blocking collectives  146 us (38%)
  waiting for transfers between devices  123 us (32%)
  local copies, waits for them, and re-layouts  43.7 us (12%)
  starting transfers between devices  27.1 us (7%)
  other arithmetic  15.6 us (4%)
  between operations  13.9 us (4%)
  matrix products  9.23 us (2%)
    all_gather x1, waiting for transfers between devices, per_device(): gathered = lax.all_gather(received, ZL, axis=0, tiled=False)  66.4 us
    all_to_all x1, blocking collectives, per_device(): partial_value = lax.all_to_all(partial_value, 'zlh', 0, 0, tiled=True)  52.8 us
    all_to_all x1, blocking collectives, per_device(): lax.all_to_all(send_rows.reshape(ctx_count, exp_local * capacity, send_wi...  28 us
    all_to_all x1, blocking collectives, per_device(): lax.all_to_all(partial_value.transpose(1, 0, 2, 3), 'zll', 0, 0, tiled=True)  25.3 us
    all_to_all x1, waiting for transfers between devices, per_device(): lax.all_to_all(expert_cols.reshape(ctx_count, capacity, col_width), CTX,...  23.3 us
    all_to_all x1, waiting for transfers between devices, per_device(): lax.all_to_all(head_part, ZL, split_axis=0, concat_axis=0, tiled=True)  16.6 us
    all_gather x1, blocking collectives, per_device(): block_part = lax.all_gather(key_value, 'zh', axis=0, tiled=False)  15 us
    all_gather x1, blocking collectives, per_device(): block_part = lax.all_gather(block_part, 'y', axis=0, tiled=False)  13.1 us
  transfers between devices with their start and end apart: 5, of which 5 were waited for; matrix products, arithmetic and copies ran while one was open for 6% of the time, Pallas kernels for 0%

profile of v7, /device:TPU:64, one launch (start us, length us, event | category | flops | bytes accessed | tf_op | source)
XLA Modules:
  0.0 378.6 jit_solution(2145529759691780152)
XLA Ops:
  8.5 15.0 %all-gather = bf16[256,128]{0,1:T(8,128)(2,1)S(1)} all-gather(bf16[128,128]{0,1:T(8,128)(2,1)S(1)} %pad_maximum_fusion.1), channel_id=2, replica_groups=mesh['zh'=2,'y'=4,'x'=4,'zlh'=4,'zll'=2,'c'=2] {'zh'}, dimensions={0}, use_global_device_ids=true | all-gather | bytes 98304 | tf_op jit(solution)/shard_map/all_gather | solution.py:113
  23.7 13.1 %all-gather.1 = bf16[8,128,128]{2,1,0:T(8,128)(2,1)S(1)} all-gather(bf16[2,128,128]{2,1,0:T(8,128)(2,1)S(1)} %bitcast.92), channel_id=3, replica_groups=mesh['zh'=2,'y'=4,'x'=4,'zlh'=4,'zll'=2,'c'=2] {'y'}, dimensions={0}, use_global_device_ids=true | all-gather | bytes 327680 | tf_op jit(solution)/shard_map/all_gather | solution.py:114
  38.5 4.3 %all-to-all-start = ((bf16[4,4,2,128,128]{3,2,1,4,0:T(2,128)(2,1)}), bf16[4,4,2,128,128]{3,2,1,4,0:T(2,128)(2,1)S(1)}, u32[]{:S(2)}, u32[]{:S(2)}) async-start(bf16[4,4,2,128,128]{3,2,1,4,0:T(2,128)(2,1)} %broadcast_in_dim.19), calls=%async_computation | async-start | bytes 2097152 | tf_op jit(solution)/shard_map/all_to_all | solution.py:115
  45.2 8.5 %all-to-all-done = bf16[4,4,2,128,128]{3,2,1,4,0:T(2,128)(2,1)S(1)} async-done(((bf16[4,4,2,128,128]{3,2,1,4,0:T(2,128)(2,1)}), bf16[4,4,2,128,128]{3,2,1,4,0:T(2,128)(2,1)S(1)}, u32[]{:S(2)}, u32[]{:S(2)}) %all-to-all-start) | async-done | bytes 1048608 | tf_op jit(solution)/shard_map/all_to_all | solution.py:115
  56.9 2.1 fusion.21
  59.6 4.3 %all_to_all.40 = bf16[2,8,128,180]{2,1,3,0:T(8,128)(2,1)S(1)} all-to-all(bf16[2,8,128,180]{2,1,3,0:T(8,128)(2,1)S(1)} %copy.90), channel_id=1, replica_groups=mesh['zh'=2,'y'=4,'x'=4,'zlh'=4,'zll'=2,'c'=2] {'c'}, dimensions={0} | all-to-all | bytes 1474560 | tf_op jit(solution)/shard_map/all_to_all | solution.py:157
  65.1 11.3 %all-to-all-start.2 = ((bf16[8,128,180]{1,2,0:T(8,128)(2,1)}), bf16[8,128,180]{1,2,0:T(8,128)(2,1)S(1)}, u32[]{:S(2)}, u32[]{:S(2)}) async-start(bf16[8,128,180]{1,2,0:T(8,128)(2,1)} %copy.116), calls=%async_computation.2 | async-start | bytes 753664 | tf_op jit(solution)/shard_map/all_to_all | solution.py:159
  79.5 16.6 %all-to-all-done.2 = bf16[8,128,180]{1,2,0:T(8,128)(2,1)S(1)} async-done(((bf16[8,128,180]{1,2,0:T(8,128)(2,1)}), bf16[8,128,180]{1,2,0:T(8,128)(2,1)S(1)}, u32[]{:S(2)}, u32[]{:S(2)}) %all-to-all-start.2) | async-done | bytes 368672 | tf_op jit(solution)/shard_map/all_to_all | solution.py:159
  98.1 2.4 scatter_custom_fusion
  100.6 28.0 %all_to_all.41 = bf16[32,20,182]{2,1,0:T(8,128)(2,1)S(1)} all-to-all(bf16[32,20,182]{2,1,0:T(8,128)(2,1)S(1)} %reshape.375), channel_id=1, replica_groups=mesh['zh'=2,'y'=4,'x'=4,'zlh'=4,'zll'=2,'c'=2] {'zh','y','x'}, dimensions={0} | all-to-all | bytes 465920 | tf_op jit(solution)/shard_map/all_to_all | solution.py:193
  129.7 66.4 %all-gather.6.cloned.1.call-done = bf16[8,640,182]{1,2,0:T(8,128)(2,1)} async-done(((bf16[1,640,182]{1,2,0:T(8,128)(2,1)}), bf16[8,640,182]{1,2,0:T(8,128)(2,1)}) %all-gather.6.cloned.1.call-update) | async-done | bytes 1863696 | tf_op jit(solution)/shard_map/all_gather | solution.py:200
  196.1 3.0 copy.100
  201.0 9.7 %reshape.376 = bf16[8,2,180,360]{2,1,0,3:T(2,128)(2,1)} reshape(bf16[1,2880,2,180]{1,3,2,0:T(8,128)(2,1)S(1)} %copy.102) | data formatting | bytes 4147200 | tf_op jit(solution)/shard_map/reshape | solution.py:208
  210.7 6.4 %reshape.378 = bf16[180,4,2,2,180]{4,3,2,1,0:T(2,128)(2,1)S(1)} reshape(bf16[1,180,2880]{2,1,0:T(8,128)(2,1)} %param.23) | data formatting | bytes 2073600 | tf_op jit(solution)/shard_map/reshape | solution.py:222
  217.1 7.9 %all-gather.8.cloned.1.call-done = bf16[16,640,182]{1,0,2:T(8,128)(2,1)} async-done(((bf16[8,640,182]{1,0,2:T(8,128)(2,1)}), bf16[16,640,182]{1,0,2:T(8,128)(2,1)}) %all-gather.8.cloned.1.call-update) | async-done | bytes 3727376 | tf_op jit(solution)/shard_map/all_gather | solution.py:201
  225.0 3.0 copy.101
  228.2 4.1 %fusion.14 = f32[640,360]{0,1:T(8,128)} fusion(bf16[8,2,180,360]{2,1,0,3:T(2,128)(2,1)S(1)} %copy-done.1, bf16[2,8,640,182]{2,3,1,0:T(8,128)(2,1)S(1)} %bitcast.89, f32[640]{0:T(1024)S(1)} %add_rsqrt_fusion), kind=kOutput, calls=%fused_computation.17 | convolution fusion | flops 1327334400 | bytes 6725120 | tf_op jit(solution)/shard_map/czrk,zckf->rf/dot_general | solution.py:209
  237.3 7.7 %all_to_all.42 = bf16[2,4,2,640,180]{3,1,4,2,0:T(4,128)(2,1)} all-to-all(bf16[2,4,2,640,180]{3,1,4,2,0:T(4,128)(2,1)S(1)} %copy.105), channel_id=1, replica_groups=mesh['zh'=2,'y'=4,'x'=4,'zlh'=4,'zll'=2,'c'=2] {'c'}, dimensions={0} | all-to-all | bytes 7372800 | tf_op jit(solution)/shard_map/all_to_all | solution.py:226
  245.0 5.0 %reduce_sum.111 = bf16[4,2,640,180]{2,0,3,1:T(4,128)(2,1)S(1)} reduce(bf16[2,4,2,640,180]{3,1,4,2,0:T(4,128)(2,1)} %all_to_all.42, bf16[]{:T(256)} %constant.90.clone.1), dimensions={0}, to_apply=%region_10.11 | reduce | flops 921600 | bytes 5529602 | tf_op jit(solution)/shard_map/reduce_sum | solution.py:227
  251.0 25.3 %all_to_all.43 = bf16[2,4,640,180]{2,1,3,0:T(4,128)(2,1)S(1)} all-to-all(bf16[2,4,640,180]{2,1,3,0:T(4,128)(2,1)S(1)} %copy.107), channel_id=1, replica_groups=mesh['zh'=2,'y'=4,'x'=4,'zlh'=4,'zll'=2,'c'=2] {'zll'}, dimensions={0} | all-to-all | bytes 3686400 | tf_op jit(solution)/shard_map/all_to_all | solution.py:228
  276.3 2.0 reduce_sum.112
  278.4 52.8 %all_to_all.44 = bf16[4,640,180]{1,2,0:T(8,128)(2,1)S(1)} all-to-all(bf16[4,640,180]{1,2,0:T(8,128)(2,1)S(1)} %copy.108), channel_id=1, replica_groups=mesh['zh'=2,'y'=4,'x'=4,'zlh'=4,'zll'=2,'c'=2] {'zlh'}, dimensions={0} | all-to-all | bytes 1843200 | tf_op jit(solution)/shard_map/all_to_all | solution.py:230
  332.5 11.5 %all-to-all-start.7 = ((bf16[32,20,180]{2,1,0:T(8,128)(2,1)}), bf16[32,20,180]{2,1,0:T(8,128)(2,1)S(1)}, u32[]{:S(2)}, u32[]{:S(2)}) async-start(bf16[32,20,180]{2,1,0:T(8,128)(2,1)} %reshape.379), calls=%async_computation.7 | async-start | bytes 786432 | tf_op jit(solution)/shard_map/all_to_all | solution.py:232
  344.3 23.3 %all-to-all-done.7 = bf16[32,20,180]{2,1,0:T(8,128)(2,1)S(1)} async-done(((bf16[32,20,180]{2,1,0:T(8,128)(2,1)}), bf16[32,20,180]{2,1,0:T(8,128)(2,1)S(1)}, u32[]{:S(2)}, u32[]{:S(2)}) %all-to-all-start.7) | async-done | bytes 230432 | tf_op jit(solution)/shard_map/all_to_all | solution.py:232
  (102 shorter events, 30.8 us)
Async XLA Ops:
  6.5 52.4 %copy-start = (bf16[128,2880]{0,1:T(8,128)(2,1)S(1)}, bf16[128,2880]{0,1:T(8,128)(2,1)}, u32[]{:S(2)}) copy-start(bf16[128,2880]{0,1:T(8,128)(2,1)} %param.18) | copy-start | bytes 2211844
  6.5 36.3 %copy-start.6 = (f32[32]{0:T(128)S(1)}, f32[32]{0:T(128)}, u32[]{:S(2)}) copy-start(f32[32]{0:T(128)} %constant.97.clone) | copy-start | bytes 388
  6.5 36.4 %copy-start.4 = (bf16[128,128]{1,0:T(8,128)(2,1)S(1)}, bf16[128,128]{1,0:T(8,128)(2,1)}, u32[]{:S(2)}) copy-start(bf16[128,128]{1,0:T(8,128)(2,1)} %param.14) | copy-start | bytes 98308
  38.5 15.2 %all-to-all-start = ((bf16[4,4,2,128,128]{3,2,1,4,0:T(2,128)(2,1)}), bf16[4,4,2,128,128]{3,2,1,4,0:T(2,128)(2,1)S(1)}, u32[]{:S(2)}, u32[]{:S(2)}) async-start(bf16[4,4,2,128,128]{3,2,1,4,0:T(2,128)(2,1)} %broadcast_in_dim.19), calls=%async_computation | async-start | bytes 2097152 | tf_op jit(solution)/shard_map/all_to_all | solution.py:115
  54.4 1.7 copy-start.8
  59.3 17.1 %copy-start.5 = (s32[128,4]{0,1:T(4,128)S(1)}, s32[128,4]{0,1:T(4,128)}, u32[]{:S(2)}) copy-start(s32[128,4]{0,1:T(4,128)} %param.20) | copy-start | bytes 6148
  65.1 31.1 %all-to-all-start.2 = ((bf16[8,128,180]{1,2,0:T(8,128)(2,1)}), bf16[8,128,180]{1,2,0:T(8,128)(2,1)S(1)}, u32[]{:S(2)}, u32[]{:S(2)}) async-start(bf16[8,128,180]{1,2,0:T(8,128)(2,1)} %copy.116), calls=%async_computation.2 | async-start | bytes 753664 | tf_op jit(solution)/shard_map/all_to_all | solution.py:159
  76.4 119.7 %all-gather.6.cloned.1.call-start = ((), (), s32[]{:S(2)}) async-start(), calls=%async_computation.8 | async-start | bytes 2119680 | tf_op jit(solution)/shard_map/all_gather | solution.py:200
  96.2 0.6 copy-start.2
  129.7 95.4 %all-gather.8.cloned.1.call-start = ((), (), s32[]{:S(2)}) async-start(), calls=%async_computation.9 | async-start | bytes 5591040 | tf_op jit(solution)/shard_map/all_gather | solution.py:201
  225.0 3.1 copy-start.1
  278.3 65.9 %copy-start.7 = (f32[128,4]{0,1:T(4,128)S(1)}, f32[128,4]{0,1:T(4,128)}, u32[]{:S(2)}) copy-start(f32[128,4]{0,1:T(4,128)} %param.21) | copy-start | bytes 6148
  331.5 38.9 %copy-start.3 = (f32[128,180]{0,1:T(8,128)S(1)}, f32[128,180]{0,1:T(8,128)}, u32[]{:S(2)}) copy-start(f32[128,180]{0,1:T(8,128)} %copy-done.2) | copy-start | bytes 276484
  332.5 35.1 %all-to-all-start.7 = ((bf16[32,20,180]{2,1,0:T(8,128)(2,1)}), bf16[32,20,180]{2,1,0:T(8,128)(2,1)S(1)}, u32[]{:S(2)}, u32[]{:S(2)}) async-start(bf16[32,20,180]{2,1,0:T(8,128)(2,1)} %reshape.379), calls=%async_computation.7 | async-start | bytes 786432 | tf_op jit(solution)/shard_map/all_to_all | solution.py:232
Sparse Core Ops, SparseCore 0:
  129.8 66.2 all-gather.5
  199.3 25.7 all-gather.7

commit v8 on v7

--- a/solution.py
+++ b/solution.py
@@ -110,8 +110,15 @@
     )
     key_value = jnp.concatenate([key_rot, value_block], axis=1)
     score_scale = 1.0 / math.sqrt(HEAD_SIZE)
-    block_part = lax.all_gather(key_value, "zh", axis=0, tiled=False)
-    block_part = lax.all_gather(block_part, "y", axis=0, tiled=False)
+    block_part = key_value
+    for axis_name in ("zh", "y"):
+        block_part = lax.all_to_all(
+            jnp.broadcast_to(block_part[None], (lax.axis_size(axis_name),) + block_part.shape),
+            axis_name,
+            0,
+            0,
+            tiled=True,
+        )
     block_part = lax.all_to_all(
         jnp.broadcast_to(block_part[None], (lax.axis_size("x"),) + block_part.shape),
         "x",

time: 380 us -> 381 us (level)
  blocking collectives: 146 us -> 112 us
  waiting for transfers between devices: 123 us -> 142 us
  starting transfers between devices: 27.1 us -> 40.4 us
    all_gather x2 -> x0, blocking collectives: 28.1 us -> none  [the longest x1 15 us: per_device(): block_part = lax.all_gather(key_value, 'zh', axis=0, tiled=False)]
    all_to_all x0 -> x2, waiting for transfers between devices: none -> 17.8 us  [per_device(): lax.all_to_all(jnp.broadcast_to(block_part[None], (lax.axis_size(axis_nam...]
    all_to_all x0 -> x2, starting transfers between devices: none -> 17.7 us  [per_device(): lax.all_to_all(jnp.broadcast_to(block_part[None], (lax.axis_size(axis_nam...]
    all_to_all x1, blocking collectives: 28 us -> 21.7 us  [per_device(): lax.all_to_all(send_rows.reshape(ctx_count, exp_local * capacity, send_wi...]
    all_to_all x1, starting transfers between devices: 11.3 us -> 6.82 us  [per_device(): lax.all_to_all(head_part, ZL, split_axis=0, concat_axis=0, tiled=True)]
  transfers between devices with their start and end apart: 5 -> 7, of which waited for: 5 -> 7; matrix products, arithmetic and copies ran while one was open for 6% -> 7% of each run, Pallas kernels for 0% -> 0%
where the time goes in v8:
time: 381 us; the launch traced here: 380 us
  waiting for transfers between devices  142 us (37%)
  blocking collectives  112 us (29%)
  local copies, waits for them, and re-layouts  45.9 us (12%)
  starting transfers between devices  40.4 us (11%)
  other arithmetic  16.2 us (4%)
  between operations  13.9 us (4%)
  matrix products  9.23 us (2%)
    all_gather x1, waiting for transfers between devices, per_device(): gathered = lax.all_gather(received, ZL, axis=0, tiled=False)  66.4 us
    all_to_all x1, blocking collectives, per_device(): partial_value = lax.all_to_all(partial_value, 'zlh', 0, 0, tiled=True)  52.8 us
    all_to_all x1, blocking collectives, per_device(): lax.all_to_all(partial_value.transpose(1, 0, 2, 3), 'zll', 0, 0, tiled=True)  25.3 us
    all_to_all x1, waiting for transfers between devices, per_device(): lax.all_to_all(expert_cols.reshape(ctx_count, capacity, col_width), CTX,...  23.3 us
    all_to_all x1, blocking collectives, per_device(): lax.all_to_all(send_rows.reshape(ctx_count, exp_local * capacity, send_wi...  21.7 us
    all_to_all x2, waiting for transfers between devices, per_device(): lax.all_to_all(jnp.broadcast_to(block_part[None], (lax.axis_size(axis_nam...  17.8 us
    all_to_all x2, starting transfers between devices, per_device(): lax.all_to_all(jnp.broadcast_to(block_part[None], (lax.axis_size(axis_nam...  17.7 us
    all_to_all x1, waiting for transfers between devices, per_device(): lax.all_to_all(head_part, ZL, split_axis=0, concat_axis=0, tiled=True)  16.6 us
  transfers between devices with their start and end apart: 7, of which 7 were waited for; matrix products, arithmetic and copies ran while one was open for 7% of the time, Pallas kernels for 0%

profile of v8, /device:TPU:64, one launch (start us, length us, event | category | flops | bytes accessed | tf_op | source)
XLA Modules:
  0.0 379.6 jit_solution(13934790284559736053)
XLA Ops:
  9.2 13.3 %all-to-all-start = ((bf16[2,128,128]{1,2,0:T(8,128)(2,1)}), bf16[2,128,128]{1,2,0:T(8,128)(2,1)S(1)}, u32[]{:S(2)}, u32[]{:S(2)}) async-start(bf16[2,128,128]{1,2,0:T(8,128)(2,1)} %broadcast_in_dim.23), calls=%async_computation | async-start | bytes 131072 | tf_op jit(solution)/shard_map/all_to_all | solution.py:115
  24.2 11.2 %all-to-all-done = bf16[2,128,128]{1,2,0:T(8,128)(2,1)S(1)} async-done(((bf16[2,128,128]{1,2,0:T(8,128)(2,1)}), bf16[2,128,128]{1,2,0:T(8,128)(2,1)S(1)}, u32[]{:S(2)}, u32[]{:S(2)}) %all-to-all-start) | async-done | bytes 65568 | tf_op jit(solution)/shard_map/all_to_all | solution.py:115
  36.4 4.5 %all-to-all-start.1 = ((bf16[4,2,128,128]{2,1,3,0:T(2,128)(2,1)}), bf16[4,2,128,128]{2,1,3,0:T(2,128)(2,1)S(1)}, u32[]{:S(2)}, u32[]{:S(2)}) async-start(bf16[4,2,128,128]{2,1,3,0:T(2,128)(2,1)} %broadcast_in_dim.24), calls=%async_computation.1 | async-start | bytes 524288 | tf_op jit(solution)/shard_map/all_to_all | solution.py:115
  40.9 6.6 %all-to-all-done.1 = bf16[4,2,128,128]{2,1,3,0:T(2,128)(2,1)S(1)} async-done(((bf16[4,2,128,128]{2,1,3,0:T(2,128)(2,1)}), bf16[4,2,128,128]{2,1,3,0:T(2,128)(2,1)S(1)}, u32[]{:S(2)}, u32[]{:S(2)}) %all-to-all-start.1) | async-done | bytes 262176 | tf_op jit(solution)/shard_map/all_to_all | solution.py:115
  49.2 4.3 %all-to-all-start.2 = ((bf16[4,4,2,128,128]{3,2,1,4,0:T(2,128)(2,1)}), bf16[4,4,2,128,128]{3,2,1,4,0:T(2,128)(2,1)S(1)}, u32[]{:S(2)}, u32[]{:S(2)}) async-start(bf16[4,4,2,128,128]{3,2,1,4,0:T(2,128)(2,1)} %broadcast_in_dim.25), calls=%async_computation.2 | async-start | bytes 2097152 | tf_op jit(solution)/shard_map/all_to_all | solution.py:122
  55.4 10.2 %all-to-all-done.2 = bf16[4,4,2,128,128]{3,2,1,4,0:T(2,128)(2,1)S(1)} async-done(((bf16[4,4,2,128,128]{3,2,1,4,0:T(2,128)(2,1)}), bf16[4,4,2,128,128]{3,2,1,4,0:T(2,128)(2,1)S(1)}, u32[]{:S(2)}, u32[]{:S(2)}) %all-to-all-start.2) | async-done | bytes 1048608 | tf_op jit(solution)/shard_map/all_to_all | solution.py:122
  71.5 4.3 %all_to_all.50 = bf16[2,8,128,180]{2,1,3,0:T(8,128)(2,1)S(1)} all-to-all(bf16[2,8,128,180]{2,1,3,0:T(8,128)(2,1)S(1)} %copy.94), channel_id=1, replica_groups=mesh['zh'=2,'y'=4,'x'=4,'zlh'=4,'zll'=2,'c'=2] {'c'}, dimensions={0} | all-to-all | bytes 1474560 | tf_op jit(solution)/shard_map/all_to_all | solution.py:164
  76.9 6.8 %all-to-all-start.4 = ((bf16[8,128,180]{1,2,0:T(8,128)(2,1)}), bf16[8,128,180]{1,2,0:T(8,128)(2,1)S(1)}, u32[]{:S(2)}, u32[]{:S(2)}) async-start(bf16[8,128,180]{1,2,0:T(8,128)(2,1)} %copy.119), calls=%async_computation.4 | async-start | bytes 753664 | tf_op jit(solution)/shard_map/all_to_all | solution.py:166
  86.9 16.6 %all-to-all-done.4 = bf16[8,128,180]{1,2,0:T(8,128)(2,1)S(1)} async-done(((bf16[8,128,180]{1,2,0:T(8,128)(2,1)}), bf16[8,128,180]{1,2,0:T(8,128)(2,1)S(1)}, u32[]{:S(2)}, u32[]{:S(2)}) %all-to-all-start.4) | async-done | bytes 368672 | tf_op jit(solution)/shard_map/all_to_all | solution.py:166
  105.5 2.4 scatter_custom_fusion
  108.0 21.7 %all_to_all.51 = bf16[32,20,182]{2,1,0:T(8,128)(2,1)S(1)} all-to-all(bf16[32,20,182]{2,1,0:T(8,128)(2,1)S(1)} %reshape.377), channel_id=1, replica_groups=mesh['zh'=2,'y'=4,'x'=4,'zlh'=4,'zll'=2,'c'=2] {'zh','y','x'}, dimensions={0} | all-to-all | bytes 465920 | tf_op jit(solution)/shard_map/all_to_all | solution.py:200
  130.7 66.4 %all-gather.4.cloned.1.call-done = bf16[8,640,182]{1,2,0:T(8,128)(2,1)} async-done(((bf16[1,640,182]{1,2,0:T(8,128)(2,1)}), bf16[8,640,182]{1,2,0:T(8,128)(2,1)}) %all-gather.4.cloned.1.call-update) | async-done | bytes 1863696 | tf_op jit(solution)/shard_map/all_gather | solution.py:207
  197.1 3.0 copy.104
  202.0 9.7 %reshape.378 = bf16[8,2,180,360]{2,1,0,3:T(2,128)(2,1)} reshape(bf16[1,2880,2,180]{1,3,2,0:T(8,128)(2,1)S(1)} %copy.106) | data formatting | bytes 4147200 | tf_op jit(solution)/shard_map/reshape | solution.py:215
  211.7 6.4 %reshape.380 = bf16[180,4,2,2,180]{4,3,2,1,0:T(2,128)(2,1)S(1)} reshape(bf16[1,180,2880]{2,1,0:T(8,128)(2,1)} %param.23) | data formatting | bytes 2073600 | tf_op jit(solution)/shard_map/reshape | solution.py:229
  218.1 7.9 %all-gather.6.cloned.1.call-done = bf16[16,640,182]{1,0,2:T(8,128)(2,1)} async-done(((bf16[8,640,182]{1,0,2:T(8,128)(2,1)}), bf16[16,640,182]{1,0,2:T(8,128)(2,1)}) %all-gather.6.cloned.1.call-update) | async-done | bytes 3727376 | tf_op jit(solution)/shard_map/all_gather | solution.py:208
  226.0 3.0 copy.105
  229.1 4.1 %fusion.14 = f32[640,360]{0,1:T(8,128)} fusion(bf16[8,2,180,360]{2,1,0,3:T(2,128)(2,1)S(1)} %copy-done.1, bf16[2,8,640,182]{2,3,1,0:T(8,128)(2,1)S(1)} %bitcast.87, f32[640]{0:T(1024)S(1)} %add_rsqrt_fusion), kind=kOutput, calls=%fused_computation.17 | convolution fusion | flops 1327334400 | bytes 6725120 | tf_op jit(solution)/shard_map/czrk,zckf->rf/dot_general | solution.py:216
  238.3 7.7 %all_to_all.52 = bf16[2,4,2,640,180]{3,1,4,2,0:T(4,128)(2,1)} all-to-all(bf16[2,4,2,640,180]{3,1,4,2,0:T(4,128)(2,1)S(1)} %copy.109), channel_id=1, replica_groups=mesh['zh'=2,'y'=4,'x'=4,'zlh'=4,'zll'=2,'c'=2] {'c'}, dimensions={0} | all-to-all | bytes 7372800 | tf_op jit(solution)/shard_map/all_to_all | solution.py:233
  246.0 5.0 %reduce_sum.111 = bf16[4,2,640,180]{2,0,3,1:T(4,128)(2,1)S(1)} reduce(bf16[2,4,2,640,180]{3,1,4,2,0:T(4,128)(2,1)} %all_to_all.52, bf16[]{:T(256)} %constant.90.clone.1), dimensions={0}, to_apply=%region_10.11 | reduce | flops 921600 | bytes 5529602 | tf_op jit(solution)/shard_map/reduce_sum | solution.py:234
  252.0 25.3 %all_to_all.53 = bf16[2,4,640,180]{2,1,3,0:T(4,128)(2,1)S(1)} all-to-all(bf16[2,4,640,180]{2,1,3,0:T(4,128)(2,1)S(1)} %copy.111), channel_id=1, replica_groups=mesh['zh'=2,'y'=4,'x'=4,'zlh'=4,'zll'=2,'c'=2] {'zll'}, dimensions={0} | all-to-all | bytes 3686400 | tf_op jit(solution)/shard_map/all_to_all | solution.py:235
  279.4 52.8 %all_to_all.54 = bf16[4,640,180]{1,2,0:T(8,128)(2,1)S(1)} all-to-all(bf16[4,640,180]{1,2,0:T(8,128)(2,1)S(1)} %copy.112), channel_id=1, replica_groups=mesh['zh'=2,'y'=4,'x'=4,'zlh'=4,'zll'=2,'c'=2] {'zlh'}, dimensions={0} | all-to-all | bytes 1843200 | tf_op jit(solution)/shard_map/all_to_all | solution.py:237
  333.5 11.5 %all-to-all-start.9 = ((bf16[32,20,180]{2,1,0:T(8,128)(2,1)}), bf16[32,20,180]{2,1,0:T(8,128)(2,1)S(1)}, u32[]{:S(2)}, u32[]{:S(2)}) async-start(bf16[32,20,180]{2,1,0:T(8,128)(2,1)} %reshape.381), calls=%async_computation.9 | async-start | bytes 786432 | tf_op jit(solution)/shard_map/all_to_all | solution.py:239
  345.3 23.3 %all-to-all-done.9 = bf16[32,20,180]{2,1,0:T(8,128)(2,1)S(1)} async-done(((bf16[32,20,180]{2,1,0:T(8,128)(2,1)}), bf16[32,20,180]{2,1,0:T(8,128)(2,1)S(1)}, u32[]{:S(2)}, u32[]{:S(2)}) %all-to-all-start.9) | async-done | bytes 230432 | tf_op jit(solution)/shard_map/all_to_all | solution.py:239
  (102 shorter events, 37.7 us)
Async XLA Ops:
  6.5 64.3 %copy-start = (bf16[128,2880]{0,1:T(8,128)(2,1)S(1)}, bf16[128,2880]{0,1:T(8,128)(2,1)}, u32[]{:S(2)}) copy-start(bf16[128,2880]{0,1:T(8,128)(2,1)} %param.18) | copy-start | bytes 2211844
  9.2 26.3 %all-to-all-start = ((bf16[2,128,128]{1,2,0:T(8,128)(2,1)}), bf16[2,128,128]{1,2,0:T(8,128)(2,1)S(1)}, u32[]{:S(2)}, u32[]{:S(2)}) async-start(bf16[2,128,128]{1,2,0:T(8,128)(2,1)} %broadcast_in_dim.23), calls=%async_computation | async-start | bytes 131072 | tf_op jit(solution)/shard_map/all_to_all | solution.py:115
  36.4 11.1 %all-to-all-start.1 = ((bf16[4,2,128,128]{2,1,3,0:T(2,128)(2,1)}), bf16[4,2,128,128]{2,1,3,0:T(2,128)(2,1)S(1)}, u32[]{:S(2)}, u32[]{:S(2)}) async-start(bf16[4,2,128,128]{2,1,3,0:T(2,128)(2,1)} %broadcast_in_dim.24), calls=%async_computation.1 | async-start | bytes 524288 | tf_op jit(solution)/shard_map/all_to_all | solution.py:115
  49.2 16.4 %all-to-all-start.2 = ((bf16[4,4,2,128,128]{3,2,1,4,0:T(2,128)(2,1)}), bf16[4,4,2,128,128]{3,2,1,4,0:T(2,128)(2,1)S(1)}, u32[]{:S(2)}, u32[]{:S(2)}) async-start(bf16[4,4,2,128,128]{3,2,1,4,0:T(2,128)(2,1)} %broadcast_in_dim.25), calls=%async_computation.2 | async-start | bytes 2097152 | tf_op jit(solution)/shard_map/all_to_all | solution.py:122
  66.3 1.7 copy-start.6
  71.2 12.6 %copy-start.4 = (s32[128,4]{0,1:T(4,128)S(1)}, s32[128,4]{0,1:T(4,128)}, u32[]{:S(2)}) copy-start(s32[128,4]{0,1:T(4,128)} %param.20) | copy-start | bytes 6148
  76.9 26.6 %all-to-all-start.4 = ((bf16[8,128,180]{1,2,0:T(8,128)(2,1)}), bf16[8,128,180]{1,2,0:T(8,128)(2,1)S(1)}, u32[]{:S(2)}, u32[]{:S(2)}) async-start(bf16[8,128,180]{1,2,0:T(8,128)(2,1)} %copy.119), calls=%async_computation.4 | async-start | bytes 753664 | tf_op jit(solution)/shard_map/all_to_all | solution.py:166
  83.8 113.3 %all-gather.4.cloned.1.call-start = ((), (), s32[]{:S(2)}) async-start(), calls=%async_computation.10 | async-start | bytes 2119680 | tf_op jit(solution)/shard_map/all_gather | solution.py:207
  103.6 0.6 copy-start.2
  130.7 95.4 %all-gather.6.cloned.1.call-start = ((), (), s32[]{:S(2)}) async-start(), calls=%async_computation.11 | async-start | bytes 5591040 | tf_op jit(solution)/shard_map/all_gather | solution.py:208
  226.0 3.1 copy-start.1
  279.3 65.9 %copy-start.5 = (f32[128,4]{0,1:T(4,128)S(1)}, f32[128,4]{0,1:T(4,128)}, u32[]{:S(2)}) copy-start(f32[128,4]{0,1:T(4,128)} %param.21) | copy-start | bytes 6148
  332.4 38.9 %copy-start.3 = (f32[128,180]{0,1:T(8,128)S(1)}, f32[128,180]{0,1:T(8,128)}, u32[]{:S(2)}) copy-start(f32[128,180]{0,1:T(8,128)} %copy-done.2) | copy-start | bytes 276484
  333.5 35.1 %all-to-all-start.9 = ((bf16[32,20,180]{2,1,0:T(8,128)(2,1)}), bf16[32,20,180]{2,1,0:T(8,128)(2,1)S(1)}, u32[]{:S(2)}, u32[]{:S(2)}) async-start(bf16[32,20,180]{2,1,0:T(8,128)(2,1)} %reshape.381), calls=%async_computation.9 | async-start | bytes 786432 | tf_op jit(solution)/shard_map/all_to_all | solution.py:239
Sparse Core Ops, SparseCore 0:
  130.8 66.2 all-gather.3
  200.3 25.7 all-gather.5

commit v9 on v7

--- a/solution.py
+++ b/solution.py
@@ -227,8 +227,7 @@
     partial_value = jnp.sum(partial_value.astype(jnp.float32), axis=0).astype(jnp.bfloat16)
     partial_value = lax.all_to_all(partial_value.transpose(1, 0, 2, 3), "zll", 0, 0, tiled=True)
     partial_value = jnp.sum(partial_value.astype(jnp.float32), axis=0).astype(jnp.bfloat16)
-    partial_value = lax.all_to_all(partial_value, "zlh", 0, 0, tiled=True)
-    expert_cols = jnp.sum(partial_value.astype(jnp.float32), axis=0).astype(jnp.bfloat16)
+    expert_cols = lax.psum_scatter(partial_value, "zlh", scatter_dimension=0, tiled=True)[0]
     returned = lax.all_to_all(
         expert_cols.reshape(ctx_count, capacity, col_width),
         CTX,

time: 380 us -> 392 us (1.032)
  the two profiles are of different devices: /device:TPU:64 before, /device:TPU:32 now
where the time goes in v9:
time: 392 us; the launch traced here: 391 us
  waiting for transfers between devices  164 us (42%)
  blocking collectives  104 us (27%)
  local copies, waits for them, and re-layouts  45.6 us (12%)
  starting transfers between devices  39.8 us (10%)
  other arithmetic  15.4 us (4%)
  between operations  13.6 us (3%)
  matrix products  9.22 us (2%)
    all_gather x1, waiting for transfers between devices, per_device(): gathered = lax.all_gather(received, ZL, axis=0, tiled=False)  57.4 us
    unnamed x4, waiting for transfers between devices  47.6 us
    all_to_all x1, blocking collectives, per_device(): lax.all_to_all(send_rows.reshape(ctx_count, exp_local * capacity, send_wi...  37.5 us
    all_to_all x1, waiting for transfers between devices, per_device(): lax.all_to_all(expert_cols.reshape(ctx_count, capacity, col_width), CTX,...  26.9 us
    all_to_all x1, blocking collectives, per_device(): lax.all_to_all(partial_value.transpose(1, 0, 2, 3), 'zll', 0, 0, tiled=True)  25 us
    all_to_all x1, starting transfers between devices, per_device(): lax.all_to_all(expert_cols.reshape(ctx_count, capacity, col_width), CTX,...  24.5 us
    all_to_all x1, waiting for transfers between devices, per_device(): lax.all_to_all(head_part, ZL, split_axis=0, concat_axis=0, tiled=True)  18 us
    all_gather x1, blocking collectives, per_device(): block_part = lax.all_gather(key_value, 'zh', axis=0, tiled=False)  15.9 us
  transfers between devices with their start and end apart: 6, of which 6 were waited for; matrix products, arithmetic and copies ran while one was open for 6% of the time, Pallas kernels for 0%

profile of v9, /device:TPU:32, one launch (start us, length us, event | category | flops | bytes accessed | tf_op | source)
XLA Modules:
  0.0 391.5 jit_solution(13716107392366885719)
XLA Ops:
  8.5 15.9 %all-gather = bf16[256,128]{0,1:T(8,128)(2,1)S(1)} all-gather(bf16[128,128]{0,1:T(8,128)(2,1)S(1)} %pad_maximum_fusion.1), channel_id=2, replica_groups=mesh['zh'=2,'y'=4,'x'=4,'zlh'=4,'zll'=2,'c'=2] {'zh'}, dimensions={0}, use_global_device_ids=true | all-gather | bytes 98304 | tf_op jit(solution)/shard_map/all_gather | solution.py:113
  24.6 13.1 %all-gather.1 = bf16[8,128,128]{2,1,0:T(8,128)(2,1)S(1)} all-gather(bf16[2,128,128]{2,1,0:T(8,128)(2,1)S(1)} %bitcast.93), channel_id=3, replica_groups=mesh['zh'=2,'y'=4,'x'=4,'zlh'=4,'zll'=2,'c'=2] {'y'}, dimensions={0}, use_global_device_ids=true | all-gather | bytes 327680 | tf_op jit(solution)/shard_map/all_gather | solution.py:114
  39.4 4.3 %all-to-all-start = ((bf16[4,4,2,128,128]{3,2,1,4,0:T(2,128)(2,1)}), bf16[4,4,2,128,128]{3,2,1,4,0:T(2,128)(2,1)S(1)}, u32[]{:S(2)}, u32[]{:S(2)}) async-start(bf16[4,4,2,128,128]{3,2,1,4,0:T(2,128)(2,1)} %broadcast_in_dim.19), calls=%async_computation | async-start | bytes 2097152 | tf_op jit(solution)/shard_map/all_to_all | solution.py:115
  46.0 8.5 %all-to-all-done = bf16[4,4,2,128,128]{3,2,1,4,0:T(2,128)(2,1)S(1)} async-done(((bf16[4,4,2,128,128]{3,2,1,4,0:T(2,128)(2,1)}), bf16[4,4,2,128,128]{3,2,1,4,0:T(2,128)(2,1)S(1)}, u32[]{:S(2)}, u32[]{:S(2)}) %all-to-all-start) | async-done | bytes 1048608 | tf_op jit(solution)/shard_map/all_to_all | solution.py:115
  57.7 2.1 fusion.21
  60.5 4.3 %all_to_all.35 = bf16[2,8,128,180]{2,1,3,0:T(8,128)(2,1)S(1)} all-to-all(bf16[2,8,128,180]{2,1,3,0:T(8,128)(2,1)S(1)} %copy.114), channel_id=1, replica_groups=mesh['zh'=2,'y'=4,'x'=4,'zlh'=4,'zll'=2,'c'=2] {'c'}, dimensions={0} | all-to-all | bytes 1474560 | tf_op jit(solution)/shard_map/all_to_all | solution.py:157
  65.9 10.9 %all-to-all-start.2 = ((bf16[8,128,180]{1,2,0:T(8,128)(2,1)}), bf16[8,128,180]{1,2,0:T(8,128)(2,1)S(1)}, u32[]{:S(2)}, u32[]{:S(2)}) async-start(bf16[8,128,180]{1,2,0:T(8,128)(2,1)} %copy.140), calls=%async_computation.2 | async-start | bytes 753664 | tf_op jit(solution)/shard_map/all_to_all | solution.py:159
  80.0 18.0 %all-to-all-done.2 = bf16[8,128,180]{1,2,0:T(8,128)(2,1)S(1)} async-done(((bf16[8,128,180]{1,2,0:T(8,128)(2,1)}), bf16[8,128,180]{1,2,0:T(8,128)(2,1)S(1)}, u32[]{:S(2)}, u32[]{:S(2)}) %all-to-all-start.2) | async-done | bytes 368672 | tf_op jit(solution)/shard_map/all_to_all | solution.py:159
  100.0 2.4 scatter_custom_fusion
  102.5 37.5 %all_to_all.36 = bf16[32,20,182]{2,1,0:T(8,128)(2,1)S(1)} all-to-all(bf16[32,20,182]{2,1,0:T(8,128)(2,1)S(1)} %reshape.372), channel_id=1, replica_groups=mesh['zh'=2,'y'=4,'x'=4,'zlh'=4,'zll'=2,'c'=2] {'zh','y','x'}, dimensions={0} | all-to-all | bytes 465920 | tf_op jit(solution)/shard_map/all_to_all | solution.py:193
  141.1 57.4 %all-gather.6.cloned.1.call-done = bf16[8,640,182]{1,2,0:T(8,128)(2,1)} async-done(((bf16[1,640,182]{1,2,0:T(8,128)(2,1)}), bf16[8,640,182]{1,2,0:T(8,128)(2,1)}) %all-gather.6.cloned.1.call-update) | async-done | bytes 1863696 | tf_op jit(solution)/shard_map/all_gather | solution.py:200
  198.4 3.0 copy.124
  203.3 9.7 %reshape.373 = bf16[8,2,180,360]{2,1,0,3:T(2,128)(2,1)} reshape(bf16[1,2880,2,180]{1,3,2,0:T(8,128)(2,1)S(1)} %copy.126) | data formatting | bytes 4147200 | tf_op jit(solution)/shard_map/reshape | solution.py:208
  213.1 6.4 %reshape.375 = bf16[180,4,2,2,180]{4,3,2,1,0:T(2,128)(2,1)S(1)} reshape(bf16[1,180,2880]{2,1,0:T(8,128)(2,1)} %param.23) | data formatting | bytes 2073600 | tf_op jit(solution)/shard_map/reshape | solution.py:222
  219.5 5.9 %all-gather.8.cloned.1.call-done = bf16[16,640,182]{1,0,2:T(8,128)(2,1)} async-done(((bf16[8,640,182]{1,0,2:T(8,128)(2,1)}), bf16[16,640,182]{1,0,2:T(8,128)(2,1)}) %all-gather.8.cloned.1.call-update) | async-done | bytes 3727376 | tf_op jit(solution)/shard_map/all_gather | solution.py:201
  225.4 3.0 copy.125
  228.5 4.1 %fusion.14 = f32[640,360]{0,1:T(8,128)} fusion(bf16[8,2,180,360]{2,1,0,3:T(2,128)(2,1)S(1)} %copy-done.1, bf16[2,8,640,182]{2,3,1,0:T(8,128)(2,1)S(1)} %bitcast.90, f32[640]{0:T(1024)S(1)} %add_rsqrt_fusion), kind=kOutput, calls=%fused_computation.17 | convolution fusion | flops 1327334400 | bytes 6725120 | tf_op jit(solution)/shard_map/czrk,zckf->rf/dot_general | solution.py:209
  237.6 7.7 %all_to_all.37 = bf16[2,4,2,640,180]{3,1,4,2,0:T(4,128)(2,1)} all-to-all(bf16[2,4,2,640,180]{3,1,4,2,0:T(4,128)(2,1)S(1)} %copy.129), channel_id=1, replica_groups=mesh['zh'=2,'y'=4,'x'=4,'zlh'=4,'zll'=2,'c'=2] {'c'}, dimensions={0} | all-to-all | bytes 7372800 | tf_op jit(solution)/shard_map/all_to_all | solution.py:226
  245.4 5.0 %reduce_sum.99 = bf16[4,2,640,180]{2,0,3,1:T(4,128)(2,1)S(1)} reduce(bf16[2,4,2,640,180]{3,1,4,2,0:T(4,128)(2,1)} %all_to_all.37, bf16[]{:T(256)} %constant.89.clone.1), dimensions={0}, to_apply=%region_10.11 | reduce | flops 921600 | bytes 5529602 | tf_op jit(solution)/shard_map/reduce_sum | solution.py:227
  251.4 25.0 %all_to_all.38 = bf16[2,4,640,180]{2,1,3,0:T(4,128)(2,1)S(1)} all-to-all(bf16[2,4,640,180]{2,1,3,0:T(4,128)(2,1)S(1)} %copy.131), channel_id=1, replica_groups=mesh['zh'=2,'y'=4,'x'=4,'zlh'=4,'zll'=2,'c'=2] {'zll'}, dimensions={0} | all-to-all | bytes 3686400 | tf_op jit(solution)/shard_map/all_to_all | solution.py:228
  276.4 2.0 reduce_sum.100
  279.5 47.5 %reduce-scatter.5.cloned.1.call-done = bf16[1,640,180]{1,2,0:T(8,128)(2,1)} async-done(((bf16[4,640,180]{1,2,0:T(8,128)(2,1)}), bf16[1,640,180]{1,2,0:T(8,128)(2,1)}) %reduce-scatter.5.cloned.1.call-update) | async-done | bytes 230416
  328.9 24.5 %all-to-all-start.6 = ((bf16[32,20,180]{2,1,0:T(8,128)(2,1)}), bf16[32,20,180]{2,1,0:T(8,128)(2,1)S(1)}, u32[]{:S(2)}, u32[]{:S(2)}) async-start(bf16[32,20,180]{2,1,0:T(8,128)(2,1)} %reshape_squeeze.3), calls=%async_computation.6 | async-start | bytes 786432 | tf_op jit(solution)/shard_map/all_to_all | solution.py:231
  353.8 26.9 %all-to-all-done.6 = bf16[32,20,180]{2,1,0:T(8,128)(2,1)S(1)} async-done(((bf16[32,20,180]{2,1,0:T(8,128)(2,1)}), bf16[32,20,180]{2,1,0:T(8,128)(2,1)S(1)}, u32[]{:S(2)}, u32[]{:S(2)}) %all-to-all-start.6) | async-done | bytes 230432 | tf_op jit(solution)/shard_map/all_to_all | solution.py:231
  (103 shorter events, 32.5 us)
Async XLA Ops:
  6.5 53.3 %copy-start = (bf16[128,2880]{0,1:T(8,128)(2,1)S(1)}, bf16[128,2880]{0,1:T(8,128)(2,1)}, u32[]{:S(2)}) copy-start(bf16[128,2880]{0,1:T(8,128)(2,1)} %param.18) | copy-start | bytes 2211844
  6.5 37.1 %copy-start.6 = (f32[32]{0:T(128)S(1)}, f32[32]{0:T(128)}, u32[]{:S(2)}) copy-start(f32[32]{0:T(128)} %constant.96.clone) | copy-start | bytes 388
  6.5 37.3 %copy-start.4 = (bf16[128,128]{1,0:T(8,128)(2,1)S(1)}, bf16[128,128]{1,0:T(8,128)(2,1)}, u32[]{:S(2)}) copy-start(bf16[128,128]{1,0:T(8,128)(2,1)} %param.14) | copy-start | bytes 98308
  39.4 15.2 %all-to-all-start = ((bf16[4,4,2,128,128]{3,2,1,4,0:T(2,128)(2,1)}), bf16[4,4,2,128,128]{3,2,1,4,0:T(2,128)(2,1)S(1)}, u32[]{:S(2)}, u32[]{:S(2)}) async-start(bf16[4,4,2,128,128]{3,2,1,4,0:T(2,128)(2,1)} %broadcast_in_dim.19), calls=%async_computation | async-start | bytes 2097152 | tf_op jit(solution)/shard_map/all_to_all | solution.py:115
  55.3 1.7 copy-start.8
  60.1 16.7 %copy-start.5 = (s32[128,4]{0,1:T(4,128)S(1)}, s32[128,4]{0,1:T(4,128)}, u32[]{:S(2)}) copy-start(s32[128,4]{0,1:T(4,128)} %param.20) | copy-start | bytes 6148
  65.9 32.1 %all-to-all-start.2 = ((bf16[8,128,180]{1,2,0:T(8,128)(2,1)}), bf16[8,128,180]{1,2,0:T(8,128)(2,1)S(1)}, u32[]{:S(2)}, u32[]{:S(2)}) async-start(bf16[8,128,180]{1,2,0:T(8,128)(2,1)} %copy.140), calls=%async_computation.2 | async-start | bytes 753664 | tf_op jit(solution)/shard_map/all_to_all | solution.py:159
  76.9 121.6 %all-gather.6.cloned.1.call-start = ((), (), s32[]{:S(2)}) async-start(), calls=%async_computation.8 | async-start | bytes 2119680 | tf_op jit(solution)/shard_map/all_gather | solution.py:200
  98.1 0.6 copy-start.2
  141.0 84.4 %all-gather.8.cloned.1.call-start = ((), (), s32[]{:S(2)}) async-start(), calls=%async_computation.9 | async-start | bytes 5591040 | tf_op jit(solution)/shard_map/all_gather | solution.py:201
  201.5 125.5 %reduce-scatter.5.cloned.1.call-start = ((), (), s32[]{:S(2)}) async-start(), calls=%async_computation.10 | async-start | bytes 1177600
  225.4 3.1 copy-start.1
  276.4 77.3 %copy-start.7 = (f32[128,4]{0,1:T(4,128)S(1)}, f32[128,4]{0,1:T(4,128)}, u32[]{:S(2)}) copy-start(f32[128,4]{0,1:T(4,128)} %param.21) | copy-start | bytes 6148
  279.5 104.0 %copy-start.3 = (f32[128,180]{0,1:T(8,128)S(1)}, f32[128,180]{0,1:T(8,128)}, u32[]{:S(2)}) copy-start(f32[128,180]{0,1:T(8,128)} %copy-done.2) | copy-start | bytes 276484
  328.9 51.8 %all-to-all-start.6 = ((bf16[32,20,180]{2,1,0:T(8,128)(2,1)}), bf16[32,20,180]{2,1,0:T(8,128)(2,1)S(1)}, u32[]{:S(2)}, u32[]{:S(2)}) async-start(bf16[32,20,180]{2,1,0:T(8,128)(2,1)} %reshape_squeeze.3), calls=%async_computation.6 | async-start | bytes 786432 | tf_op jit(solution)/shard_map/all_to_all | solution.py:231
Sparse Core Ops, SparseCore 0:
  141.1 57.2 all-gather.5
  201.6 23.7 all-gather.7
  279.6 47.3 reduce-scatter.4

commit v10 on v7

--- a/solution.py
+++ b/solution.py
@@ -197,8 +197,10 @@
         concat_axis=0,
         tiled=True,
     ).reshape(bucket_rows, send_width)
-    gathered = lax.all_gather(received, ZL, axis=0, tiled=False)
+    gathered = lax.all_gather(received, "zll", axis=0, tiled=False)
+    gathered = lax.all_gather(gathered, "zlh", axis=0, tiled=False)
     gathered = lax.all_gather(gathered, "c", axis=0, tiled=False)
+    gathered = gathered.reshape(c_count, zl_count, bucket_rows, send_width)
     row_squares = jnp.sum(
         gathered[:, :, :, col_width].astype(jnp.float32)
         + gathered[:, :, :, col_width + 1].astype(jnp.float32),

time: 380 us -> 403 us (1.061)
  blocking collectives: 146 us -> 157 us
  waiting for transfers between devices: 123 us -> 134 us
    all_gather x1, waiting for transfers between devices: 66.4 us -> 81.2 us  [per_device(): gathered = lax.all_gather(gathered, 'zlh', axis=0, tiled=False)]
    all_gather x0 -> x1, blocking collectives: none -> 11.1 us  [per_device(): gathered = lax.all_gather(received, 'zll', axis=0, tiled=False)]
where the time goes in v10:
time: 403 us; the launch traced here: 402 us
  blocking collectives  157 us (39%)
  waiting for transfers between devices  134 us (33%)
  local copies, waits for them, and re-layouts  44.3 us (11%)
  starting transfers between devices  27.1 us (7%)
  other arithmetic  15.6 us (4%)
  between operations  13.9 us (3%)
  matrix products  9.23 us (2%)
    all_gather x1, waiting for transfers between devices, per_device(): gathered = lax.all_gather(gathered, 'zlh', axis=0, tiled=False)  81.2 us
    all_to_all x1, blocking collectives, per_device(): partial_value = lax.all_to_all(partial_value, 'zlh', 0, 0, tiled=True)  52.9 us
    all_to_all x1, blocking collectives, per_device(): lax.all_to_all(send_rows.reshape(ctx_count, exp_local * capacity, send_wi...  28 us
    all_to_all x1, blocking collectives, per_device(): lax.all_to_all(partial_value.transpose(1, 0, 2, 3), 'zll', 0, 0, tiled=True)  25.3 us
    all_to_all x1, waiting for transfers between devices, per_device(): lax.all_to_all(expert_cols.reshape(ctx_count, capacity, col_width), CTX,...  23.3 us
    all_to_all x1, waiting for transfers between devices, per_device(): lax.all_to_all(head_part, ZL, split_axis=0, concat_axis=0, tiled=True)  16.6 us
    all_gather x1, blocking collectives, per_device(): block_part = lax.all_gather(key_value, 'zh', axis=0, tiled=False)  15 us
    all_gather x1, blocking collectives, per_device(): block_part = lax.all_gather(block_part, 'y', axis=0, tiled=False)  13.1 us
  transfers between devices with their start and end apart: 5, of which 5 were waited for; matrix products, arithmetic and copies ran while one was open for 6% of the time, Pallas kernels for 0%

profile of v10, /device:TPU:64, one launch (start us, length us, event | category | flops | bytes accessed | tf_op | source)
XLA Modules:
  0.0 401.9 jit_solution(3239185662968899080)
XLA Ops:
  8.5 15.0 %all-gather = bf16[256,128]{0,1:T(8,128)(2,1)S(1)} all-gather(bf16[128,128]{0,1:T(8,128)(2,1)S(1)} %pad_maximum_fusion.1), channel_id=2, replica_groups=mesh['zh'=2,'y'=4,'x'=4,'zlh'=4,'zll'=2,'c'=2] {'zh'}, dimensions={0}, use_global_device_ids=true | all-gather | bytes 98304 | tf_op jit(solution)/shard_map/all_gather | solution.py:113
  23.7 13.1 %all-gather.1 = bf16[8,128,128]{2,1,0:T(8,128)(2,1)S(1)} all-gather(bf16[2,128,128]{2,1,0:T(8,128)(2,1)S(1)} %bitcast.94), channel_id=3, replica_groups=mesh['zh'=2,'y'=4,'x'=4,'zlh'=4,'zll'=2,'c'=2] {'y'}, dimensions={0}, use_global_device_ids=true | all-gather | bytes 327680 | tf_op jit(solution)/shard_map/all_gather | solution.py:114
  38.5 4.3 %all-to-all-start = ((bf16[4,4,2,128,128]{3,2,1,4,0:T(2,128)(2,1)}), bf16[4,4,2,128,128]{3,2,1,4,0:T(2,128)(2,1)S(1)}, u32[]{:S(2)}, u32[]{:S(2)}) async-start(bf16[4,4,2,128,128]{3,2,1,4,0:T(2,128)(2,1)} %broadcast_in_dim.19), calls=%async_computation | async-start | bytes 2097152 | tf_op jit(solution)/shard_map/all_to_all | solution.py:115
  45.2 8.5 %all-to-all-done = bf16[4,4,2,128,128]{3,2,1,4,0:T(2,128)(2,1)S(1)} async-done(((bf16[4,4,2,128,128]{3,2,1,4,0:T(2,128)(2,1)}), bf16[4,4,2,128,128]{3,2,1,4,0:T(2,128)(2,1)S(1)}, u32[]{:S(2)}, u32[]{:S(2)}) %all-to-all-start) | async-done | bytes 1048608 | tf_op jit(solution)/shard_map/all_to_all | solution.py:115
  56.9 2.1 fusion.21
  59.6 4.3 %all_to_all.40 = bf16[2,8,128,180]{2,1,3,0:T(8,128)(2,1)S(1)} all-to-all(bf16[2,8,128,180]{2,1,3,0:T(8,128)(2,1)S(1)} %copy.90), channel_id=1, replica_groups=mesh['zh'=2,'y'=4,'x'=4,'zlh'=4,'zll'=2,'c'=2] {'c'}, dimensions={0} | all-to-all | bytes 1474560 | tf_op jit(solution)/shard_map/all_to_all | solution.py:157
  65.1 11.3 %all-to-all-start.2 = ((bf16[8,128,180]{1,2,0:T(8,128)(2,1)}), bf16[8,128,180]{1,2,0:T(8,128)(2,1)S(1)}, u32[]{:S(2)}, u32[]{:S(2)}) async-start(bf16[8,128,180]{1,2,0:T(8,128)(2,1)} %copy.116), calls=%async_computation.2 | async-start | bytes 753664 | tf_op jit(solution)/shard_map/all_to_all | solution.py:159
  79.5 16.6 %all-to-all-done.2 = bf16[8,128,180]{1,2,0:T(8,128)(2,1)S(1)} async-done(((bf16[8,128,180]{1,2,0:T(8,128)(2,1)}), bf16[8,128,180]{1,2,0:T(8,128)(2,1)S(1)}, u32[]{:S(2)}, u32[]{:S(2)}) %all-to-all-start.2) | async-done | bytes 368672 | tf_op jit(solution)/shard_map/all_to_all | solution.py:159
  98.1 2.4 scatter_custom_fusion
  100.6 28.0 %all_to_all.41 = bf16[32,20,182]{2,1,0:T(8,128)(2,1)S(1)} all-to-all(bf16[32,20,182]{2,1,0:T(8,128)(2,1)S(1)} %reshape.378), channel_id=1, replica_groups=mesh['zh'=2,'y'=4,'x'=4,'zlh'=4,'zll'=2,'c'=2] {'zh','y','x'}, dimensions={0} | all-to-all | bytes 465920 | tf_op jit(solution)/shard_map/all_to_all | solution.py:193
  129.0 11.1 %all_gather.31 = bf16[2,640,182]{1,2,0:T(8,128)(2,1)} all-gather(bf16[1,640,182]{1,2,0:T(8,128)(2,1)S(1)} %copy.99), channel_id=1, replica_groups=mesh['zh'=2,'y'=4,'x'=4,'zlh'=4,'zll'=2,'c'=2] {'zll'}, dimensions={0}, use_global_device_ids=true | all-gather | bytes 698880 | tf_op jit(solution)/shard_map/all_gather | solution.py:200
  140.1 81.2 %all-gather.7.cloned.1.call-done = bf16[8,640,182]{1,2,0:T(8,128)(2,1)} async-done(((bf16[2,640,182]{1,2,0:T(8,128)(2,1)}), bf16[8,640,182]{1,2,0:T(8,128)(2,1)}) %all-gather.7.cloned.1.call-update) | async-done | bytes 1863696 | tf_op jit(solution)/shard_map/all_gather | solution.py:201
  221.3 4.2 %copy.100 = bf16[4,2,640,182]{2,1,3,0:T(2,128)(2,1)} copy(bf16[4,2,640,182]{2,3,1,0:T(8,128)(2,1)} %bitcast.92) | data formatting | bytes 3727360 | tf_op jit(solution)/shard_map/all_gather | solution.py:201
  227.4 9.7 %reshape.380 = bf16[8,2,180,360]{2,1,0,3:T(2,128)(2,1)} reshape(bf16[1,2880,2,180]{1,3,2,0:T(8,128)(2,1)S(1)} %copy.102) | data formatting | bytes 4147200 | tf_op jit(solution)/shard_map/reshape | solution.py:210
  237.1 6.6 %reshape.382 = bf16[180,4,2,2,180]{4,3,2,1,0:T(2,128)(2,1)S(1)} reshape(bf16[1,180,2880]{2,1,0:T(8,128)(2,1)} %param.23) | data formatting | bytes 2073600 | tf_op jit(solution)/shard_map/reshape | solution.py:224
  243.8 4.7 %all-gather.9.cloned.1.call-done = bf16[8,2,640,182]{2,1,3,0:T(2,128)(2,1)} async-done(((bf16[4,2,640,182]{2,1,3,0:T(2,128)(2,1)}), bf16[8,2,640,182]{2,1,3,0:T(2,128)(2,1)}) %all-gather.9.cloned.1.call-update) | async-done | bytes 3727376 | tf_op jit(solution)/shard_map/all_gather | solution.py:202
  248.4 2.7 copy.101
  251.4 4.1 %fusion.14 = f32[640,360]{0,1:T(8,128)} fusion(bf16[8,2,180,360]{2,1,0,3:T(2,128)(2,1)S(1)} %copy-done.1, bf16[2,8,640,182]{2,3,1,0:T(8,128)(2,1)S(1)} %bitcast.90, f32[640]{0:T(1024)S(1)} %add_rsqrt_fusion), kind=kOutput, calls=%fused_computation.17 | convolution fusion | flops 1327334400 | bytes 6725120 | tf_op jit(solution)/shard_map/czrk,zckf->rf/dot_general | solution.py:211
  260.5 7.7 %all_to_all.42 = bf16[2,4,2,640,180]{3,1,4,2,0:T(4,128)(2,1)} all-to-all(bf16[2,4,2,640,180]{3,1,4,2,0:T(4,128)(2,1)S(1)} %copy.105), channel_id=1, replica_groups=mesh['zh'=2,'y'=4,'x'=4,'zlh'=4,'zll'=2,'c'=2] {'c'}, dimensions={0} | all-to-all | bytes 7372800 | tf_op jit(solution)/shard_map/all_to_all | solution.py:228
  268.3 5.0 %reduce_sum.111 = bf16[4,2,640,180]{2,0,3,1:T(4,128)(2,1)S(1)} reduce(bf16[2,4,2,640,180]{3,1,4,2,0:T(4,128)(2,1)} %all_to_all.42, bf16[]{:T(256)} %constant.90.clone.1), dimensions={0}, to_apply=%region_10.11 | reduce | flops 921600 | bytes 5529602 | tf_op jit(solution)/shard_map/reduce_sum | solution.py:229
  274.3 25.3 %all_to_all.43 = bf16[2,4,640,180]{2,1,3,0:T(4,128)(2,1)S(1)} all-to-all(bf16[2,4,640,180]{2,1,3,0:T(4,128)(2,1)S(1)} %copy.107), channel_id=1, replica_groups=mesh['zh'=2,'y'=4,'x'=4,'zlh'=4,'zll'=2,'c'=2] {'zll'}, dimensions={0} | all-to-all | bytes 3686400 | tf_op jit(solution)/shard_map/all_to_all | solution.py:230
  301.7 52.9 %all_to_all.44 = bf16[4,640,180]{1,2,0:T(8,128)(2,1)S(1)} all-to-all(bf16[4,640,180]{1,2,0:T(8,128)(2,1)S(1)} %copy.108), channel_id=1, replica_groups=mesh['zh'=2,'y'=4,'x'=4,'zlh'=4,'zll'=2,'c'=2] {'zlh'}, dimensions={0} | all-to-all | bytes 1843200 | tf_op jit(solution)/shard_map/all_to_all | solution.py:232
  355.8 11.5 %all-to-all-start.7 = ((bf16[32,20,180]{2,1,0:T(8,128)(2,1)}), bf16[32,20,180]{2,1,0:T(8,128)(2,1)S(1)}, u32[]{:S(2)}, u32[]{:S(2)}) async-start(bf16[32,20,180]{2,1,0:T(8,128)(2,1)} %reshape.383), calls=%async_computation.7 | async-start | bytes 786432 | tf_op jit(solution)/shard_map/all_to_all | solution.py:234
  367.6 23.3 %all-to-all-done.7 = bf16[32,20,180]{2,1,0:T(8,128)(2,1)S(1)} async-done(((bf16[32,20,180]{2,1,0:T(8,128)(2,1)}), bf16[32,20,180]{2,1,0:T(8,128)(2,1)S(1)}, u32[]{:S(2)}, u32[]{:S(2)}) %all-to-all-start.7) | async-done | bytes 230432 | tf_op jit(solution)/shard_map/all_to_all | solution.py:234
  (103 shorter events, 32.3 us)
Async XLA Ops:
  6.5 52.4 %copy-start = (bf16[128,2880]{0,1:T(8,128)(2,1)S(1)}, bf16[128,2880]{0,1:T(8,128)(2,1)}, u32[]{:S(2)}) copy-start(bf16[128,2880]{0,1:T(8,128)(2,1)} %param.18) | copy-start | bytes 2211844
  6.5 36.3 %copy-start.6 = (f32[32]{0:T(128)S(1)}, f32[32]{0:T(128)}, u32[]{:S(2)}) copy-start(f32[32]{0:T(128)} %constant.97.clone) | copy-start | bytes 388
  6.5 36.4 %copy-start.4 = (bf16[128,128]{1,0:T(8,128)(2,1)S(1)}, bf16[128,128]{1,0:T(8,128)(2,1)}, u32[]{:S(2)}) copy-start(bf16[128,128]{1,0:T(8,128)(2,1)} %param.14) | copy-start | bytes 98308
  38.5 15.2 %all-to-all-start = ((bf16[4,4,2,128,128]{3,2,1,4,0:T(2,128)(2,1)}), bf16[4,4,2,128,128]{3,2,1,4,0:T(2,128)(2,1)S(1)}, u32[]{:S(2)}, u32[]{:S(2)}) async-start(bf16[4,4,2,128,128]{3,2,1,4,0:T(2,128)(2,1)} %broadcast_in_dim.19), calls=%async_computation | async-start | bytes 2097152 | tf_op jit(solution)/shard_map/all_to_all | solution.py:115
  54.4 1.7 copy-start.8
  59.3 17.1 %copy-start.5 = (s32[128,4]{0,1:T(4,128)S(1)}, s32[128,4]{0,1:T(4,128)}, u32[]{:S(2)}) copy-start(s32[128,4]{0,1:T(4,128)} %param.20) | copy-start | bytes 6148
  65.1 31.1 %all-to-all-start.2 = ((bf16[8,128,180]{1,2,0:T(8,128)(2,1)}), bf16[8,128,180]{1,2,0:T(8,128)(2,1)S(1)}, u32[]{:S(2)}, u32[]{:S(2)}) async-start(bf16[8,128,180]{1,2,0:T(8,128)(2,1)} %copy.116), calls=%async_computation.2 | async-start | bytes 753664 | tf_op jit(solution)/shard_map/all_to_all | solution.py:159
  76.4 144.9 %all-gather.7.cloned.1.call-start = ((), (), s32[]{:S(2)}) async-start(), calls=%async_computation.8 | async-start | bytes 2355200 | tf_op jit(solution)/shard_map/all_gather | solution.py:201
  96.2 0.6 copy-start.2
  140.1 108.4 %all-gather.9.cloned.1.call-start = ((), (), s32[]{:S(2)}) async-start(), calls=%async_computation.9 | async-start | bytes 5591040 | tf_op jit(solution)/shard_map/all_gather | solution.py:202
  248.4 3.0 copy-start.1
  301.6 65.9 %copy-start.7 = (f32[128,4]{0,1:T(4,128)S(1)}, f32[128,4]{0,1:T(4,128)}, u32[]{:S(2)}) copy-start(f32[128,4]{0,1:T(4,128)} %param.21) | copy-start | bytes 6148
  354.8 38.9 %copy-start.3 = (f32[128,180]{0,1:T(8,128)S(1)}, f32[128,180]{0,1:T(8,128)}, u32[]{:S(2)}) copy-start(f32[128,180]{0,1:T(8,128)} %copy-done.2) | copy-start | bytes 276484
  355.8 35.1 %all-to-all-start.7 = ((bf16[32,20,180]{2,1,0:T(8,128)(2,1)}), bf16[32,20,180]{2,1,0:T(8,128)(2,1)S(1)}, u32[]{:S(2)}, u32[]{:S(2)}) async-start(bf16[32,20,180]{2,1,0:T(8,128)(2,1)} %reshape.383), calls=%async_computation.7 | async-start | bytes 786432 | tf_op jit(solution)/shard_map/all_to_all | solution.py:234
Sparse Core Ops, SparseCore 0:
  140.2 81.0 all-gather.6
  225.7 22.7 all-gather.8

commit v11 on v7

--- a/solution.py
+++ b/solution.py
@@ -111,7 +111,13 @@
     key_value = jnp.concatenate([key_rot, value_block], axis=1)
     score_scale = 1.0 / math.sqrt(HEAD_SIZE)
     block_part = lax.all_gather(key_value, "zh", axis=0, tiled=False)
-    block_part = lax.all_gather(block_part, "y", axis=0, tiled=False)
+    block_part = lax.all_to_all(
+        jnp.broadcast_to(block_part[None], (lax.axis_size("y"),) + block_part.shape),
+        "y",
+        0,
+        0,
+        tiled=True,
+    )
     block_part = lax.all_to_all(
         jnp.broadcast_to(block_part[None], (lax.axis_size("x"),) + block_part.shape),
         "x",

time: 380 us -> 378 us (level)
  blocking collectives: 146 us -> 132 us
  waiting for transfers between devices: 123 us -> 130 us
  starting transfers between devices: 27.1 us -> 31.5 us
    all_gather x1 -> x0, blocking collectives: 13.1 us -> none  [per_device(): block_part = lax.all_gather(block_part, 'y', axis=0, tiled=False)]
    all_to_all x0 -> x1, waiting for transfers between devices: none -> 4.81 us  [per_device(): lax.all_to_all(jnp.broadcast_to(block_part[None], (lax.axis_size('y'),) +...]
    all_to_all x0 -> x1, starting transfers between devices: none -> 4.46 us  [per_device(): lax.all_to_all(jnp.broadcast_to(block_part[None], (lax.axis_size('y'),) +...]
  transfers between devices with their start and end apart: 5 -> 6, of which waited for: 5 -> 6; matrix products, arithmetic and copies ran while one was open for 6% -> 7% of each run, Pallas kernels for 0% -> 0%
where the time goes in v11:
time: 378 us; the launch traced here: 377 us
  blocking collectives  132 us (35%)
  waiting for transfers between devices  130 us (34%)
  local copies, waits for them, and re-layouts  45.2 us (12%)
  starting transfers between devices  31.5 us (8%)
  other arithmetic  16.2 us (4%)
  between operations  13.9 us (4%)
  matrix products  9.23 us (2%)
    all_gather x1, waiting for transfers between devices, per_device(): gathered = lax.all_gather(received, ZL, axis=0, tiled=False)  66.4 us
    all_to_all x1, blocking collectives, per_device(): partial_value = lax.all_to_all(partial_value, 'zlh', 0, 0, tiled=True)  52.8 us
    all_to_all x1, blocking collectives, per_device(): lax.all_to_all(send_rows.reshape(ctx_count, exp_local * capacity, send_wi...  26.7 us
    all_to_all x1, blocking collectives, per_device(): lax.all_to_all(partial_value.transpose(1, 0, 2, 3), 'zll', 0, 0, tiled=True)  25.3 us
    all_to_all x1, waiting for transfers between devices, per_device(): lax.all_to_all(expert_cols.reshape(ctx_count, capacity, col_width), CTX,...  23.3 us
    all_to_all x1, waiting for transfers between devices, per_device(): lax.all_to_all(head_part, ZL, split_axis=0, concat_axis=0, tiled=True)  16.6 us
    all_gather x1, blocking collectives, per_device(): block_part = lax.all_gather(key_value, 'zh', axis=0, tiled=False)  15 us
    all_to_all x1, starting transfers between devices, per_device(): lax.all_to_all(expert_cols.reshape(ctx_count, capacity, col_width), CTX,...  11.5 us
  transfers between devices with their start and end apart: 6, of which 6 were waited for; matrix products, arithmetic and copies ran while one was open for 7% of the time, Pallas kernels for 0%

profile of v11, /device:TPU:64, one launch (start us, length us, event | category | flops | bytes accessed | tf_op | source)
XLA Modules:
  0.0 377.4 jit_solution(14100443398479714751)
XLA Ops:
  8.5 15.0 %all-gather = bf16[256,128]{0,1:T(8,128)(2,1)S(1)} all-gather(bf16[128,128]{0,1:T(8,128)(2,1)S(1)} %pad_maximum_fusion.1), channel_id=2, replica_groups=mesh['zh'=2,'y'=4,'x'=4,'zlh'=4,'zll'=2,'c'=2] {'zh'}, dimensions={0}, use_global_device_ids=true | all-gather | bytes 98304 | tf_op jit(solution)/shard_map/all_gather | solution.py:113
  24.4 4.5 %all-to-all-start = ((bf16[4,2,128,128]{2,1,3,0:T(2,128)(2,1)}), bf16[4,2,128,128]{2,1,3,0:T(2,128)(2,1)S(1)}, u32[]{:S(2)}, u32[]{:S(2)}) async-start(bf16[4,2,128,128]{2,1,3,0:T(2,128)(2,1)} %broadcast_in_dim.21), calls=%async_computation | async-start | bytes 524288 | tf_op jit(solution)/shard_map/all_to_all | solution.py:114
  30.8 4.8 %all-to-all-done = bf16[4,2,128,128]{2,1,3,0:T(2,128)(2,1)S(1)} async-done(((bf16[4,2,128,128]{2,1,3,0:T(2,128)(2,1)}), bf16[4,2,128,128]{2,1,3,0:T(2,128)(2,1)S(1)}, u32[]{:S(2)}, u32[]{:S(2)}) %all-to-all-start) | async-done | bytes 262176 | tf_op jit(solution)/shard_map/all_to_all | solution.py:114
  37.3 4.3 %all-to-all-start.1 = ((bf16[4,4,2,128,128]{3,2,1,4,0:T(2,128)(2,1)}), bf16[4,4,2,128,128]{3,2,1,4,0:T(2,128)(2,1)S(1)}, u32[]{:S(2)}, u32[]{:S(2)}) async-start(bf16[4,4,2,128,128]{3,2,1,4,0:T(2,128)(2,1)} %broadcast_in_dim.22), calls=%async_computation.1 | async-start | bytes 2097152 | tf_op jit(solution)/shard_map/all_to_all | solution.py:121
  43.4 10.6 %all-to-all-done.1 = bf16[4,4,2,128,128]{3,2,1,4,0:T(2,128)(2,1)S(1)} async-done(((bf16[4,4,2,128,128]{3,2,1,4,0:T(2,128)(2,1)}), bf16[4,4,2,128,128]{3,2,1,4,0:T(2,128)(2,1)S(1)}, u32[]{:S(2)}, u32[]{:S(2)}) %all-to-all-start.1) | async-done | bytes 1048608 | tf_op jit(solution)/shard_map/all_to_all | solution.py:121
  57.2 2.1 fusion.21
  60.0 4.3 %all_to_all.45 = bf16[2,8,128,180]{2,1,3,0:T(8,128)(2,1)S(1)} all-to-all(bf16[2,8,128,180]{2,1,3,0:T(8,128)(2,1)S(1)} %copy.91), channel_id=1, replica_groups=mesh['zh'=2,'y'=4,'x'=4,'zlh'=4,'zll'=2,'c'=2] {'c'}, dimensions={0} | all-to-all | bytes 1474560 | tf_op jit(solution)/shard_map/all_to_all | solution.py:163
  65.4 11.2 %all-to-all-start.3 = ((bf16[8,128,180]{1,2,0:T(8,128)(2,1)}), bf16[8,128,180]{1,2,0:T(8,128)(2,1)S(1)}, u32[]{:S(2)}, u32[]{:S(2)}) async-start(bf16[8,128,180]{1,2,0:T(8,128)(2,1)} %copy.116), calls=%async_computation.3 | async-start | bytes 753664 | tf_op jit(solution)/shard_map/all_to_all | solution.py:165
  79.7 16.6 %all-to-all-done.3 = bf16[8,128,180]{1,2,0:T(8,128)(2,1)S(1)} async-done(((bf16[8,128,180]{1,2,0:T(8,128)(2,1)}), bf16[8,128,180]{1,2,0:T(8,128)(2,1)S(1)}, u32[]{:S(2)}, u32[]{:S(2)}) %all-to-all-start.3) | async-done | bytes 368672 | tf_op jit(solution)/shard_map/all_to_all | solution.py:165
  98.3 2.4 scatter_custom_fusion
  100.8 26.7 %all_to_all.46 = bf16[32,20,182]{2,1,0:T(8,128)(2,1)S(1)} all-to-all(bf16[32,20,182]{2,1,0:T(8,128)(2,1)S(1)} %reshape.376), channel_id=1, replica_groups=mesh['zh'=2,'y'=4,'x'=4,'zlh'=4,'zll'=2,'c'=2] {'zh','y','x'}, dimensions={0} | all-to-all | bytes 465920 | tf_op jit(solution)/shard_map/all_to_all | solution.py:199
  128.6 66.4 %all-gather.5.cloned.1.call-done = bf16[8,640,182]{1,2,0:T(8,128)(2,1)} async-done(((bf16[1,640,182]{1,2,0:T(8,128)(2,1)}), bf16[8,640,182]{1,2,0:T(8,128)(2,1)}) %all-gather.5.cloned.1.call-update) | async-done | bytes 1863696 | tf_op jit(solution)/shard_map/all_gather | solution.py:206
  195.0 3.0 copy.101
  199.8 9.7 %reshape.377 = bf16[8,2,180,360]{2,1,0,3:T(2,128)(2,1)} reshape(bf16[1,2880,2,180]{1,3,2,0:T(8,128)(2,1)S(1)} %copy.103) | data formatting | bytes 4147200 | tf_op jit(solution)/shard_map/reshape | solution.py:214
  209.5 6.4 %reshape.379 = bf16[180,4,2,2,180]{4,3,2,1,0:T(2,128)(2,1)S(1)} reshape(bf16[1,180,2880]{2,1,0:T(8,128)(2,1)} %param.23) | data formatting | bytes 2073600 | tf_op jit(solution)/shard_map/reshape | solution.py:228
  216.0 7.9 %all-gather.7.cloned.1.call-done = bf16[16,640,182]{1,0,2:T(8,128)(2,1)} async-done(((bf16[8,640,182]{1,0,2:T(8,128)(2,1)}), bf16[16,640,182]{1,0,2:T(8,128)(2,1)}) %all-gather.7.cloned.1.call-update) | async-done | bytes 3727376 | tf_op jit(solution)/shard_map/all_gather | solution.py:207
  223.9 3.0 copy.102
  227.0 4.1 %fusion.14 = f32[640,360]{0,1:T(8,128)} fusion(bf16[8,2,180,360]{2,1,0,3:T(2,128)(2,1)S(1)} %copy-done.1, bf16[2,8,640,182]{2,3,1,0:T(8,128)(2,1)S(1)} %bitcast.89, f32[640]{0:T(1024)S(1)} %add_rsqrt_fusion), kind=kOutput, calls=%fused_computation.17 | convolution fusion | flops 1327334400 | bytes 6725120 | tf_op jit(solution)/shard_map/czrk,zckf->rf/dot_general | solution.py:215
  236.1 7.7 %all_to_all.47 = bf16[2,4,2,640,180]{3,1,4,2,0:T(4,128)(2,1)} all-to-all(bf16[2,4,2,640,180]{3,1,4,2,0:T(4,128)(2,1)S(1)} %copy.106), channel_id=1, replica_groups=mesh['zh'=2,'y'=4,'x'=4,'zlh'=4,'zll'=2,'c'=2] {'c'}, dimensions={0} | all-to-all | bytes 7372800 | tf_op jit(solution)/shard_map/all_to_all | solution.py:232
  243.8 5.0 %reduce_sum.111 = bf16[4,2,640,180]{2,0,3,1:T(4,128)(2,1)S(1)} reduce(bf16[2,4,2,640,180]{3,1,4,2,0:T(4,128)(2,1)} %all_to_all.47, bf16[]{:T(256)} %constant.90.clone.1), dimensions={0}, to_apply=%region_10.11 | reduce | flops 921600 | bytes 5529602 | tf_op jit(solution)/shard_map/reduce_sum | solution.py:233
  249.8 25.3 %all_to_all.48 = bf16[2,4,640,180]{2,1,3,0:T(4,128)(2,1)S(1)} all-to-all(bf16[2,4,640,180]{2,1,3,0:T(4,128)(2,1)S(1)} %copy.108), channel_id=1, replica_groups=mesh['zh'=2,'y'=4,'x'=4,'zlh'=4,'zll'=2,'c'=2] {'zll'}, dimensions={0} | all-to-all | bytes 3686400 | tf_op jit(solution)/shard_map/all_to_all | solution.py:234
  277.3 52.8 %all_to_all.49 = bf16[4,640,180]{1,2,0:T(8,128)(2,1)S(1)} all-to-all(bf16[4,640,180]{1,2,0:T(8,128)(2,1)S(1)} %copy.109), channel_id=1, replica_groups=mesh['zh'=2,'y'=4,'x'=4,'zlh'=4,'zll'=2,'c'=2] {'zlh'}, dimensions={0} | all-to-all | bytes 1843200 | tf_op jit(solution)/shard_map/all_to_all | solution.py:236
  331.3 11.5 %all-to-all-start.8 = ((bf16[32,20,180]{2,1,0:T(8,128)(2,1)}), bf16[32,20,180]{2,1,0:T(8,128)(2,1)S(1)}, u32[]{:S(2)}, u32[]{:S(2)}) async-start(bf16[32,20,180]{2,1,0:T(8,128)(2,1)} %reshape.380), calls=%async_computation.8 | async-start | bytes 786432 | tf_op jit(solution)/shard_map/all_to_all | solution.py:238
  343.1 23.3 %all-to-all-done.8 = bf16[32,20,180]{2,1,0:T(8,128)(2,1)S(1)} async-done(((bf16[32,20,180]{2,1,0:T(8,128)(2,1)}), bf16[32,20,180]{2,1,0:T(8,128)(2,1)S(1)}, u32[]{:S(2)}, u32[]{:S(2)}) %all-to-all-start.8) | async-done | bytes 230432 | tf_op jit(solution)/shard_map/all_to_all | solution.py:238
  (100 shorter events, 34.9 us)
Async XLA Ops:
  6.5 52.7 %copy-start = (bf16[128,2880]{0,1:T(8,128)(2,1)S(1)}, bf16[128,2880]{0,1:T(8,128)(2,1)}, u32[]{:S(2)}) copy-start(bf16[128,2880]{0,1:T(8,128)(2,1)} %param.18) | copy-start | bytes 2211844
  24.4 11.1 %all-to-all-start = ((bf16[4,2,128,128]{2,1,3,0:T(2,128)(2,1)}), bf16[4,2,128,128]{2,1,3,0:T(2,128)(2,1)S(1)}, u32[]{:S(2)}, u32[]{:S(2)}) async-start(bf16[4,2,128,128]{2,1,3,0:T(2,128)(2,1)} %broadcast_in_dim.21), calls=%async_computation | async-start | bytes 524288 | tf_op jit(solution)/shard_map/all_to_all | solution.py:114
  37.3 16.7 %all-to-all-start.1 = ((bf16[4,4,2,128,128]{3,2,1,4,0:T(2,128)(2,1)}), bf16[4,4,2,128,128]{3,2,1,4,0:T(2,128)(2,1)S(1)}, u32[]{:S(2)}, u32[]{:S(2)}) async-start(bf16[4,4,2,128,128]{3,2,1,4,0:T(2,128)(2,1)} %broadcast_in_dim.22), calls=%async_computation.1 | async-start | bytes 2097152 | tf_op jit(solution)/shard_map/all_to_all | solution.py:121
  54.8 1.7 copy-start.6
  59.6 17.0 %copy-start.4 = (s32[128,4]{0,1:T(4,128)S(1)}, s32[128,4]{0,1:T(4,128)}, u32[]{:S(2)}) copy-start(s32[128,4]{0,1:T(4,128)} %param.20) | copy-start | bytes 6148
  65.4 30.9 %all-to-all-start.3 = ((bf16[8,128,180]{1,2,0:T(8,128)(2,1)}), bf16[8,128,180]{1,2,0:T(8,128)(2,1)S(1)}, u32[]{:S(2)}, u32[]{:S(2)}) async-start(bf16[8,128,180]{1,2,0:T(8,128)(2,1)} %copy.116), calls=%async_computation.3 | async-start | bytes 753664 | tf_op jit(solution)/shard_map/all_to_all | solution.py:165
  76.6 118.3 %all-gather.5.cloned.1.call-start = ((), (), s32[]{:S(2)}) async-start(), calls=%async_computation.9 | async-start | bytes 2119680 | tf_op jit(solution)/shard_map/all_gather | solution.py:206
  96.4 0.6 copy-start.2
  128.5 95.4 %all-gather.7.cloned.1.call-start = ((), (), s32[]{:S(2)}) async-start(), calls=%async_computation.10 | async-start | bytes 5591040 | tf_op jit(solution)/shard_map/all_gather | solution.py:207
  223.9 3.1 copy-start.1
  277.1 65.9 %copy-start.5 = (f32[128,4]{0,1:T(4,128)S(1)}, f32[128,4]{0,1:T(4,128)}, u32[]{:S(2)}) copy-start(f32[128,4]{0,1:T(4,128)} %param.21) | copy-start | bytes 6148
  330.3 38.9 %copy-start.3 = (f32[128,180]{0,1:T(8,128)S(1)}, f32[128,180]{0,1:T(8,128)}, u32[]{:S(2)}) copy-start(f32[128,180]{0,1:T(8,128)} %copy-done.2) | copy-start | bytes 276484
  331.3 35.1 %all-to-all-start.8 = ((bf16[32,20,180]{2,1,0:T(8,128)(2,1)}), bf16[32,20,180]{2,1,0:T(8,128)(2,1)S(1)}, u32[]{:S(2)}, u32[]{:S(2)}) async-start(bf16[32,20,180]{2,1,0:T(8,128)(2,1)} %reshape.380), calls=%async_computation.8 | async-start | bytes 786432 | tf_op jit(solution)/shard_map/all_to_all | solution.py:238
Sparse Core Ops, SparseCore 0:
  128.6 66.2 all-gather.4
  198.1 25.7 all-gather.6

commit v12 on v11

--- a/solution.py
+++ b/solution.py
@@ -110,7 +110,14 @@
     )
     key_value = jnp.concatenate([key_rot, value_block], axis=1)
     score_scale = 1.0 / math.sqrt(HEAD_SIZE)
-    block_part = lax.all_gather(key_value, "zh", axis=0, tiled=False)
+    partner_value = lax.ppermute(key_value, "zh", [(0, 1), (1, 0)])
+    lower_half = lax.axis_index("zh") == 0
+    block_part = jnp.stack(
+        [
+            jnp.where(lower_half, key_value, partner_value),
+            jnp.where(lower_half, partner_value, key_value),
+        ]
+    )
     block_part = lax.all_to_all(
         jnp.broadcast_to(block_part[None], (lax.axis_size("y"),) + block_part.shape),
         "y",

time: 378 us -> 380 us (level)
  blocking collectives: 132 us -> 117 us
  starting transfers between devices: 31.5 us -> 45 us
    all_gather x1 -> x0, blocking collectives: 15 us -> none  [per_device(): block_part = lax.all_gather(key_value, 'zh', axis=0, tiled=False)]
    ppermute x0 -> x1, starting transfers between devices: none -> 13.9 us  [per_device(): partner_value = lax.ppermute(key_value, 'zh', [(0, 1), (1, 0)])]
  transfers between devices with their start and end apart: 6 -> 7, of which waited for: 6 -> 7; matrix products, arithmetic and copies ran while one was open for 7% -> 7% of each run, Pallas kernels for 0% -> 0%
where the time goes in v12:
time: 380 us; the launch traced here: 379 us
  waiting for transfers between devices  132 us (35%)
  blocking collectives  117 us (31%)
  local copies, waits for them, and re-layouts  45.3 us (12%)
  starting transfers between devices  45 us (12%)
  other arithmetic  16.2 us (4%)
  between operations  13.9 us (4%)
  matrix products  9.23 us (2%)
    all_gather x1, waiting for transfers between devices, per_device(): gathered = lax.all_gather(received, ZL, axis=0, tiled=False)  66.4 us
    all_to_all x1, blocking collectives, per_device(): partial_value = lax.all_to_all(partial_value, 'zlh', 0, 0, tiled=True)  52.8 us
    all_to_all x1, blocking collectives, per_device(): lax.all_to_all(send_rows.reshape(ctx_count, exp_local * capacity, send_wi...  26.6 us
    all_to_all x1, blocking collectives, per_device(): lax.all_to_all(partial_value.transpose(1, 0, 2, 3), 'zll', 0, 0, tiled=True)  25.3 us
    all_to_all x1, waiting for transfers between devices, per_device(): lax.all_to_all(expert_cols.reshape(ctx_count, capacity, col_width), CTX,...  23.3 us
    all_to_all x1, waiting for transfers between devices, per_device(): lax.all_to_all(head_part, ZL, split_axis=0, concat_axis=0, tiled=True)  16.6 us
    ppermute x1, starting transfers between devices, per_device(): partner_value = lax.ppermute(key_value, 'zh', [(0, 1), (1, 0)])  13.9 us
    all_to_all x1, starting transfers between devices, per_device(): lax.all_to_all(expert_cols.reshape(ctx_count, capacity, col_width), CTX,...  11.5 us
  transfers between devices with their start and end apart: 7, of which 7 were waited for; matrix products, arithmetic and copies ran while one was open for 7% of the time, Pallas kernels for 0%

profile of v12, /device:TPU:64, one launch (start us, length us, event | category | flops | bytes accessed | tf_op | source)
XLA Modules:
  0.0 378.7 jit_solution(15294161636583983559)
XLA Ops:
  8.5 13.9 %collective-permute-start = (bf16[128,128]{0,1:T(8,128)(2,1)S(1)}, bf16[128,128]{0,1:T(8,128)(2,1)S(1)}, u32[]{:S(2)}, u32[]{:S(2)}) collective-permute-start(bf16[128,128]{0,1:T(8,128)(2,1)S(1)} %pad_maximum_fusion.2), channel_id=1, source_target_pairs={{0,256},{256,0},{1,257},{257,1},{2,258},{258,2},{3,259},{259,3},{4... | collective-permute-start | bytes 98312 | tf_op jit(solution)/shard_map/ppermute | solution.py:113
  25.7 4.5 %all-to-all-start = ((bf16[4,2,128,128]{2,1,3,0:T(2,128)(2,1)}), bf16[4,2,128,128]{2,1,3,0:T(2,128)(2,1)S(1)}, u32[]{:S(2)}, u32[]{:S(2)}) async-start(bf16[4,2,128,128]{2,1,3,0:T(2,128)(2,1)} %broadcast_in_dim.21), calls=%async_computation | async-start | bytes 524288 | tf_op jit(solution)/shard_map/all_to_all | solution.py:121
  30.3 6.6 %all-to-all-done = bf16[4,2,128,128]{2,1,3,0:T(2,128)(2,1)S(1)} async-done(((bf16[4,2,128,128]{2,1,3,0:T(2,128)(2,1)}), bf16[4,2,128,128]{2,1,3,0:T(2,128)(2,1)S(1)}, u32[]{:S(2)}, u32[]{:S(2)}) %all-to-all-start) | async-done | bytes 262176 | tf_op jit(solution)/shard_map/all_to_all | solution.py:121
  38.6 4.3 %all-to-all-start.1 = ((bf16[4,4,2,128,128]{3,2,1,4,0:T(2,128)(2,1)}), bf16[4,4,2,128,128]{3,2,1,4,0:T(2,128)(2,1)S(1)}, u32[]{:S(2)}, u32[]{:S(2)}) async-start(bf16[4,4,2,128,128]{3,2,1,4,0:T(2,128)(2,1)} %broadcast_in_dim.22), calls=%async_computation.1 | async-start | bytes 2097152 | tf_op jit(solution)/shard_map/all_to_all | solution.py:128
  44.7 11.0 %all-to-all-done.1 = bf16[4,4,2,128,128]{3,2,1,4,0:T(2,128)(2,1)S(1)} async-done(((bf16[4,4,2,128,128]{3,2,1,4,0:T(2,128)(2,1)}), bf16[4,4,2,128,128]{3,2,1,4,0:T(2,128)(2,1)S(1)}, u32[]{:S(2)}, u32[]{:S(2)}) %all-to-all-start.1) | async-done | bytes 1048608 | tf_op jit(solution)/shard_map/all_to_all | solution.py:128
  58.9 2.1 fusion.21
  61.7 4.3 %all_to_all.45 = bf16[2,8,128,180]{2,1,3,0:T(8,128)(2,1)S(1)} all-to-all(bf16[2,8,128,180]{2,1,3,0:T(8,128)(2,1)S(1)} %copy.92), channel_id=1, replica_groups=mesh['zh'=2,'y'=4,'x'=4,'zlh'=4,'zll'=2,'c'=2] {'c'}, dimensions={0} | all-to-all | bytes 1474560 | tf_op jit(solution)/shard_map/all_to_all | solution.py:170
  67.1 10.8 %all-to-all-start.3 = ((bf16[8,128,180]{1,2,0:T(8,128)(2,1)}), bf16[8,128,180]{1,2,0:T(8,128)(2,1)S(1)}, u32[]{:S(2)}, u32[]{:S(2)}) async-start(bf16[8,128,180]{1,2,0:T(8,128)(2,1)} %copy.117), calls=%async_computation.3 | async-start | bytes 753664 | tf_op jit(solution)/shard_map/all_to_all | solution.py:172
  81.1 16.6 %all-to-all-done.3 = bf16[8,128,180]{1,2,0:T(8,128)(2,1)S(1)} async-done(((bf16[8,128,180]{1,2,0:T(8,128)(2,1)}), bf16[8,128,180]{1,2,0:T(8,128)(2,1)S(1)}, u32[]{:S(2)}, u32[]{:S(2)}) %all-to-all-start.3) | async-done | bytes 368672 | tf_op jit(solution)/shard_map/all_to_all | solution.py:172
  99.7 2.4 scatter_custom_fusion
  102.2 26.6 %all_to_all.46 = bf16[32,20,182]{2,1,0:T(8,128)(2,1)S(1)} all-to-all(bf16[32,20,182]{2,1,0:T(8,128)(2,1)S(1)} %reshape.376), channel_id=1, replica_groups=mesh['zh'=2,'y'=4,'x'=4,'zlh'=4,'zll'=2,'c'=2] {'zh','y','x'}, dimensions={0} | all-to-all | bytes 465920 | tf_op jit(solution)/shard_map/all_to_all | solution.py:206
  129.8 66.4 %all-gather.4.cloned.1.call-done = bf16[8,640,182]{1,2,0:T(8,128)(2,1)} async-done(((bf16[1,640,182]{1,2,0:T(8,128)(2,1)}), bf16[8,640,182]{1,2,0:T(8,128)(2,1)}) %all-gather.4.cloned.1.call-update) | async-done | bytes 1863696 | tf_op jit(solution)/shard_map/all_gather | solution.py:213
  196.2 3.0 copy.102
  201.1 9.7 %reshape.377 = bf16[8,2,180,360]{2,1,0,3:T(2,128)(2,1)} reshape(bf16[1,2880,2,180]{1,3,2,0:T(8,128)(2,1)S(1)} %copy.104) | data formatting | bytes 4147200 | tf_op jit(solution)/shard_map/reshape | solution.py:221
  210.8 6.4 %reshape.379 = bf16[180,4,2,2,180]{4,3,2,1,0:T(2,128)(2,1)S(1)} reshape(bf16[1,180,2880]{2,1,0:T(8,128)(2,1)} %param.23) | data formatting | bytes 2073600 | tf_op jit(solution)/shard_map/reshape | solution.py:235
  217.3 7.9 %all-gather.6.cloned.1.call-done = bf16[16,640,182]{1,0,2:T(8,128)(2,1)} async-done(((bf16[8,640,182]{1,0,2:T(8,128)(2,1)}), bf16[16,640,182]{1,0,2:T(8,128)(2,1)}) %all-gather.6.cloned.1.call-update) | async-done | bytes 3727376 | tf_op jit(solution)/shard_map/all_gather | solution.py:214
  225.2 3.0 copy.103
  228.3 4.1 %fusion.14 = f32[640,360]{0,1:T(8,128)} fusion(bf16[8,2,180,360]{2,1,0,3:T(2,128)(2,1)S(1)} %copy-done.1, bf16[2,8,640,182]{2,3,1,0:T(8,128)(2,1)S(1)} %bitcast.91, f32[640]{0:T(1024)S(1)} %add_rsqrt_fusion), kind=kOutput, calls=%fused_computation.17 | convolution fusion | flops 1327334400 | bytes 6725120 | tf_op jit(solution)/shard_map/czrk,zckf->rf/dot_general | solution.py:222
  237.4 7.7 %all_to_all.47 = bf16[2,4,2,640,180]{3,1,4,2,0:T(4,128)(2,1)} all-to-all(bf16[2,4,2,640,180]{3,1,4,2,0:T(4,128)(2,1)S(1)} %copy.107), channel_id=1, replica_groups=mesh['zh'=2,'y'=4,'x'=4,'zlh'=4,'zll'=2,'c'=2] {'c'}, dimensions={0} | all-to-all | bytes 7372800 | tf_op jit(solution)/shard_map/all_to_all | solution.py:239
  245.1 5.0 %reduce_sum.111 = bf16[4,2,640,180]{2,0,3,1:T(4,128)(2,1)S(1)} reduce(bf16[2,4,2,640,180]{3,1,4,2,0:T(4,128)(2,1)} %all_to_all.47, bf16[]{:T(256)} %constant.90.clone.1), dimensions={0}, to_apply=%region_10.11 | reduce | flops 921600 | bytes 5529602 | tf_op jit(solution)/shard_map/reduce_sum | solution.py:240
  251.1 25.3 %all_to_all.48 = bf16[2,4,640,180]{2,1,3,0:T(4,128)(2,1)S(1)} all-to-all(bf16[2,4,640,180]{2,1,3,0:T(4,128)(2,1)S(1)} %copy.109), channel_id=1, replica_groups=mesh['zh'=2,'y'=4,'x'=4,'zlh'=4,'zll'=2,'c'=2] {'zll'}, dimensions={0} | all-to-all | bytes 3686400 | tf_op jit(solution)/shard_map/all_to_all | solution.py:241
  278.6 52.8 %all_to_all.49 = bf16[4,640,180]{1,2,0:T(8,128)(2,1)S(1)} all-to-all(bf16[4,640,180]{1,2,0:T(8,128)(2,1)S(1)} %copy.110), channel_id=1, replica_groups=mesh['zh'=2,'y'=4,'x'=4,'zlh'=4,'zll'=2,'c'=2] {'zlh'}, dimensions={0} | all-to-all | bytes 1843200 | tf_op jit(solution)/shard_map/all_to_all | solution.py:243
  332.6 11.5 %all-to-all-start.8 = ((bf16[32,20,180]{2,1,0:T(8,128)(2,1)}), bf16[32,20,180]{2,1,0:T(8,128)(2,1)S(1)}, u32[]{:S(2)}, u32[]{:S(2)}) async-start(bf16[32,20,180]{2,1,0:T(8,128)(2,1)} %reshape.380), calls=%async_computation.8 | async-start | bytes 786432 | tf_op jit(solution)/shard_map/all_to_all | solution.py:245
  344.4 23.3 %all-to-all-done.8 = bf16[32,20,180]{2,1,0:T(8,128)(2,1)S(1)} async-done(((bf16[32,20,180]{2,1,0:T(8,128)(2,1)}), bf16[32,20,180]{2,1,0:T(8,128)(2,1)S(1)}, u32[]{:S(2)}, u32[]{:S(2)}) %all-to-all-start.8) | async-done | bytes 230432 | tf_op jit(solution)/shard_map/all_to_all | solution.py:245
  (103 shorter events, 35.5 us)
Async XLA Ops:
  6.5 54.5 %copy-start = (bf16[128,2880]{0,1:T(8,128)(2,1)S(1)}, bf16[128,2880]{0,1:T(8,128)(2,1)}, u32[]{:S(2)}) copy-start(bf16[128,2880]{0,1:T(8,128)(2,1)} %param.18) | copy-start | bytes 2211844
  8.5 16.3 %collective-permute-start = (bf16[128,128]{0,1:T(8,128)(2,1)S(1)}, bf16[128,128]{0,1:T(8,128)(2,1)S(1)}, u32[]{:S(2)}, u32[]{:S(2)}) collective-permute-start(bf16[128,128]{0,1:T(8,128)(2,1)S(1)} %pad_maximum_fusion.2), channel_id=1, source_target_pairs={{0,256},{256,0},{1,257},{257,1},{2,258},{258,2},{3,259},{259,3},{4... | collective-permute-start | bytes 98312 | tf_op jit(solution)/shard_map/ppermute | solution.py:113
  25.7 11.1 %all-to-all-start = ((bf16[4,2,128,128]{2,1,3,0:T(2,128)(2,1)}), bf16[4,2,128,128]{2,1,3,0:T(2,128)(2,1)S(1)}, u32[]{:S(2)}, u32[]{:S(2)}) async-start(bf16[4,2,128,128]{2,1,3,0:T(2,128)(2,1)} %broadcast_in_dim.21), calls=%async_computation | async-start | bytes 524288 | tf_op jit(solution)/shard_map/all_to_all | solution.py:121
  38.6 17.2 %all-to-all-start.1 = ((bf16[4,4,2,128,128]{3,2,1,4,0:T(2,128)(2,1)}), bf16[4,4,2,128,128]{3,2,1,4,0:T(2,128)(2,1)S(1)}, u32[]{:S(2)}, u32[]{:S(2)}) async-start(bf16[4,4,2,128,128]{3,2,1,4,0:T(2,128)(2,1)} %broadcast_in_dim.22), calls=%async_computation.1 | async-start | bytes 2097152 | tf_op jit(solution)/shard_map/all_to_all | solution.py:128
  56.5 1.7 copy-start.6
  61.4 16.6 %copy-start.4 = (s32[128,4]{0,1:T(4,128)S(1)}, s32[128,4]{0,1:T(4,128)}, u32[]{:S(2)}) copy-start(s32[128,4]{0,1:T(4,128)} %param.20) | copy-start | bytes 6148
  67.1 30.5 %all-to-all-start.3 = ((bf16[8,128,180]{1,2,0:T(8,128)(2,1)}), bf16[8,128,180]{1,2,0:T(8,128)(2,1)S(1)}, u32[]{:S(2)}, u32[]{:S(2)}) async-start(bf16[8,128,180]{1,2,0:T(8,128)(2,1)} %copy.117), calls=%async_computation.3 | async-start | bytes 753664 | tf_op jit(solution)/shard_map/all_to_all | solution.py:172
  77.9 118.3 %all-gather.4.cloned.1.call-start = ((), (), s32[]{:S(2)}) async-start(), calls=%async_computation.9 | async-start | bytes 2119680 | tf_op jit(solution)/shard_map/all_gather | solution.py:213
  97.7 0.6 copy-start.2
  129.8 95.4 %all-gather.6.cloned.1.call-start = ((), (), s32[]{:S(2)}) async-start(), calls=%async_computation.10 | async-start | bytes 5591040 | tf_op jit(solution)/shard_map/all_gather | solution.py:214
  225.2 3.1 copy-start.1
  278.4 65.9 %copy-start.5 = (f32[128,4]{0,1:T(4,128)S(1)}, f32[128,4]{0,1:T(4,128)}, u32[]{:S(2)}) copy-start(f32[128,4]{0,1:T(4,128)} %param.21) | copy-start | bytes 6148
  331.6 38.9 %copy-start.3 = (f32[128,180]{0,1:T(8,128)S(1)}, f32[128,180]{0,1:T(8,128)}, u32[]{:S(2)}) copy-start(f32[128,180]{0,1:T(8,128)} %copy-done.2) | copy-start | bytes 276484
  332.6 35.1 %all-to-all-start.8 = ((bf16[32,20,180]{2,1,0:T(8,128)(2,1)}), bf16[32,20,180]{2,1,0:T(8,128)(2,1)S(1)}, u32[]{:S(2)}, u32[]{:S(2)}) async-start(bf16[32,20,180]{2,1,0:T(8,128)(2,1)} %reshape.380), calls=%async_computation.8 | async-start | bytes 786432 | tf_op jit(solution)/shard_map/all_to_all | solution.py:245
Sparse Core Ops, SparseCore 0:
  129.9 66.2 all-gather.3
  199.4 25.7 all-gather.5
